TPU v7x, 256 devices: a whole 4x4x8 slice. The times are simulated.
256 devices in a mesh: gx: 32 (over x, z_hi, core), gy: 8 (over y, z_lo).
Axes of the slice: x: 4, y: 4, z: 8 (z_hi: 4, z_lo: 2; z = z_hi * 2 + z_lo), core: 2. Of those that a mesh axis runs over, the one named last changes fastest.
Arguments:
- state: float32 [1024, 512, 384], P('gx', 'gy'), may hold values from -3 to 3
- obs_owner: int32 [2, 4096], replicated, may hold values from 0 to 255
- obs_cell: int32 [2, 4096], replicated, may hold values from 0 to 2047
- obs_level: int32 [2, 4096], replicated, may hold values from 0 to 3
- obs_coef: float32 [2, 3, 4096], replicated, may hold values from -1 to 1
- obs_value: float32 [2, 4096], replicated, may hold values from -8 to 8
- obs_error: float32 [2, 4096], replicated, may hold values from 0.5 to 2
- pattern: int32 [32, 8, 2, 16], P('gx', 'gy'), may hold values 0 or 1
Outputs:
- analysis: float32 [1024, 512, 384], P('gx', 'gy')
Inputs may be any that keep to these rules, and one draw needn't show every extreme that they name: `obs_owner`: the tile numbered (its gx index) * 8 + (its gy index). `obs_cell`: cell i * 64 + j of the owner tile, i along the first dimension. `pattern`: 1 where the tile uses the block.
All inputs are finite; a program needn't handle non-finite values. Where the computation divides by a largest or mean magnitude, that divisor is 1e-20 or more.
Results may differ from a plain program's by a relative error of at most 0.0003.
Values sent between devices are 32-bit elements; how exact they have to be, the bound alone decides.
No kernel may reach another device: no remote copies, remote signals or barrier semaphores. Data moves between devices by JAX's collectives and lax.ppermute only.
A program may use at most 128 MiB of HBM per device.

v0:
```python
import math

import jax
import jax.numpy as jnp
from jax import lax
from jax.experimental import pallas as pl
from jax.experimental.pallas import tpu as pltpu
from jax.sharding import PartitionSpec as P

ENS = 32
LEV = 4
COMP = 3
NSIT = 4


courant = 0.1
diffusion = 0.08
radius_share = 0.25


def advance_once(field):
    halos = []
    for axis, dim in (("gx", 0), ("gy", 1)):
        size, length = lax.axis_size(axis), field.shape[dim]
        up = [(i, (i + 1) % size) for i in range(size)]
        down = [(j, i) for i, j in up]
        last = lax.slice_in_dim(field, length - 1, length, axis=dim)
        initial = lax.slice_in_dim(field, 0, 1, axis=dim)
        halos += [lax.ppermute(last, axis, up), lax.ppermute(initial, axis, down)]
    return step(field, *halos)


def gather_kernel(cell_ref, level_ref, coef_ref, field_ref, out_ref):
    count = cell_ref.shape[0]
    width = field_ref.shape[1] // 3
    lane_level = lax.broadcasted_iota(jnp.int32, (1, width), 1) // ENS
    sublane = lax.broadcasted_iota(jnp.int32, (8, width), 0)
    groups = width // ENS

    def body(block, carry):
        gathered = [jnp.zeros((8, width), jnp.float32) for k in range(groups)]
        for i in range(8):
            for k in range(groups):
                j = (block * 8 + i) * groups + k
                picked = field_ref[pl.ds(cell_ref[j], 1), :]
                value = (
                    coef_ref[j] * picked[:, 0:width]
                    + coef_ref[count + j] * picked[:, width:2 * width]
                    + coef_ref[2 * count + j] * picked[:, 2 * width:3 * width]
                )
                value = jnp.where(lane_level == level_ref[j], value, 0.0)
                gathered[k] = jnp.where(sublane == i, value, gathered[k])
        first = pl.multiple_of(block * 8, 8)
        for k in range(groups):
            out_ref[pl.ds(first, 8), k * width:(k + 1) * width] = gathered[k]
        return carry

    lax.fori_loop(0, count // (8 * groups), body, 0)


def gather_rows(cells, levels, coefs, field):
    count = cells.shape[0]
    width = field.shape[1] // 3
    groups = width // ENS
    smem = pl.BlockSpec(memory_space=pltpu.SMEM)
    vmem = pl.BlockSpec(memory_space=pltpu.VMEM)
    return pl.pallas_call(
        gather_kernel,
        out_shape=jax.ShapeDtypeStruct((count // groups, groups * width), jnp.float32),
        in_specs=[smem, smem, smem, vmem],
        out_specs=vmem,
    )(cells, levels, coefs.reshape(-1), field)

def step_kernel(field_ref, west_ref, east_ref, south_ref, north_ref, out_ref):
    nx, ny, feat = field_ref.shape
    width = feat // 3
    row_id = lax.broadcasted_iota(jnp.int32, (ny, width), 0)

    def body(x, carry):
        centre = field_ref[x]
        west = jnp.where(x == 0, west_ref[0], field_ref[jnp.maximum(x - 1, 0)])
        east = jnp.where(x == nx - 1, east_ref[0], field_ref[jnp.minimum(x + 1, nx - 1)])
        south_edge = south_ref[x]
        north_edge = north_ref[x]
        u = centre[:, 0:width]
        v = centre[:, width:2 * width]
        pu, mu = jnp.maximum(u, 0.0), jnp.minimum(u, 0.0)
        pv, mv = jnp.maximum(v, 0.0), jnp.minimum(v, 0.0)
        for b in range(3):
            lanes = slice(b * width, (b + 1) * width)
            c = centre[:, lanes]
            w = west[:, lanes]
            e = east[:, lanes]
            s = jnp.where(row_id == 0, south_edge[:, lanes], pltpu.roll(c, 1, 0))
            n = jnp.where(row_id == ny - 1, north_edge[:, lanes], pltpu.roll(c, ny - 1, 0))
            flux = pu * (c - w) + mu * (e - c) + pv * (c - s) + mv * (n - c)
            out_ref[x, :, lanes] = c - courant * flux + diffusion * (w + e + (s + n) - 4.0 * c)
        return carry

    lax.fori_loop(0, nx, body, 0)

def step(field, west, east, south, north):
    vmem = pl.BlockSpec(memory_space=pltpu.VMEM)
    return pl.pallas_call(
        step_kernel,
        out_shape=jax.ShapeDtypeStruct(field.shape, field.dtype),
        in_specs=[vmem] * 5,
        out_specs=vmem,
    )(field, west, east, south, north)


def product(left, right):
    return jnp.dot(left, right, precision=lax.Precision.HIGHEST, preferred_element_type=jnp.float32)


def mix_kernel(rows_ref, first_ref, second_ref, out_ref):
    width = first_ref.shape[0]
    for block in range(rows_ref.shape[1] // width):
        lanes = slice(block * width, (block + 1) * width)
        once = product(rows_ref[:, lanes], first_ref[...])
        out_ref[:, lanes] = product(once, second_ref[...])


def mixed_twice(rows, first, second):
    count, features = rows.shape
    width = first.shape[0]
    tile = 256
    return pl.pallas_call(
        mix_kernel,
        out_shape=jax.ShapeDtypeStruct(rows.shape, rows.dtype),
        grid=(count // tile,),
        in_specs=[
            pl.BlockSpec((tile, features), lambda i: (i, 0)),
            pl.BlockSpec((width, width), lambda i: (0, 0)),
            pl.BlockSpec((width, width), lambda i: (0, 0)),
        ],
        out_specs=pl.BlockSpec((tile, features), lambda i: (i, 0)),
    )(rows, first, second)


def summed_everywhere(rows):
    axes = ("gx", "gy")
    devices = lax.axis_size("gx") * lax.axis_size("gy")
    parts = lax.all_to_all(rows, axes, 0, 0, tiled=True)
    chunk = parts.reshape((devices, rows.shape[0] // devices) + rows.shape[1:]).sum(axis=0)
    copies = jnp.broadcast_to(chunk[None], (devices,) + chunk.shape).reshape(rows.shape)
    return lax.all_to_all(copies, axes, 0, 0, tiled=True)


def localize(
    owners,
    obs_cells,
    block_mask,
    tile_east,
    tile_north,
    span_east,
    span_north,
    tiles_north,
    grid_east,
    grid_north,
):
    place_east = (owners // tiles_north * span_east + obs_cells // span_north).astype(jnp.float32)
    place_north = (owners % tiles_north * span_north + obs_cells % span_north).astype(jnp.float32)
    centre_east = (tile_east * span_east).astype(jnp.float32) + (span_east - 1) / 2.0
    centre_north = (tile_north * span_north).astype(jnp.float32) + (span_north - 1) / 2.0
    gap_east = (
        jnp.remainder(place_east - centre_east + grid_east / 2.0, grid_east) - grid_east / 2.0
    )
    gap_north = (
        jnp.remainder(place_north - centre_north + grid_north / 2.0, grid_north) - grid_north / 2.0
    )
    scale_east = gap_east / (radius_share * grid_east)
    scale_north = gap_north / (radius_share * grid_north)
    weight = jnp.exp(-0.5 * (scale_east * scale_east + scale_north * scale_north))
    blocks = block_mask.shape[0]
    return (weight.reshape(blocks, -1) * block_mask.astype(jnp.float32)[:, None]).reshape(-1)


def transform(predicted, obs_value, obs_error, weight_obs):
    rows, width = predicted.shape
    groups = width // ENS
    members = ENS

    def spread(per_obs):
        return jnp.broadcast_to(per_obs.reshape(rows, groups, 1), (rows, groups, ENS)).reshape(rows, width)

    lane_in = lax.broadcasted_iota(jnp.int32, (width, width), 0) // ENS
    lane_out = lax.broadcasted_iota(jnp.int32, (width, width), 1) // ENS
    averaging = jnp.where(lane_in == lane_out, 1.0 / members, 0.0).astype(jnp.float32)
    centre_obs = product(predicted, averaging)
    error = spread(obs_error)
    deviation = (predicted - centre_obs) / error
    innovation = (spread(obs_value) - centre_obs) / error
    weighted = deviation * spread(weight_obs)
    blocks = product(weighted.T, deviation)
    covariance = sum(blocks[k * ENS:(k + 1) * ENS, k * ENS:(k + 1) * ENS] for k in range(groups))
    projected = jnp.sum(weighted * innovation, axis=0)
    projection = sum(projected[k * ENS:(k + 1) * ENS] for k in range(groups))
    unit_matrix = jnp.eye(members, dtype=jnp.float32)
    system = (members - 1.0) * unit_matrix + covariance
    row_bound = jnp.max(jnp.sum(jnp.abs(system), axis=1))

    def refine(sweep_index, iterates):
        approach, inverse_root = iterates
        middle = 1.5 * unit_matrix - 0.5 * product(inverse_root, approach)
        return (product(approach, middle), product(middle, inverse_root))

    approach, inverse_root = lax.fori_loop(0, NSIT, refine, (system / row_bound, unit_matrix))
    inverse = product(inverse_root, inverse_root) / row_bound
    weights = product(inverse, projection[:, None])[:, 0]
    centring = unit_matrix - 1.0 / members
    shifts = weights[:, None] + math.sqrt(members - 1.0) * inverse_root / jnp.sqrt(row_bound)
    return 1.0 / members + product(centring, shifts)


def block_diagonal(mix, copies):
    return jnp.kron(jnp.eye(copies, dtype=mix.dtype), mix)


def local(state, obs_owner, obs_cell, obs_level, obs_coef, obs_value, obs_error, pattern):
    span_east, span_north, features = state.shape
    tiles_east = lax.axis_size("gx")
    tiles_north = lax.axis_size("gy")
    tile_east = lax.axis_index("gx")
    tile_north = lax.axis_index("gy")
    own_tile = tile_east * tiles_north + tile_north
    field = state
    for substep in range(2):
        field = advance_once(field)
    cells = field.reshape(span_east * span_north, features)
    width = features // COMP
    groups = width // ENS
    owned = (obs_owner == own_tile).astype(jnp.float32)
    masked_coefs = jnp.transpose(obs_coef * owned[:, None, :], (1, 0, 2)).reshape(COMP, -1)
    spread = gather_rows(obs_cell.reshape(-1), obs_level.reshape(-1), masked_coefs, cells)
    spread_lane = lax.broadcasted_iota(jnp.int32, (groups * width, groups * ENS), 0)
    dense_lane = lax.broadcasted_iota(jnp.int32, (groups * width, groups * ENS), 1)
    fold = (
        (spread_lane // width == dense_lane // ENS) & (spread_lane % ENS == dense_lane % ENS)
    ).astype(jnp.float32)
    dense = product(spread, fold)
    per_batch = dense.shape[0] // 2

    def mixing(local_terms, batch_index):
        predicted = summed_everywhere(local_terms)
        weight_obs = localize(
            obs_owner[batch_index],
            obs_cell[batch_index],
            pattern[0, 0, batch_index],
            tile_east,
            tile_north,
            span_east,
            span_north,
            tiles_north,
            span_east * tiles_east,
            span_north * tiles_north,
        )
        return transform(predicted, obs_value[batch_index], obs_error[batch_index], weight_obs)

    first_mix = mixing(dense[:per_batch], 0)
    second_terms = product(dense[per_batch:], block_diagonal(first_mix, groups))
    second_mix = mixing(second_terms, 1)
    rows = mixed_twice(cells, block_diagonal(first_mix, groups), block_diagonal(second_mix, groups))
    return rows.reshape(span_east, span_north, features)


def solution(mesh):
    placed = (P("gx", "gy", None), P(), P(), P(), P(), P(), P(), P("gx", "gy", None, None))
    return jax.shard_map(
        local, mesh=mesh, in_specs=placed, out_specs=P("gx", "gy", None), check_vma=False
    )
```

profile of v0, /device:TPU:1, one launch (start us, length us, event | category | flops | bytes accessed | tf_op | source)
XLA Modules:
  0.0 227.4 jit_solution(9045654529821430702)
XLA Ops:
  0.0 1.0 fusion.149
  1.0 4.5 %collective-permute-start = (f32[1,64,384]{2,1,0:T(8,128)S(1)}, f32[1,64,384]{2,1,0:T(8,128)S(1)}, u32[]{:S(2)}, u32[]{:S(2)}) collective-permute-start(f32[1,64,384]{2,1,0:T(8,128)S(1)} %get-tuple-element.122), channel_id=1, source_target_pairs={{0,8},{8,16},{16,24},{24,32},{32,40},{40,48},{48,56},{56,64},{64,7... | collective-permute-start | bytes 294920 | tf_op jit(solution)/shard_map/ppermute | solution.py:29
  5.4 1.2 fusion.148
  6.6 1.7 collective-permute-start.2
  8.3 2.5 %collective-permute-start.3 = (f32[32,1,384]{2,1,0:T(1,128)S(1)}, f32[32,1,384]{2,1,0:T(1,128)S(1)}, u32[]{:S(2)}, u32[]{:S(2)}) collective-permute-start(f32[32,1,384]{2,1,0:T(1,128)S(1)} %get-tuple-element.119), channel_id=1, source_target_pairs={{1,0},{2,1},{3,2},{4,3},{5,4},{6,5},{7,6},{0,7},{9,8},{10,9},{11,1... | collective-permute-start | bytes 147464 | tf_op jit(solution)/shard_map/ppermute | solution.py:29
  10.9 0.8 compare_convert_fusion
  11.7 0.9 multiply_bitcast_fusion
  12.7 0.6 collective-permute-done.2.south_ref
  13.3 0.6 copy-done.6
  14.0 0.6 copy-done.3
  14.6 6.7 %shard_map.82.field_ref = f32[32,64,384]{2,1,0:T(8,128)} custom-call(f32[32,64,384]{2,1,0:T(8,128)} %field_ref.1, f32[1,64,384]{2,1,0:T(8,128)} %copy-done.2, f32[1,64,384]{2,1,0:T(8,128)} %copy-done.3, f32[32,1,384]{2,1,0:T(1,128)} %copy-done.6, f32[32,1,384]{2,1,0:T(1,128)} %copy-done.7), custom_call_target="tpu_custom_call" | custom-call | tf_op jit(solution)/shard_map/pallas_call | solution.py:104
  21.3 1.0 fusion.147
  22.3 1.2 fusion.146
  23.5 3.6 %collective-permute-start.4 = (f32[1,64,384]{2,1,0:T(8,128)S(1)}, f32[1,64,384]{2,1,0:T(8,128)S(1)}, u32[]{:S(2)}, u32[]{:S(2)}) collective-permute-start(f32[1,64,384]{2,1,0:T(8,128)S(1)} %get-tuple-element.118), channel_id=1, source_target_pairs={{0,8},{8,16},{16,24},{24,32},{32,40},{40,48},{48,56},{56,64},{64,7... | collective-permute-start | bytes 294920 | tf_op jit(solution)/shard_map/ppermute | solution.py:29
  27.1 1.3 collective-permute-start.5
  28.4 1.5 collective-permute-start.6
  29.9 2.3 %collective-permute-start.7 = (f32[32,1,384]{2,1,0:T(1,128)S(1)}, f32[32,1,384]{2,1,0:T(1,128)S(1)}, u32[]{:S(2)}, u32[]{:S(2)}) collective-permute-start(f32[32,1,384]{2,1,0:T(1,128)S(1)} %get-tuple-element.115), channel_id=1, source_target_pairs={{1,0},{2,1},{3,2},{4,3},{5,4},{6,5},{7,6},{0,7},{9,8},{10,9},{11,1... | collective-permute-start | bytes 147464 | tf_op jit(solution)/shard_map/ppermute | solution.py:29
  32.2 0.6 copy.87
  32.9 0.6 copy.85
  33.5 0.6 copy.86
  34.3 0.6 copy-done.8
  34.9 0.6 copy-done.5
  35.6 6.7 %shard_map.83 = f32[32,64,384]{2,1,0:T(8,128)} custom-call(f32[32,64,384]{2,1,0:T(8,128)} %shard_map.82.field_ref, f32[1,64,384]{2,1,0:T(8,128)} %copy-done.4, f32[1,64,384]{2,1,0:T(8,128)} %copy-done.5, f32[32,1,384]{2,1,0:T(1,128)} %copy-done.8, f32[32,1,384]{2,1,0:T(1,128)} %copy-done.9), custom_call_target="tpu_custom_call" | custom-call | tf_op jit(solution)/shard_map/pallas_call | solution.py:104
  42.3 37.1 %shard_map.84 = f32[2048,512]{1,0:T(8,128)} custom-call(s32[8192]{0:T(1024)} %bitcast.103, s32[8192]{0:T(1024)} %bitcast.104, f32[24576]{0:T(1024)} %bitcast.102, f32[2048,384]{1,0:T(8,128)} %bitcast.88), custom_call_target="tpu_custom_call" | custom-call | tf_op jit(solution)/shard_map/pallas_call | solution.py:67
  79.4 4.7 %fusion.13 = f32[2048,128]{1,0:T(8,128)S(1)} fusion(f32[2048,512]{1,0:T(8,128)} %shard_map.84, s32[128]{0:T(128)S(1)} %get-tuple-element.144, s32[128]{0:T(128)S(1)} %get-tuple-element.145, s32[512]{0:T(512)S(1)} %get-tuple-element.135, s32[512]{0:T(512)S(1)} %get-tuple-element.137, s32[128]{0:T(128)S(1)} %get-tuple-element.143, ...), kind=kOutput, calls=%fused_computation.29 | convolution fusion | flops 1611071488 | bytes 5254400 | tf_op jit(solution)/shard_map/dot_general | solution.py:113
  84.2 35.1 %all_to_all.33 = f32[256,4,128]{2,1,0:T(4,128)S(1)} all-to-all(f32[256,4,128]{2,1,0:T(4,128)S(1)} %bitcast.97), channel_id=1, replica_groups=mesh['gx'=32,'gy'=8] {'gx','gy'}, dimensions={0} | all-to-all | bytes 1048576 | tf_op jit(solution)/shard_map/all_to_all | solution.py:144
  119.5 0.9 broadcast_in_dim.73
  120.4 5.4 %all-to-all-start.1 = ((f32[256,4,128]{2,1,0:T(4,128)}), f32[256,4,128]{2,1,0:T(4,128)S(1)}, u32[]{:S(2)}, u32[]{:S(2)}) async-start(f32[256,4,128]{2,1,0:T(4,128)} %broadcast_in_dim.73), calls=%async_computation.1 | async-start | bytes 1048576 | tf_op jit(solution)/shard_map/all_to_all | solution.py:147
  130.2 16.5 %all-to-all-done.1 = f32[256,4,128]{2,1,0:T(4,128)S(1)} async-done(((f32[256,4,128]{2,1,0:T(4,128)}), f32[256,4,128]{2,1,0:T(4,128)S(1)}, u32[]{:S(2)}, u32[]{:S(2)}) %all-to-all-start.1) | async-done | bytes 524320 | tf_op jit(solution)/shard_map/all_to_all | solution.py:147
  146.7 0.8 multiply_reduce_fusion.1
  147.4 1.1 fusion.10
  148.6 0.6 reduce_max.18
  149.9 0.6 broadcast_divide_fusion.1
  150.6 2.2 while.26
  152.8 0.9 convolution_divide_fusion.1
  155.3 26.0 %all_to_all.34 = f32[256,4,128]{2,1,0:T(4,128)S(1)} all-to-all(f32[256,4,128]{2,1,0:T(4,128)S(1)} %copy.66), channel_id=1, replica_groups=mesh['gx'=32,'gy'=8] {'gx','gy'}, dimensions={0} | all-to-all | bytes 1048576 | tf_op jit(solution)/shard_map/all_to_all | solution.py:144
  181.6 0.9 broadcast_in_dim.81
  182.4 5.4 %all-to-all-start.3 = ((f32[256,4,128]{2,1,0:T(4,128)}), f32[256,4,128]{2,1,0:T(4,128)S(1)}, u32[]{:S(2)}, u32[]{:S(2)}) async-start(f32[256,4,128]{2,1,0:T(4,128)} %broadcast_in_dim.81), calls=%async_computation.3 | async-start | bytes 1048576 | tf_op jit(solution)/shard_map/all_to_all | solution.py:147
  191.8 0.8 mul.243.first_ref
  192.6 16.0 %all-to-all-done.3 = f32[256,4,128]{2,1,0:T(4,128)S(1)} async-done(((f32[256,4,128]{2,1,0:T(4,128)}), f32[256,4,128]{2,1,0:T(4,128)S(1)}, u32[]{:S(2)}, u32[]{:S(2)}) %all-to-all-start.3) | async-done | bytes 524320 | tf_op jit(solution)/shard_map/all_to_all | solution.py:147
  208.6 0.8 multiply_reduce_fusion
  209.4 1.1 fusion.8
  210.6 0.6 reduce_max.19
  211.9 0.6 broadcast_divide_fusion
  212.5 2.2 while.27
  214.8 0.9 convolution_divide_fusion
  216.2 0.8 mul.258.second_ref
  217.0 10.4 %shard_map.85 = f32[2048,384]{1,0:T(8,128)} custom-call(f32[2048,384]{1,0:T(8,128)} %bitcast.89, f32[128,128]{1,0:T(8,128)} %mul.243.first_ref, f32[128,128]{1,0:T(8,128)} %mul.258.second_ref), custom_call_target="tpu_custom_call" | custom-call | tf_op jit(solution)/shard_map/pallas_call | solution.py:128
  (133 shorter events, 15.7 us)
Async XLA Ops:
  1.0 12.4 %collective-permute-start = (f32[1,64,384]{2,1,0:T(8,128)S(1)}, f32[1,64,384]{2,1,0:T(8,128)S(1)}, u32[]{:S(2)}, u32[]{:S(2)}) collective-permute-start(f32[1,64,384]{2,1,0:T(8,128)S(1)} %get-tuple-element.122), channel_id=1, source_target_pairs={{0,8},{8,16},{16,24},{24,32},{32,40},{40,48},{48,56},{56,64},{64,7... | collective-permute-start | bytes 294920 | tf_op jit(solution)/shard_map/ppermute | solution.py:29
  5.4 7.9 %collective-permute-start.1 = (f32[1,64,384]{2,1,0:T(8,128)S(1)}, f32[1,64,384]{2,1,0:T(8,128)S(1)}, u32[]{:S(2)}, u32[]{:S(2)}) collective-permute-start(f32[1,64,384]{2,1,0:T(8,128)S(1)} %get-tuple-element.121), channel_id=1, source_target_pairs={{8,0},{16,8},{24,16},{32,24},{40,32},{48,40},{56,48},{64,56},{72,6... | collective-permute-start | bytes 294920 | tf_op jit(solution)/shard_map/ppermute | solution.py:29
  6.6 6.7 %collective-permute-start.2 = (f32[32,1,384]{2,1,0:T(1,128)S(1)}, f32[32,1,384]{2,1,0:T(1,128)S(1)}, u32[]{:S(2)}, u32[]{:S(2)}) collective-permute-start(f32[32,1,384]{2,1,0:T(1,128)S(1)} %get-tuple-element.120), channel_id=1, source_target_pairs={{0,1},{1,2},{2,3},{3,4},{4,5},{5,6},{6,7},{7,0},{8,9},{9,10},{10,1... | collective-permute-start | bytes 147464 | tf_op jit(solution)/shard_map/ppermute | solution.py:29
  8.3 5.0 %collective-permute-start.3 = (f32[32,1,384]{2,1,0:T(1,128)S(1)}, f32[32,1,384]{2,1,0:T(1,128)S(1)}, u32[]{:S(2)}, u32[]{:S(2)}) collective-permute-start(f32[32,1,384]{2,1,0:T(1,128)S(1)} %get-tuple-element.119), channel_id=1, source_target_pairs={{1,0},{2,1},{3,2},{4,3},{5,4},{6,5},{7,6},{0,7},{9,8},{10,9},{11,1... | collective-permute-start | bytes 147464 | tf_op jit(solution)/shard_map/ppermute | solution.py:29
  12.6 20.2 %copy-start = (s32[2,4096]{1,0:T(2,128)S(1)}, s32[2,4096]{1,0:T(2,128)}, u32[]{:S(2)}) copy-start(s32[2,4096]{1,0:T(2,128)} %param.14) | copy-start | bytes 98308
  12.6 20.8 %copy-start.10 = (s32[2,4096]{1,0:T(2,128)S(1)}, s32[2,4096]{1,0:T(2,128)}, u32[]{:S(2)}) copy-start(s32[2,4096]{1,0:T(2,128)} %param.15) | copy-start | bytes 98308
  13.3 0.6 copy-start.6
  13.3 0.6 copy-start.7
  13.3 0.7 copy-start.2
  14.0 0.6 copy-start.3
  23.5 10.8 %collective-permute-start.4 = (f32[1,64,384]{2,1,0:T(8,128)S(1)}, f32[1,64,384]{2,1,0:T(8,128)S(1)}, u32[]{:S(2)}, u32[]{:S(2)}) collective-permute-start(f32[1,64,384]{2,1,0:T(8,128)S(1)} %get-tuple-element.118), channel_id=1, source_target_pairs={{0,8},{8,16},{16,24},{24,32},{32,40},{40,48},{48,56},{56,64},{64,7... | collective-permute-start | bytes 294920 | tf_op jit(solution)/shard_map/ppermute | solution.py:29
  27.1 7.2 %collective-permute-start.5 = (f32[1,64,384]{2,1,0:T(8,128)S(1)}, f32[1,64,384]{2,1,0:T(8,128)S(1)}, u32[]{:S(2)}, u32[]{:S(2)}) collective-permute-start(f32[1,64,384]{2,1,0:T(8,128)S(1)} %get-tuple-element.117), channel_id=1, source_target_pairs={{8,0},{16,8},{24,16},{32,24},{40,32},{48,40},{56,48},{64,56},{72,6... | collective-permute-start | bytes 294920 | tf_op jit(solution)/shard_map/ppermute | solution.py:29
  28.4 5.9 %collective-permute-start.6 = (f32[32,1,384]{2,1,0:T(1,128)S(1)}, f32[32,1,384]{2,1,0:T(1,128)S(1)}, u32[]{:S(2)}, u32[]{:S(2)}) collective-permute-start(f32[32,1,384]{2,1,0:T(1,128)S(1)} %get-tuple-element.116), channel_id=1, source_target_pairs={{0,1},{1,2},{2,3},{3,4},{4,5},{5,6},{6,7},{7,0},{8,9},{9,10},{10,1... | collective-permute-start | bytes 147464 | tf_op jit(solution)/shard_map/ppermute | solution.py:29
  29.9 4.4 %collective-permute-start.7 = (f32[32,1,384]{2,1,0:T(1,128)S(1)}, f32[32,1,384]{2,1,0:T(1,128)S(1)}, u32[]{:S(2)}, u32[]{:S(2)}) collective-permute-start(f32[32,1,384]{2,1,0:T(1,128)S(1)} %get-tuple-element.115), channel_id=1, source_target_pairs={{1,0},{2,1},{3,2},{4,3},{5,4},{6,5},{7,6},{0,7},{9,8},{10,9},{11,1... | collective-permute-start | bytes 147464 | tf_op jit(solution)/shard_map/ppermute | solution.py:29
  34.3 0.6 copy-start.8
  34.3 0.6 copy-start.9
  34.3 0.7 copy-start.4
  34.9 0.6 copy-start.5
  84.1 41.7 %copy-start.1 = (s32[2,4096]{1,0:T(2,128)S(1)}, s32[2,4096]{1,0:T(2,128)}, u32[]{:S(2)}) copy-start(s32[2,4096]{1,0:T(2,128)} %param.13) | copy-start | bytes 98308
  84.2 43.2 %copy-start.13 = (s32[1,1,2,16]{3,2,1,0:T(2,128)S(1)}, s32[1,1,2,16]{3,2,1,0:T(2,128)}, u32[]{:S(2)}) copy-start(s32[1,1,2,16]{3,2,1,0:T(2,128)} %param.19) | copy-start | bytes 388
  119.2 8.7 %copy-start.11 = (f32[2,4096]{1,0:T(2,128)S(1)}, f32[2,4096]{1,0:T(2,128)}, u32[]{:S(2)}) copy-start(f32[2,4096]{1,0:T(2,128)} %param.17) | copy-start | bytes 98308
  119.2 8.7 %copy-start.12 = (f32[2,4096]{1,0:T(2,128)S(1)}, f32[2,4096]{1,0:T(2,128)}, u32[]{:S(2)}) copy-start(f32[2,4096]{1,0:T(2,128)} %param.18) | copy-start | bytes 98308
  120.4 26.3 %all-to-all-start.1 = ((f32[256,4,128]{2,1,0:T(4,128)}), f32[256,4,128]{2,1,0:T(4,128)S(1)}, u32[]{:S(2)}, u32[]{:S(2)}) async-start(f32[256,4,128]{2,1,0:T(4,128)} %broadcast_in_dim.73), calls=%async_computation.1 | async-start | bytes 1048576 | tf_op jit(solution)/shard_map/all_to_all | solution.py:147
  182.4 26.2 %all-to-all-start.3 = ((f32[256,4,128]{2,1,0:T(4,128)}), f32[256,4,128]{2,1,0:T(4,128)S(1)}, u32[]{:S(2)}, u32[]{:S(2)}) async-start(f32[256,4,128]{2,1,0:T(4,128)} %broadcast_in_dim.81), calls=%async_computation.3 | async-start | bytes 1048576 | tf_op jit(solution)/shard_map/all_to_all | solution.py:147
where the time goes:
time: 228 us; the launch traced here: 227 us
  Pallas kernels  61 us (27%)
  blocking collectives  61 us (27%)
  waiting for transfers between devices  33.3 us (15%)
  starting transfers between devices  28.2 us (12%)
  local copies, waits for them, and re-layouts  20.5 us (9%)
  matrix products  15.6 us (7%)
  other arithmetic  5.5 us (2%)
    all_to_all x2, blocking collectives, summed_everywhere(): parts = lax.all_to_all(rows, axes, 0, 0, tiled=True)  61 us
    pallas_call x1, Pallas kernels, gather_rows(): pl.pallas_call(gather_kernel, out_shape=jax.ShapeDtypeStruct((count // gr...  37.1 us
    all_to_all x2, waiting for transfers between devices, summed_everywhere(): return lax.all_to_all(copies, axes, 0, 0, tiled=True)  32.5 us
    ppermute x8, starting transfers between devices, advance_once(): halos += [lax.ppermute(last, axis, up), lax.ppermute(initial, axis, down)]  17.4 us
    dot_general x36, matrix products, product(): jnp.dot(left, right, precision=lax.Precision.HIGHEST, preferred_element_t...  15.6 us
    pallas_call x2, Pallas kernels, step(): pl.pallas_call(step_kernel, out_shape=jax.ShapeDtypeStruct(field.shape, f...  13.5 us
    all_to_all x2, starting transfers between devices, summed_everywhere(): return lax.all_to_all(copies, axes, 0, 0, tiled=True)  10.7 us
    pallas_call x1, Pallas kernels, mixed_twice(): pl.pallas_call(mix_kernel, out_shape=jax.ShapeDtypeStruct(rows.shape, row...  10.4 us
  transfers between devices with their start and end apart: 10, of which 4 were waited for; matrix products, arithmetic and copies ran while one was open for 6% of the time, Pallas kernels for 0%

commit v1 on v0

--- a/solution.py
+++ b/solution.py
@@ -113,17 +113,16 @@
     return jnp.dot(left, right, precision=lax.Precision.HIGHEST, preferred_element_type=jnp.float32)
 
 
-def mix_kernel(rows_ref, first_ref, second_ref, out_ref):
-    width = first_ref.shape[0]
+def mix_kernel(rows_ref, mix_ref, out_ref):
+    width = mix_ref.shape[0]
     for block in range(rows_ref.shape[1] // width):
         lanes = slice(block * width, (block + 1) * width)
-        once = product(rows_ref[:, lanes], first_ref[...])
-        out_ref[:, lanes] = product(once, second_ref[...])
-
-
-def mixed_twice(rows, first, second):
+        out_ref[:, lanes] = product(rows_ref[:, lanes], mix_ref[...])
+
+
+def mixed_once(rows, mix):
     count, features = rows.shape
-    width = first.shape[0]
+    width = mix.shape[0]
     tile = 256
     return pl.pallas_call(
         mix_kernel,
@@ -132,10 +131,9 @@
         in_specs=[
             pl.BlockSpec((tile, features), lambda i: (i, 0)),
             pl.BlockSpec((width, width), lambda i: (0, 0)),
-            pl.BlockSpec((width, width), lambda i: (0, 0)),
         ],
         out_specs=pl.BlockSpec((tile, features), lambda i: (i, 0)),
-    )(rows, first, second)
+    )(rows, mix)
 
 
 def summed_everywhere(rows):
@@ -231,15 +229,17 @@
     width = features // COMP
     groups = width // ENS
     owned = (obs_owner == own_tile).astype(jnp.float32)
-    masked_coefs = jnp.transpose(obs_coef * owned[:, None, :], (1, 0, 2)).reshape(COMP, -1)
-    spread = gather_rows(obs_cell.reshape(-1), obs_level.reshape(-1), masked_coefs, cells)
     spread_lane = lax.broadcasted_iota(jnp.int32, (groups * width, groups * ENS), 0)
     dense_lane = lax.broadcasted_iota(jnp.int32, (groups * width, groups * ENS), 1)
     fold = (
         (spread_lane // width == dense_lane // ENS) & (spread_lane % ENS == dense_lane % ENS)
     ).astype(jnp.float32)
-    dense = product(spread, fold)
-    per_batch = dense.shape[0] // 2
+
+    def observed(batch_index):
+        masked_coefs = obs_coef[batch_index] * owned[batch_index][None, :]
+        spread = gather_rows(obs_cell[batch_index], obs_level[batch_index], masked_coefs, cells)
+        return product(spread, fold)
+
 
     def mixing(local_terms, batch_index):
         predicted = summed_everywhere(local_terms)
@@ -257,10 +257,10 @@
         )
         return transform(predicted, obs_value[batch_index], obs_error[batch_index], weight_obs)
 
-    first_mix = mixing(dense[:per_batch], 0)
-    second_terms = product(dense[per_batch:], block_diagonal(first_mix, groups))
+    first_mix = mixing(observed(0), 0)
+    second_terms = product(observed(1), block_diagonal(first_mix, groups))
     second_mix = mixing(second_terms, 1)
-    rows = mixed_twice(cells, block_diagonal(first_mix, groups), block_diagonal(second_mix, groups))
+    rows = mixed_once(cells, block_diagonal(product(first_mix, second_mix), groups))
     return rows.reshape(span_east, span_north, features)
 
 

time: 228 us -> 223 us (0.978)
  blocking collectives: 61 us -> 34.4 us
  starting transfers between devices: 28.2 us -> 43.1 us
  waiting for transfers between devices: 33.3 us -> 37.4 us
  matrix products: 15.6 us -> 17.9 us
    all_to_all x2 -> x1, blocking collectives: 61 us -> 34.4 us  [summed_everywhere(): parts = lax.all_to_all(rows, axes, 0, 0, tiled=True)]
    all_to_all x0 -> x1, waiting for transfers between devices: none -> 19.7 us  [summed_everywhere(): parts = lax.all_to_all(rows, axes, 0, 0, tiled=True)]
    all_to_all x2, waiting for transfers between devices: 32.5 us -> 16.8 us  [summed_everywhere(): return lax.all_to_all(copies, axes, 0, 0, tiled=True)]
    all_to_all x0 -> x1, starting transfers between devices: none -> 14.8 us  [summed_everywhere(): parts = lax.all_to_all(rows, axes, 0, 0, tiled=True)]
    slice x2 -> x4, local copies, waits for them, and re-layouts: 0.22 us -> 4.09 us  [the longest x1 1.52 us: mixing(): obs_owner[batch_index]]
    pallas_call x1, Pallas kernels: 10.4 us -> 7.74 us  [mixed_once(): pl.pallas_call(mix_kernel, out_shape=jax.ShapeDtypeStruct(rows.shape, row...]
    dot_general x36 -> x38, matrix products: 15.6 us -> 17.9 us  [product(): jnp.dot(left, right, precision=lax.Precision.HIGHEST, preferred_element_t...]
    pallas_call x1 -> x2, Pallas kernels: 37.1 us -> 38.4 us  [gather_rows(): pl.pallas_call(gather_kernel, out_shape=jax.ShapeDtypeStruct((count // gr...]
  transfers between devices with their start and end apart: 10 -> 11, of which waited for: 4 -> 3; matrix products, arithmetic and copies ran while one was open for 6% -> 8% of each run, Pallas kernels for 0% -> 9%
where the time goes in v1:
time: 223 us
  Pallas kernels  59.6 us (27%)
  starting transfers between devices  43.1 us (19%)
  waiting for transfers between devices  37.4 us (17%)
  blocking collectives  34.4 us (15%)
  local copies, waits for them, and re-layouts  21.9 us (10%)
  matrix products  17.9 us (8%)
  other arithmetic  5.82 us (3%)
    pallas_call x2, Pallas kernels, gather_rows(): pl.pallas_call(gather_kernel, out_shape=jax.ShapeDtypeStruct((count // gr...  38.4 us
    all_to_all x1, blocking collectives, summed_everywhere(): parts = lax.all_to_all(rows, axes, 0, 0, tiled=True)  34.4 us
    all_to_all x1, waiting for transfers between devices, summed_everywhere(): parts = lax.all_to_all(rows, axes, 0, 0, tiled=True)  19.7 us
    dot_general x38, matrix products, product(): jnp.dot(left, right, precision=lax.Precision.HIGHEST, preferred_element_t...  17.9 us
    ppermute x8, starting transfers between devices, advance_once(): halos += [lax.ppermute(last, axis, up), lax.ppermute(initial, axis, down)]  17.6 us
    all_to_all x2, waiting for transfers between devices, summed_everywhere(): return lax.all_to_all(copies, axes, 0, 0, tiled=True)  16.8 us
    all_to_all x1, starting transfers between devices, summed_everywhere(): parts = lax.all_to_all(rows, axes, 0, 0, tiled=True)  14.8 us
    pallas_call x2, Pallas kernels, step(): pl.pallas_call(step_kernel, out_shape=jax.ShapeDtypeStruct(field.shape, f...  13.4 us
  transfers between devices with their start and end apart: 11, of which 3 were waited for; matrix products, arithmetic and copies ran while one was open for 8% of the time, Pallas kernels for 9%

profile of v1, /device:TPU:1, one launch (start us, length us, event | category | flops | bytes accessed | tf_op | source)
XLA Modules:
  0.0 222.5 jit_solution(14834128241318618742)
XLA Ops:
  0.0 1.0 fusion.139
  1.0 4.5 %collective-permute-start = (f32[1,64,384]{2,1,0:T(8,128)S(1)}, f32[1,64,384]{2,1,0:T(8,128)S(1)}, u32[]{:S(2)}, u32[]{:S(2)}) collective-permute-start(f32[1,64,384]{2,1,0:T(8,128)S(1)} %get-tuple-element.122), channel_id=1, source_target_pairs={{0,8},{8,16},{16,24},{24,32},{32,40},{40,48},{48,56},{56,64},{64,7... | collective-permute-start | bytes 294920 | tf_op jit(solution)/shard_map/ppermute | solution.py:29
  5.4 1.2 fusion.138
  6.6 1.7 collective-permute-start.2
  8.3 2.5 %collective-permute-start.3 = (f32[32,1,384]{2,1,0:T(1,128)S(1)}, f32[32,1,384]{2,1,0:T(1,128)S(1)}, u32[]{:S(2)}, u32[]{:S(2)}) collective-permute-start(f32[32,1,384]{2,1,0:T(1,128)S(1)} %get-tuple-element.119), channel_id=1, source_target_pairs={{1,0},{2,1},{3,2},{4,3},{5,4},{6,5},{7,6},{0,7},{9,8},{10,9},{11,1... | collective-permute-start | bytes 147464 | tf_op jit(solution)/shard_map/ppermute | solution.py:29
  10.9 0.8 compare_convert_fusion
  11.7 1.1 fusion.140
  12.8 1.5 slice_reduce_fusion.1
  14.3 1.5 fusion.142
  16.5 0.6 copy-done.4
  17.1 6.7 %shard_map.82.field_ref = f32[32,64,384]{2,1,0:T(8,128)} custom-call(f32[32,64,384]{2,1,0:T(8,128)} %field_ref.1, f32[1,64,384]{2,1,0:T(8,128)} %copy-done.3, f32[1,64,384]{2,1,0:T(8,128)} %copy-done.4, f32[32,1,384]{2,1,0:T(1,128)} %copy-done.7, f32[32,1,384]{2,1,0:T(1,128)} %copy-done.8), custom_call_target="tpu_custom_call" | custom-call | tf_op jit(solution)/shard_map/pallas_call | solution.py:104
  23.8 1.0 fusion.137
  24.8 1.2 fusion.136
  26.0 3.0 %collective-permute-start.4 = (f32[1,64,384]{2,1,0:T(8,128)S(1)}, f32[1,64,384]{2,1,0:T(8,128)S(1)}, u32[]{:S(2)}, u32[]{:S(2)}) collective-permute-start(f32[1,64,384]{2,1,0:T(8,128)S(1)} %get-tuple-element.118), channel_id=1, source_target_pairs={{0,8},{8,16},{16,24},{24,32},{32,40},{40,48},{48,56},{56,64},{64,7... | collective-permute-start | bytes 294920 | tf_op jit(solution)/shard_map/ppermute | solution.py:29
  29.0 2.3 %collective-permute-start.5 = (f32[1,64,384]{2,1,0:T(8,128)S(1)}, f32[1,64,384]{2,1,0:T(8,128)S(1)}, u32[]{:S(2)}, u32[]{:S(2)}) collective-permute-start(f32[1,64,384]{2,1,0:T(8,128)S(1)} %get-tuple-element.117), channel_id=1, source_target_pairs={{8,0},{16,8},{24,16},{32,24},{40,32},{48,40},{56,48},{64,56},{72,6... | collective-permute-start | bytes 294920 | tf_op jit(solution)/shard_map/ppermute | solution.py:29
  31.2 3.6 %collective-permute-start.7 = (f32[32,1,384]{2,1,0:T(1,128)S(1)}, f32[32,1,384]{2,1,0:T(1,128)S(1)}, u32[]{:S(2)}, u32[]{:S(2)}) collective-permute-start(f32[32,1,384]{2,1,0:T(1,128)S(1)} %get-tuple-element.115), channel_id=1, source_target_pairs={{1,0},{2,1},{3,2},{4,3},{5,4},{6,5},{7,6},{0,7},{9,8},{10,9},{11,1... | collective-permute-start | bytes 147464 | tf_op jit(solution)/shard_map/ppermute | solution.py:29
  34.9 0.6 mul.238.coef_ref
  35.5 0.9 collective-permute-done.6.south_ref
  36.4 0.6 copy-done.9
  37.1 0.6 copy-done.6
  37.7 6.7 %shard_map.83 = f32[32,64,384]{2,1,0:T(8,128)} custom-call(f32[32,64,384]{2,1,0:T(8,128)} %shard_map.82.field_ref, f32[1,64,384]{2,1,0:T(8,128)} %copy-done.5, f32[1,64,384]{2,1,0:T(8,128)} %copy-done.6, f32[32,1,384]{2,1,0:T(1,128)} %copy-done.9, f32[32,1,384]{2,1,0:T(1,128)} %copy-done.10), custom_call_target="tpu_custom_call" | custom-call | tf_op jit(solution)/shard_map/pallas_call | solution.py:104
  44.4 19.2 %shard_map.84 = f32[1024,512]{1,0:T(8,128)} custom-call(s32[4096]{0:T(1024)} %bitcast.108, s32[4096]{0:T(1024)} %bitcast.110, f32[12288]{0:T(1024)} %mul.238.coef_ref, f32[2048,384]{1,0:T(8,128)} %bitcast.91), custom_call_target="tpu_custom_call" | custom-call | tf_op jit(solution)/shard_map/pallas_call | solution.py:67
  63.7 3.8 %fusion.134 = f32[1024,128]{1,0:T(8,128)} fusion(f32[1024,512]{1,0:T(8,128)} %shard_map.84, s32[128]{0:T(128)S(1)} %get-tuple-element.152, s32[128]{0:T(128)S(1)} %get-tuple-element.153, s32[512]{0:T(512)S(1)} %get-tuple-element.143, s32[512]{0:T(512)S(1)} %get-tuple-element.145, s32[128]{0:T(128)S(1)} %get-tuple-element.151, ...), kind=kOutput, calls=%fused_computation.215 | convolution fusion | flops 805765120 | bytes 2632960 | tf_op jit(solution)/shard_map/dot_general | solution.py:113
  67.5 14.8 %all-to-all-start = ((f32[256,4,128]{2,1,0:T(4,128)}), f32[256,4,128]{2,1,0:T(4,128)S(1)}, u32[]{:S(2)}, u32[]{:S(2)}) async-start(f32[256,4,128]{2,1,0:T(4,128)} %bitcast.5), calls=%async_computation | async-start | bytes 1048576 | tf_op jit(solution)/shard_map/all_to_all | solution.py:142
  83.8 19.7 %all-to-all-done = f32[256,4,128]{2,1,0:T(4,128)S(1)} async-done(((f32[256,4,128]{2,1,0:T(4,128)}), f32[256,4,128]{2,1,0:T(4,128)S(1)}, u32[]{:S(2)}, u32[]{:S(2)}) %all-to-all-start) | async-done | bytes 524320 | tf_op jit(solution)/shard_map/all_to_all | solution.py:142
  103.8 0.9 broadcast_in_dim.70
  104.6 5.3 %all-to-all-start.1 = ((f32[256,4,128]{2,1,0:T(4,128)}), f32[256,4,128]{2,1,0:T(4,128)S(1)}, u32[]{:S(2)}, u32[]{:S(2)}) async-start(f32[256,4,128]{2,1,0:T(4,128)} %broadcast_in_dim.70), calls=%async_computation.1 | async-start | bytes 1048576 | tf_op jit(solution)/shard_map/all_to_all | solution.py:145
  112.9 0.6 mul.256.coef_ref
  113.5 19.2 %shard_map.85 = f32[1024,512]{1,0:T(8,128)} custom-call(s32[4096]{0:T(1024)} %bitcast.107, s32[4096]{0:T(1024)} %bitcast.109, f32[12288]{0:T(1024)} %mul.256.coef_ref, f32[2048,384]{1,0:T(8,128)} %bitcast.92), custom_call_target="tpu_custom_call" | custom-call | tf_op jit(solution)/shard_map/pallas_call | solution.py:67
  132.7 3.0 %fusion.132 = f32[1024,128]{1,0:T(8,128)S(1)} fusion(f32[1024,512]{1,0:T(8,128)} %shard_map.85, s32[128]{0:T(128)S(1)} %get-tuple-element.152, s32[128]{0:T(128)S(1)} %get-tuple-element.153, s32[512]{0:T(512)S(1)} %get-tuple-element.143, s32[512]{0:T(512)S(1)} %get-tuple-element.145, s32[128]{0:T(128)S(1)} %get-tuple-element.151, ...), kind=kOutput, calls=%fused_computation.214 | convolution fusion | flops 805765120 | bytes 2632960 | tf_op jit(solution)/shard_map/dot_general | solution.py:113
  135.8 0.8 multiply_reduce_fusion.1
  136.6 1.1 fusion.10
  137.8 0.6 reduce_max.18
  139.1 0.6 broadcast_divide_fusion.1
  139.7 2.2 %while.26 = (s32[]{:T(128)}, f32[32,32]{0,1:T(8,128)S(1)}, f32[32,32]{1,0:T(8,128)S(1)}, s32[]{:T(128)}) while((s32[]{:T(128)}, f32[32,32]{0,1:T(8,128)S(1)}, f32[32,32]{1,0:T(8,128)S(1)}, s32[]{:T(128)}) %tuple.82), condition=%wide.region_4.5_spmd.clone, body=%wide.region_3.4_spmd.clone.sunk | while | flops 1183746 | bytes 53301 | solution.py:206
  142.0 0.9 convolution_divide_fusion.1
  144.5 34.4 %all_to_all.33 = f32[256,4,128]{2,1,0:T(4,128)S(1)} all-to-all(f32[256,4,128]{2,1,0:T(4,128)S(1)} %copy.66), channel_id=1, replica_groups=mesh['gx'=32,'gy'=8] {'gx','gy'}, dimensions={0} | all-to-all | bytes 1048576 | tf_op jit(solution)/shard_map/all_to_all | solution.py:142
  179.2 0.9 broadcast_in_dim.78
  180.1 5.4 %all-to-all-start.3 = ((f32[256,4,128]{2,1,0:T(4,128)}), f32[256,4,128]{2,1,0:T(4,128)S(1)}, u32[]{:S(2)}, u32[]{:S(2)}) async-start(f32[256,4,128]{2,1,0:T(4,128)} %broadcast_in_dim.78), calls=%async_computation.3 | async-start | bytes 1048576 | tf_op jit(solution)/shard_map/all_to_all | solution.py:145
  189.5 16.8 %all-to-all-done.3 = f32[256,4,128]{2,1,0:T(4,128)S(1)} async-done(((f32[256,4,128]{2,1,0:T(4,128)}), f32[256,4,128]{2,1,0:T(4,128)S(1)}, u32[]{:S(2)}, u32[]{:S(2)}) %all-to-all-start.3) | async-done | bytes 524320 | tf_op jit(solution)/shard_map/all_to_all | solution.py:145
  206.3 0.7 multiply_reduce_fusion
  207.0 1.1 fusion.8
  208.2 0.6 reduce_max.19
  209.5 0.6 broadcast_divide_fusion
  210.2 2.2 %while.27 = (s32[]{:T(128)}, f32[32,32]{0,1:T(8,128)S(1)}, f32[32,32]{1,0:T(8,128)S(1)}, s32[]{:T(128)}) while((s32[]{:T(128)}, f32[32,32]{0,1:T(8,128)S(1)}, f32[32,32]{1,0:T(8,128)S(1)}, s32[]{:T(128)}) %tuple.81), condition=%wide.region_10.11_spmd.clone, body=%wide.region_9.10_spmd.clone.sunk | while | flops 1183746 | bytes 53301 | solution.py:206
  212.4 0.9 convolution_divide_fusion
  214.0 0.8 mul.274.mix_ref
  214.8 7.7 %shard_map.86 = f32[2048,384]{1,0:T(8,128)} custom-call(f32[2048,384]{1,0:T(8,128)} %bitcast.93, f32[128,128]{1,0:T(8,128)} %mul.274.mix_ref), custom_call_target="tpu_custom_call" | custom-call | tf_op jit(solution)/shard_map/pallas_call | solution.py:127
  (139 shorter events, 16.1 us)
Async XLA Ops:
  1.0 14.9 %collective-permute-start = (f32[1,64,384]{2,1,0:T(8,128)S(1)}, f32[1,64,384]{2,1,0:T(8,128)S(1)}, u32[]{:S(2)}, u32[]{:S(2)}) collective-permute-start(f32[1,64,384]{2,1,0:T(8,128)S(1)} %get-tuple-element.122), channel_id=1, source_target_pairs={{0,8},{8,16},{16,24},{24,32},{32,40},{40,48},{48,56},{56,64},{64,7... | collective-permute-start | bytes 294920 | tf_op jit(solution)/shard_map/ppermute | solution.py:29
  5.4 10.4 %collective-permute-start.1 = (f32[1,64,384]{2,1,0:T(8,128)S(1)}, f32[1,64,384]{2,1,0:T(8,128)S(1)}, u32[]{:S(2)}, u32[]{:S(2)}) collective-permute-start(f32[1,64,384]{2,1,0:T(8,128)S(1)} %get-tuple-element.121), channel_id=1, source_target_pairs={{8,0},{16,8},{24,16},{32,24},{40,32},{48,40},{56,48},{64,56},{72,6... | collective-permute-start | bytes 294920 | tf_op jit(solution)/shard_map/ppermute | solution.py:29
  6.6 9.2 %collective-permute-start.2 = (f32[32,1,384]{2,1,0:T(1,128)S(1)}, f32[32,1,384]{2,1,0:T(1,128)S(1)}, u32[]{:S(2)}, u32[]{:S(2)}) collective-permute-start(f32[32,1,384]{2,1,0:T(1,128)S(1)} %get-tuple-element.120), channel_id=1, source_target_pairs={{0,1},{1,2},{2,3},{3,4},{4,5},{5,6},{6,7},{7,0},{8,9},{9,10},{10,1... | collective-permute-start | bytes 147464 | tf_op jit(solution)/shard_map/ppermute | solution.py:29
  8.3 7.5 %collective-permute-start.3 = (f32[32,1,384]{2,1,0:T(1,128)S(1)}, f32[32,1,384]{2,1,0:T(1,128)S(1)}, u32[]{:S(2)}, u32[]{:S(2)}) collective-permute-start(f32[32,1,384]{2,1,0:T(1,128)S(1)} %get-tuple-element.119), channel_id=1, source_target_pairs={{1,0},{2,1},{3,2},{4,3},{5,4},{6,5},{7,6},{0,7},{9,8},{10,9},{11,1... | collective-permute-start | bytes 147464 | tf_op jit(solution)/shard_map/ppermute | solution.py:29
  15.8 0.6 copy-start.7
  15.8 0.6 copy-start.8
  15.8 0.6 copy-start.3
  16.5 0.6 copy-start.4
  26.0 10.4 %collective-permute-start.4 = (f32[1,64,384]{2,1,0:T(8,128)S(1)}, f32[1,64,384]{2,1,0:T(8,128)S(1)}, u32[]{:S(2)}, u32[]{:S(2)}) collective-permute-start(f32[1,64,384]{2,1,0:T(8,128)S(1)} %get-tuple-element.118), channel_id=1, source_target_pairs={{0,8},{8,16},{16,24},{24,32},{32,40},{40,48},{48,56},{56,64},{64,7... | collective-permute-start | bytes 294920 | tf_op jit(solution)/shard_map/ppermute | solution.py:29
  29.0 7.5 %collective-permute-start.5 = (f32[1,64,384]{2,1,0:T(8,128)S(1)}, f32[1,64,384]{2,1,0:T(8,128)S(1)}, u32[]{:S(2)}, u32[]{:S(2)}) collective-permute-start(f32[1,64,384]{2,1,0:T(8,128)S(1)} %get-tuple-element.117), channel_id=1, source_target_pairs={{8,0},{16,8},{24,16},{32,24},{40,32},{48,40},{56,48},{64,56},{72,6... | collective-permute-start | bytes 294920 | tf_op jit(solution)/shard_map/ppermute | solution.py:29
  31.2 5.2 %collective-permute-start.6 = (f32[32,1,384]{2,1,0:T(1,128)S(1)}, f32[32,1,384]{2,1,0:T(1,128)S(1)}, u32[]{:S(2)}, u32[]{:S(2)}) collective-permute-start(f32[32,1,384]{2,1,0:T(1,128)S(1)} %get-tuple-element.116), channel_id=1, source_target_pairs={{0,1},{1,2},{2,3},{3,4},{4,5},{5,6},{6,7},{7,0},{8,9},{9,10},{10,1... | collective-permute-start | bytes 147464 | tf_op jit(solution)/shard_map/ppermute | solution.py:29
  31.2 5.2 %collective-permute-start.7 = (f32[32,1,384]{2,1,0:T(1,128)S(1)}, f32[32,1,384]{2,1,0:T(1,128)S(1)}, u32[]{:S(2)}, u32[]{:S(2)}) collective-permute-start(f32[32,1,384]{2,1,0:T(1,128)S(1)} %get-tuple-element.115), channel_id=1, source_target_pairs={{1,0},{2,1},{3,2},{4,3},{5,4},{6,5},{7,6},{0,7},{9,8},{10,9},{11,1... | collective-permute-start | bytes 147464 | tf_op jit(solution)/shard_map/ppermute | solution.py:29
  36.4 0.6 copy-start.9
  36.4 0.6 copy-start.10
  36.4 0.7 copy-start.5
  37.1 0.6 copy-start.6
  67.5 42.5 %copy-start.13 = (s32[1,1,2,16]{3,2,1,0:T(2,128)S(1)}, s32[1,1,2,16]{3,2,1,0:T(2,128)}, u32[]{:S(2)}) copy-start(s32[1,1,2,16]{3,2,1,0:T(2,128)} %param.19) | copy-start | bytes 388
  67.5 36.0 %all-to-all-start = ((f32[256,4,128]{2,1,0:T(4,128)}), f32[256,4,128]{2,1,0:T(4,128)S(1)}, u32[]{:S(2)}, u32[]{:S(2)}) async-start(f32[256,4,128]{2,1,0:T(4,128)} %bitcast.5), calls=%async_computation | async-start | bytes 1048576 | tf_op jit(solution)/shard_map/all_to_all | solution.py:142
  82.3 28.2 %copy-start.11 = (f32[2,4096]{1,0:T(2,128)S(1)}, f32[2,4096]{1,0:T(2,128)}, u32[]{:S(2)}) copy-start(f32[2,4096]{1,0:T(2,128)} %param.17) | copy-start | bytes 98308
  82.3 28.2 %copy-start.12 = (f32[2,4096]{1,0:T(2,128)S(1)}, f32[2,4096]{1,0:T(2,128)}, u32[]{:S(2)}) copy-start(f32[2,4096]{1,0:T(2,128)} %param.18) | copy-start | bytes 98308
  104.6 31.2 %all-to-all-start.1 = ((f32[256,4,128]{2,1,0:T(4,128)}), f32[256,4,128]{2,1,0:T(4,128)S(1)}, u32[]{:S(2)}, u32[]{:S(2)}) async-start(f32[256,4,128]{2,1,0:T(4,128)} %broadcast_in_dim.70), calls=%async_computation.1 | async-start | bytes 1048576 | tf_op jit(solution)/shard_map/all_to_all | solution.py:145
  112.8 23.0 %copy-start = (f32[32,32]{1,0:T(8,128)}, f32[32,32]{1,0:T(8,128)S(1)}, u32[]{:S(2)}) copy-start(f32[32,32]{1,0:T(8,128)S(1)} %copy.60) | copy-start | bytes 12292
  135.8 3.9 %copy-start.2 = (f32[32,32]{1,0:T(8,128)S(1)}, f32[32,32]{1,0:T(8,128)}, u32[]{:S(2)}) copy-start(f32[32,32]{1,0:T(8,128)} %copy-done) | copy-start | bytes 12292
  180.1 26.2 %all-to-all-start.3 = ((f32[256,4,128]{2,1,0:T(4,128)}), f32[256,4,128]{2,1,0:T(4,128)S(1)}, u32[]{:S(2)}, u32[]{:S(2)}) async-start(f32[256,4,128]{2,1,0:T(4,128)} %broadcast_in_dim.78), calls=%async_computation.3 | async-start | bytes 1048576 | tf_op jit(solution)/shard_map/all_to_all | solution.py:145
  206.3 3.9 %copy-start.1 = (f32[32,32]{1,0:T(8,128)S(1)}, f32[32,32]{1,0:T(8,128)}, u32[]{:S(2)}) copy-start(f32[32,32]{1,0:T(8,128)} %copy-done) | copy-start | bytes 12292

commit v2 on v1

--- a/solution.py
+++ b/solution.py
@@ -30,35 +30,38 @@
     return step(field, *halos)
 
 
-def gather_kernel(cell_ref, level_ref, coef_ref, field_ref, out_ref):
+def gather_kernel(flag_ref, cell_ref, level_ref, coef_ref, field_ref, out_ref, chosen_ref):
     count = cell_ref.shape[0]
-    width = field_ref.shape[1] // 3
+    groups, rows, width = out_ref.shape
     lane_level = lax.broadcasted_iota(jnp.int32, (1, width), 1) // ENS
     sublane = lax.broadcasted_iota(jnp.int32, (8, width), 0)
-    groups = width // ENS
-
-    def body(block, carry):
-        gathered = [jnp.zeros((8, width), jnp.float32) for k in range(groups)]
-        for i in range(8):
-            for k in range(groups):
-                j = (block * 8 + i) * groups + k
-                picked = field_ref[pl.ds(cell_ref[j], 1), :]
-                value = (
-                    coef_ref[j] * picked[:, 0:width]
-                    + coef_ref[count + j] * picked[:, width:2 * width]
-                    + coef_ref[2 * count + j] * picked[:, 2 * width:3 * width]
-                )
-                value = jnp.where(lane_level == level_ref[j], value, 0.0)
-                gathered[k] = jnp.where(sublane == i, value, gathered[k])
-        first = pl.multiple_of(block * 8, 8)
-        for k in range(groups):
-            out_ref[pl.ds(first, 8), k * width:(k + 1) * width] = gathered[k]
+    out_ref[...] = jnp.zeros(out_ref.shape, out_ref.dtype)
+
+    def choose(j, taken):
+        chosen_ref[taken] = j
+        return taken + flag_ref[j]
+
+    taken = lax.fori_loop(0, count, choose, 0, unroll=8)
+
+    def body(i, carry):
+        j = chosen_ref[i]
+        picked = field_ref[pl.ds(cell_ref[j], 1), :]
+        value = (
+            coef_ref[j] * picked[:, 0:width]
+            + coef_ref[count + j] * picked[:, width:2 * width]
+            + coef_ref[2 * count + j] * picked[:, 2 * width:3 * width]
+        )
+        value = jnp.where(lane_level == level_ref[j], value, 0.0)
+        row = j // groups
+        first = pl.multiple_of((row // 8) * 8, 8)
+        tile = out_ref[j % groups, pl.ds(first, 8), :]
+        out_ref[j % groups, pl.ds(first, 8), :] = jnp.where(sublane == row % 8, value, tile)
         return carry
 
-    lax.fori_loop(0, count // (8 * groups), body, 0)
-
-
-def gather_rows(cells, levels, coefs, field):
+    lax.fori_loop(0, taken, body, 0)
+
+
+def gather_rows(flags, cells, levels, coefs, field):
     count = cells.shape[0]
     width = field.shape[1] // 3
     groups = width // ENS
@@ -66,10 +69,12 @@
     vmem = pl.BlockSpec(memory_space=pltpu.VMEM)
     return pl.pallas_call(
         gather_kernel,
-        out_shape=jax.ShapeDtypeStruct((count // groups, groups * width), jnp.float32),
-        in_specs=[smem, smem, smem, vmem],
+        out_shape=jax.ShapeDtypeStruct((groups, count // groups, width), jnp.float32),
+        in_specs=[smem, smem, smem, smem, vmem],
         out_specs=vmem,
-    )(cells, levels, coefs.reshape(-1), field)
+        scratch_shapes=[pltpu.SMEM((count,), jnp.int32)],
+    )(flags, cells, levels, coefs.reshape(-1), field)
+
 
 def step_kernel(field_ref, west_ref, east_ref, south_ref, north_ref, out_ref):
     nx, ny, feat = field_ref.shape
@@ -123,7 +128,7 @@
 def mixed_once(rows, mix):
     count, features = rows.shape
     width = mix.shape[0]
-    tile = 256
+    tile = 512
     return pl.pallas_call(
         mix_kernel,
         out_shape=jax.ShapeDtypeStruct(rows.shape, rows.dtype),
@@ -229,17 +234,27 @@
     width = features // COMP
     groups = width // ENS
     owned = (obs_owner == own_tile).astype(jnp.float32)
-    spread_lane = lax.broadcasted_iota(jnp.int32, (groups * width, groups * ENS), 0)
-    dense_lane = lax.broadcasted_iota(jnp.int32, (groups * width, groups * ENS), 1)
-    fold = (
-        (spread_lane // width == dense_lane // ENS) & (spread_lane % ENS == dense_lane % ENS)
-    ).astype(jnp.float32)
+    lane_in = lax.broadcasted_iota(jnp.int32, (groups, width, groups * ENS), 0)
+    level_lane = lax.broadcasted_iota(jnp.int32, (groups, width, groups * ENS), 1)
+    dense_lane = lax.broadcasted_iota(jnp.int32, (groups, width, groups * ENS), 2)
+    fold = ((lane_in == dense_lane // ENS) & (level_lane % ENS == dense_lane % ENS)).astype(jnp.float32)
+
+    def folded(spread):
+        return jnp.einsum(
+            "krl,klo->ro", spread, fold, precision=lax.Precision.HIGHEST,
+            preferred_element_type=jnp.float32,
+        )
 
     def observed(batch_index):
         masked_coefs = obs_coef[batch_index] * owned[batch_index][None, :]
-        spread = gather_rows(obs_cell[batch_index], obs_level[batch_index], masked_coefs, cells)
-        return product(spread, fold)
-
+        spread = gather_rows(
+            owned[batch_index].astype(jnp.int32),
+            obs_cell[batch_index],
+            obs_level[batch_index],
+            masked_coefs,
+            cells,
+        )
+        return folded(spread)
 
     def mixing(local_terms, batch_index):
         predicted = summed_everywhere(local_terms)

time: 223 us -> 219 us (0.982); the launches traced: 223 us -> 223 us
  Pallas kernels: 59.6 us -> 41.5 us
  blocking collectives: 34.4 us -> 42.1 us
  starting transfers between devices: 43.1 us -> 50.7 us
  waiting for transfers between devices: 37.4 us -> 39.7 us
    pallas_call x2, Pallas kernels: 38.4 us -> 22.2 us  [gather_rows(): pl.pallas_call(gather_kernel, out_shape=jax.ShapeDtypeStruct((groups, cou...]
    all_to_all x1, blocking collectives: 34.4 us -> 42.1 us  [summed_everywhere(): parts = lax.all_to_all(rows, axes, 0, 0, tiled=True)]
    all_to_all x1, starting transfers between devices: 14.8 us -> 22.5 us  [summed_everywhere(): parts = lax.all_to_all(rows, axes, 0, 0, tiled=True)]
    dot_general x38 -> x36, matrix products: 17.9 us -> 11 us  [product(): jnp.dot(left, right, precision=lax.Precision.HIGHEST, preferred_element_t...]
    dot_general x0 -> x2, matrix products: none -> 6.31 us  [folded(): jnp.einsum('krl,klo->ro', spread, fold, precision=lax.Precision.HIGHEST,...]
    all_to_all x2, waiting for transfers between devices: 16.8 us -> 19.7 us  [summed_everywhere(): return lax.all_to_all(copies, axes, 0, 0, tiled=True)]
  transfers between devices with their start and end apart: 11 -> 11, of which waited for: 3 -> 4; matrix products, arithmetic and copies ran while one was open for 8% -> 9% of each run, Pallas kernels for 9% -> 5%
where the time goes in v2:
time: 219 us; the launch traced here: 223 us
  starting transfers between devices  50.7 us (23%)
  blocking collectives  42.1 us (19%)
  Pallas kernels  41.5 us (19%)
  waiting for transfers between devices  39.7 us (18%)
  local copies, waits for them, and re-layouts  21.8 us (10%)
  matrix products  17.3 us (8%)
  other arithmetic  7.01 us (3%)
    all_to_all x1, blocking collectives, summed_everywhere(): parts = lax.all_to_all(rows, axes, 0, 0, tiled=True)  42.1 us
    all_to_all x1, starting transfers between devices, summed_everywhere(): parts = lax.all_to_all(rows, axes, 0, 0, tiled=True)  22.5 us
    pallas_call x2, Pallas kernels, gather_rows(): pl.pallas_call(gather_kernel, out_shape=jax.ShapeDtypeStruct((groups, cou...  22.2 us
    all_to_all x2, waiting for transfers between devices, summed_everywhere(): return lax.all_to_all(copies, axes, 0, 0, tiled=True)  19.7 us
    all_to_all x1, waiting for transfers between devices, summed_everywhere(): parts = lax.all_to_all(rows, axes, 0, 0, tiled=True)  19.7 us
    ppermute x8, starting transfers between devices, advance_once(): halos += [lax.ppermute(last, axis, up), lax.ppermute(initial, axis, down)]  17.6 us
    pallas_call x2, Pallas kernels, step(): pl.pallas_call(step_kernel, out_shape=jax.ShapeDtypeStruct(field.shape, f...  13.5 us
    dot_general x36, matrix products, product(): jnp.dot(left, right, precision=lax.Precision.HIGHEST, preferred_element_t...  11 us
  transfers between devices with their start and end apart: 11, of which 4 were waited for; matrix products, arithmetic and copies ran while one was open for 9% of the time, Pallas kernels for 5%

profile of v2, /device:TPU:1, one launch (start us, length us, event | category | flops | bytes accessed | tf_op | source)
XLA Modules:
  0.0 222.5 jit_solution(15319194497544177158)
XLA Ops:
  0.0 1.0 fusion.132
  1.0 4.5 %collective-permute-start = (f32[1,64,384]{2,1,0:T(8,128)S(1)}, f32[1,64,384]{2,1,0:T(8,128)S(1)}, u32[]{:S(2)}, u32[]{:S(2)}) collective-permute-start(f32[1,64,384]{2,1,0:T(8,128)S(1)} %get-tuple-element.122), channel_id=1, source_target_pairs={{0,8},{8,16},{16,24},{24,32},{32,40},{40,48},{48,56},{56,64},{64,7... | collective-permute-start | bytes 294920 | tf_op jit(solution)/shard_map/ppermute | solution.py:29
  5.4 1.2 fusion.131
  6.6 1.7 collective-permute-start.2
  8.3 2.5 %collective-permute-start.3 = (f32[32,1,384]{2,1,0:T(1,128)S(1)}, f32[32,1,384]{2,1,0:T(1,128)S(1)}, u32[]{:S(2)}, u32[]{:S(2)}) collective-permute-start(f32[32,1,384]{2,1,0:T(1,128)S(1)} %get-tuple-element.119), channel_id=1, source_target_pairs={{1,0},{2,1},{3,2},{4,3},{5,4},{6,5},{7,6},{0,7},{9,8},{10,9},{11,1... | collective-permute-start | bytes 147464 | tf_op jit(solution)/shard_map/ppermute | solution.py:29
  10.9 0.8 compare_convert_fusion
  11.7 1.1 fusion.133
  12.7 1.5 slice_reduce_fusion.1
  14.3 1.5 fusion.134
  16.4 0.6 copy-done.4
  17.1 6.7 %shard_map.82.field_ref = f32[32,64,384]{2,1,0:T(8,128)} custom-call(f32[32,64,384]{2,1,0:T(8,128)} %field_ref.1, f32[1,64,384]{2,1,0:T(8,128)} %copy-done.3, f32[1,64,384]{2,1,0:T(8,128)} %copy-done.4, f32[32,1,384]{2,1,0:T(1,128)} %copy-done.7, f32[32,1,384]{2,1,0:T(1,128)} %copy-done.8), custom_call_target="tpu_custom_call" | custom-call | tf_op jit(solution)/shard_map/pallas_call | solution.py:109
  23.8 1.0 fusion.130
  24.7 1.2 fusion.129
  25.9 3.0 %collective-permute-start.4 = (f32[1,64,384]{2,1,0:T(8,128)S(1)}, f32[1,64,384]{2,1,0:T(8,128)S(1)}, u32[]{:S(2)}, u32[]{:S(2)}) collective-permute-start(f32[1,64,384]{2,1,0:T(8,128)S(1)} %get-tuple-element.118), channel_id=1, source_target_pairs={{0,8},{8,16},{16,24},{24,32},{32,40},{40,48},{48,56},{56,64},{64,7... | collective-permute-start | bytes 294920 | tf_op jit(solution)/shard_map/ppermute | solution.py:29
  28.9 2.3 %collective-permute-start.5 = (f32[1,64,384]{2,1,0:T(8,128)S(1)}, f32[1,64,384]{2,1,0:T(8,128)S(1)}, u32[]{:S(2)}, u32[]{:S(2)}) collective-permute-start(f32[1,64,384]{2,1,0:T(8,128)S(1)} %get-tuple-element.117), channel_id=1, source_target_pairs={{8,0},{16,8},{24,16},{32,24},{40,32},{48,40},{56,48},{64,56},{72,6... | collective-permute-start | bytes 294920 | tf_op jit(solution)/shard_map/ppermute | solution.py:29
  31.2 3.6 %collective-permute-start.7 = (f32[32,1,384]{2,1,0:T(1,128)S(1)}, f32[32,1,384]{2,1,0:T(1,128)S(1)}, u32[]{:S(2)}, u32[]{:S(2)}) collective-permute-start(f32[32,1,384]{2,1,0:T(1,128)S(1)} %get-tuple-element.115), channel_id=1, source_target_pairs={{1,0},{2,1},{3,2},{4,3},{5,4},{6,5},{7,6},{0,7},{9,8},{10,9},{11,1... | collective-permute-start | bytes 147464 | tf_op jit(solution)/shard_map/ppermute | solution.py:29
  35.5 0.6 mul.233.coef_ref
  37.0 0.6 copy-done.6
  37.7 6.7 %shard_map.83 = f32[32,64,384]{2,1,0:T(8,128)} custom-call(f32[32,64,384]{2,1,0:T(8,128)} %shard_map.82.field_ref, f32[1,64,384]{2,1,0:T(8,128)} %copy-done.5, f32[1,64,384]{2,1,0:T(8,128)} %copy-done.6, f32[32,1,384]{2,1,0:T(1,128)} %copy-done.9, f32[32,1,384]{2,1,0:T(1,128)} %copy-done.10), custom_call_target="tpu_custom_call" | custom-call | tf_op jit(solution)/shard_map/pallas_call | solution.py:109
  44.4 11.1 %shard_map.84 = f32[4,1024,128]{2,1,0:T(8,128)} custom-call(s32[4096]{0:T(1024)} %convert_element_type.102.flag_ref, s32[4096]{0:T(1024)} %bitcast.116, s32[4096]{0:T(1024)} %bitcast.118, f32[12288]{0:T(1024)} %mul.233.coef_ref, f32[2048,384]{1,0:T(8,128)} %bitcast.95), custom_call_target="tpu_custom_call" | custom-call | tf_op jit(solution)/shard_map/pallas_call | solution.py:70
  55.5 3.6 %fusion.127 = f32[1024,128,1]{1,0,2:T(8,128)} fusion(f32[4,1024,128]{2,1,0:T(8,128)} %shard_map.84, s32[128]{0:T(128)S(1)} %get-tuple-element.146, s32[128]{0:T(128)S(1)} %get-tuple-element.147, s32[128]{0:T(128)S(1)} %get-tuple-element.145, s32[128]{0:T(128)S(1)} %get-tuple-element.148, pred[128]{0:T(512)(128)(4,1)S(1)} %get-tuple-element.143, ...), kind=kOutput, calls=%fused_computation.203 | convolution fusion | flops 805699584 | bytes 2623744 | tf_op jit(solution)/shard_map/krl,klo->ro/dot_general | solution.py:243
  59.0 22.5 %all-to-all-start = ((f32[256,4,128]{2,1,0:T(4,128)}), f32[256,4,128]{2,1,0:T(4,128)S(1)}, u32[]{:S(2)}, u32[]{:S(2)}) async-start(f32[256,4,128]{2,1,0:T(4,128)} %bitcast.6), calls=%async_computation | async-start | bytes 1048576 | tf_op jit(solution)/shard_map/all_to_all | solution.py:147
  83.0 19.7 %all-to-all-done = f32[256,4,128]{2,1,0:T(4,128)S(1)} async-done(((f32[256,4,128]{2,1,0:T(4,128)}), f32[256,4,128]{2,1,0:T(4,128)S(1)}, u32[]{:S(2)}, u32[]{:S(2)}) %all-to-all-start) | async-done | bytes 524320 | tf_op jit(solution)/shard_map/all_to_all | solution.py:147
  103.0 0.9 broadcast_in_dim.70
  103.8 5.3 %all-to-all-start.1 = ((f32[256,4,128]{2,1,0:T(4,128)}), f32[256,4,128]{2,1,0:T(4,128)S(1)}, u32[]{:S(2)}, u32[]{:S(2)}) async-start(f32[256,4,128]{2,1,0:T(4,128)} %broadcast_in_dim.70), calls=%async_computation.1 | async-start | bytes 1048576 | tf_op jit(solution)/shard_map/all_to_all | solution.py:150
  112.0 0.6 convert_element_type.109.flag_ref
  112.6 0.6 mul.250.coef_ref
  113.3 11.2 %shard_map.85 = f32[4,1024,128]{2,1,0:T(8,128)} custom-call(s32[4096]{0:T(1024)} %convert_element_type.109.flag_ref, s32[4096]{0:T(1024)} %bitcast.115, s32[4096]{0:T(1024)} %bitcast.117, f32[12288]{0:T(1024)} %mul.250.coef_ref, f32[2048,384]{1,0:T(8,128)} %bitcast.96), custom_call_target="tpu_custom_call" | custom-call | tf_op jit(solution)/shard_map/pallas_call | solution.py:70
  124.4 2.8 %fusion.125 = f32[1024,128,1]{1,0,2:T(8,128)S(1)} fusion(f32[4,1024,128]{2,1,0:T(8,128)} %shard_map.85, s32[128]{0:T(128)S(1)} %get-tuple-element.146, s32[128]{0:T(128)S(1)} %get-tuple-element.147, s32[128]{0:T(128)S(1)} %get-tuple-element.145, s32[128]{0:T(128)S(1)} %get-tuple-element.148, pred[128]{0:T(512)(128)(4,1)S(1)} %get-tuple-element.143, ...), kind=kOutput, calls=%fused_computation.202 | convolution fusion | flops 805699584 | bytes 2623744 | tf_op jit(solution)/shard_map/krl,klo->ro/dot_general | solution.py:243
  127.2 2.9 %all-to-all-done.1 = f32[256,4,128]{2,1,0:T(4,128)S(1)} async-done(((f32[256,4,128]{2,1,0:T(4,128)}), f32[256,4,128]{2,1,0:T(4,128)S(1)}, u32[]{:S(2)}, u32[]{:S(2)}) %all-to-all-start.1) | async-done | bytes 524320 | tf_op jit(solution)/shard_map/all_to_all | solution.py:150
  130.1 0.8 multiply_reduce_fusion.1
  130.9 1.1 fusion.10
  132.0 0.6 reduce_max.18
  133.3 0.6 broadcast_divide_fusion.1
  134.0 2.2 %while.26 = (s32[]{:T(128)}, f32[32,32]{0,1:T(8,128)S(1)}, f32[32,32]{1,0:T(8,128)S(1)}, s32[]{:T(128)}) while((s32[]{:T(128)}, f32[32,32]{0,1:T(8,128)S(1)}, f32[32,32]{1,0:T(8,128)S(1)}, s32[]{:T(128)}) %tuple.79), condition=%wide.region_4.5_spmd.clone, body=%wide.region_3.4_spmd.clone.sunk | while | flops 1183746 | bytes 53301 | solution.py:211
  136.3 0.9 convolution_divide_fusion.1
  138.8 42.1 %all_to_all.33 = f32[256,4,128]{2,1,0:T(4,128)S(1)} all-to-all(f32[256,4,128]{2,1,0:T(4,128)S(1)} %copy.66), channel_id=1, replica_groups=mesh['gx'=32,'gy'=8] {'gx','gy'}, dimensions={0} | all-to-all | bytes 1048576 | tf_op jit(solution)/shard_map/all_to_all | solution.py:147
  181.1 0.9 broadcast_in_dim.78
  182.0 5.4 %all-to-all-start.3 = ((f32[256,4,128]{2,1,0:T(4,128)}), f32[256,4,128]{2,1,0:T(4,128)S(1)}, u32[]{:S(2)}, u32[]{:S(2)}) async-start(f32[256,4,128]{2,1,0:T(4,128)} %broadcast_in_dim.78), calls=%async_computation.3 | async-start | bytes 1048576 | tf_op jit(solution)/shard_map/all_to_all | solution.py:150
  191.4 16.8 %all-to-all-done.3 = f32[256,4,128]{2,1,0:T(4,128)S(1)} async-done(((f32[256,4,128]{2,1,0:T(4,128)}), f32[256,4,128]{2,1,0:T(4,128)S(1)}, u32[]{:S(2)}, u32[]{:S(2)}) %all-to-all-start.3) | async-done | bytes 524320 | tf_op jit(solution)/shard_map/all_to_all | solution.py:150
  208.2 0.7 multiply_reduce_fusion
  208.9 1.1 fusion.8
  210.1 0.6 reduce_max.19
  211.4 0.6 broadcast_divide_fusion
  212.1 2.2 %while.27 = (s32[]{:T(128)}, f32[32,32]{0,1:T(8,128)S(1)}, f32[32,32]{1,0:T(8,128)S(1)}, s32[]{:T(128)}) while((s32[]{:T(128)}, f32[32,32]{0,1:T(8,128)S(1)}, f32[32,32]{1,0:T(8,128)S(1)}, s32[]{:T(128)}) %tuple.78), condition=%wide.region_10.11_spmd.clone, body=%wide.region_9.10_spmd.clone.sunk | while | flops 1183746 | bytes 53301 | solution.py:211
  214.3 0.9 convolution_divide_fusion
  215.9 0.8 mul.268.mix_ref
  216.7 5.9 %shard_map.86 = f32[2048,384]{1,0:T(8,128)} custom-call(f32[2048,384]{1,0:T(8,128)} %bitcast.97, f32[128,128]{1,0:T(8,128)} %mul.268.mix_ref), custom_call_target="tpu_custom_call" | custom-call | tf_op jit(solution)/shard_map/pallas_call | solution.py:132
  (138 shorter events, 17.6 us)
Async XLA Ops:
  1.0 14.8 %collective-permute-start = (f32[1,64,384]{2,1,0:T(8,128)S(1)}, f32[1,64,384]{2,1,0:T(8,128)S(1)}, u32[]{:S(2)}, u32[]{:S(2)}) collective-permute-start(f32[1,64,384]{2,1,0:T(8,128)S(1)} %get-tuple-element.122), channel_id=1, source_target_pairs={{0,8},{8,16},{16,24},{24,32},{32,40},{40,48},{48,56},{56,64},{64,7... | collective-permute-start | bytes 294920 | tf_op jit(solution)/shard_map/ppermute | solution.py:29
  5.4 10.4 %collective-permute-start.1 = (f32[1,64,384]{2,1,0:T(8,128)S(1)}, f32[1,64,384]{2,1,0:T(8,128)S(1)}, u32[]{:S(2)}, u32[]{:S(2)}) collective-permute-start(f32[1,64,384]{2,1,0:T(8,128)S(1)} %get-tuple-element.121), channel_id=1, source_target_pairs={{8,0},{16,8},{24,16},{32,24},{40,32},{48,40},{56,48},{64,56},{72,6... | collective-permute-start | bytes 294920 | tf_op jit(solution)/shard_map/ppermute | solution.py:29
  6.6 9.1 %collective-permute-start.2 = (f32[32,1,384]{2,1,0:T(1,128)S(1)}, f32[32,1,384]{2,1,0:T(1,128)S(1)}, u32[]{:S(2)}, u32[]{:S(2)}) collective-permute-start(f32[32,1,384]{2,1,0:T(1,128)S(1)} %get-tuple-element.120), channel_id=1, source_target_pairs={{0,1},{1,2},{2,3},{3,4},{4,5},{5,6},{6,7},{7,0},{8,9},{9,10},{10,1... | collective-permute-start | bytes 147464 | tf_op jit(solution)/shard_map/ppermute | solution.py:29
  8.3 7.4 %collective-permute-start.3 = (f32[32,1,384]{2,1,0:T(1,128)S(1)}, f32[32,1,384]{2,1,0:T(1,128)S(1)}, u32[]{:S(2)}, u32[]{:S(2)}) collective-permute-start(f32[32,1,384]{2,1,0:T(1,128)S(1)} %get-tuple-element.119), channel_id=1, source_target_pairs={{1,0},{2,1},{3,2},{4,3},{5,4},{6,5},{7,6},{0,7},{9,8},{10,9},{11,1... | collective-permute-start | bytes 147464 | tf_op jit(solution)/shard_map/ppermute | solution.py:29
  15.8 0.6 copy-start.7
  15.8 0.6 copy-start.8
  15.8 0.6 copy-start.3
  16.4 0.6 copy-start.4
  25.9 10.4 %collective-permute-start.4 = (f32[1,64,384]{2,1,0:T(8,128)S(1)}, f32[1,64,384]{2,1,0:T(8,128)S(1)}, u32[]{:S(2)}, u32[]{:S(2)}) collective-permute-start(f32[1,64,384]{2,1,0:T(8,128)S(1)} %get-tuple-element.118), channel_id=1, source_target_pairs={{0,8},{8,16},{16,24},{24,32},{32,40},{40,48},{48,56},{56,64},{64,7... | collective-permute-start | bytes 294920 | tf_op jit(solution)/shard_map/ppermute | solution.py:29
  28.9 7.5 %collective-permute-start.5 = (f32[1,64,384]{2,1,0:T(8,128)S(1)}, f32[1,64,384]{2,1,0:T(8,128)S(1)}, u32[]{:S(2)}, u32[]{:S(2)}) collective-permute-start(f32[1,64,384]{2,1,0:T(8,128)S(1)} %get-tuple-element.117), channel_id=1, source_target_pairs={{8,0},{16,8},{24,16},{32,24},{40,32},{48,40},{56,48},{64,56},{72,6... | collective-permute-start | bytes 294920 | tf_op jit(solution)/shard_map/ppermute | solution.py:29
  31.2 5.2 %collective-permute-start.6 = (f32[32,1,384]{2,1,0:T(1,128)S(1)}, f32[32,1,384]{2,1,0:T(1,128)S(1)}, u32[]{:S(2)}, u32[]{:S(2)}) collective-permute-start(f32[32,1,384]{2,1,0:T(1,128)S(1)} %get-tuple-element.116), channel_id=1, source_target_pairs={{0,1},{1,2},{2,3},{3,4},{4,5},{5,6},{6,7},{7,0},{8,9},{9,10},{10,1... | collective-permute-start | bytes 147464 | tf_op jit(solution)/shard_map/ppermute | solution.py:29
  31.2 5.2 %collective-permute-start.7 = (f32[32,1,384]{2,1,0:T(1,128)S(1)}, f32[32,1,384]{2,1,0:T(1,128)S(1)}, u32[]{:S(2)}, u32[]{:S(2)}) collective-permute-start(f32[32,1,384]{2,1,0:T(1,128)S(1)} %get-tuple-element.115), channel_id=1, source_target_pairs={{1,0},{2,1},{3,2},{4,3},{5,4},{6,5},{7,6},{0,7},{9,8},{10,9},{11,1... | collective-permute-start | bytes 147464 | tf_op jit(solution)/shard_map/ppermute | solution.py:29
  36.4 0.6 copy-start.9
  36.4 0.6 copy-start.10
  36.4 0.7 copy-start.5
  37.0 0.6 copy-start.6
  59.0 50.1 %copy-start.13 = (s32[1,1,2,16]{3,2,1,0:T(2,128)S(1)}, s32[1,1,2,16]{3,2,1,0:T(2,128)}, u32[]{:S(2)}) copy-start(s32[1,1,2,16]{3,2,1,0:T(2,128)} %param.19) | copy-start | bytes 388
  59.0 43.6 %all-to-all-start = ((f32[256,4,128]{2,1,0:T(4,128)}), f32[256,4,128]{2,1,0:T(4,128)S(1)}, u32[]{:S(2)}, u32[]{:S(2)}) async-start(f32[256,4,128]{2,1,0:T(4,128)} %bitcast.6), calls=%async_computation | async-start | bytes 1048576 | tf_op jit(solution)/shard_map/all_to_all | solution.py:147
  81.5 28.2 %copy-start.11 = (f32[2,4096]{1,0:T(2,128)S(1)}, f32[2,4096]{1,0:T(2,128)}, u32[]{:S(2)}) copy-start(f32[2,4096]{1,0:T(2,128)} %param.17) | copy-start | bytes 98308
  81.5 28.2 %copy-start.12 = (f32[2,4096]{1,0:T(2,128)S(1)}, f32[2,4096]{1,0:T(2,128)}, u32[]{:S(2)}) copy-start(f32[2,4096]{1,0:T(2,128)} %param.18) | copy-start | bytes 98308
  103.8 26.3 %all-to-all-start.1 = ((f32[256,4,128]{2,1,0:T(4,128)}), f32[256,4,128]{2,1,0:T(4,128)S(1)}, u32[]{:S(2)}, u32[]{:S(2)}) async-start(f32[256,4,128]{2,1,0:T(4,128)} %broadcast_in_dim.70), calls=%async_computation.1 | async-start | bytes 1048576 | tf_op jit(solution)/shard_map/all_to_all | solution.py:150
  112.0 15.2 %copy-start = (f32[32,32]{1,0:T(8,128)}, f32[32,32]{1,0:T(8,128)S(1)}, u32[]{:S(2)}) copy-start(f32[32,32]{1,0:T(8,128)S(1)} %copy.60) | copy-start | bytes 12292
  130.1 3.9 %copy-start.2 = (f32[32,32]{1,0:T(8,128)S(1)}, f32[32,32]{1,0:T(8,128)}, u32[]{:S(2)}) copy-start(f32[32,32]{1,0:T(8,128)} %copy-done) | copy-start | bytes 12292
  182.0 26.2 %all-to-all-start.3 = ((f32[256,4,128]{2,1,0:T(4,128)}), f32[256,4,128]{2,1,0:T(4,128)S(1)}, u32[]{:S(2)}, u32[]{:S(2)}) async-start(f32[256,4,128]{2,1,0:T(4,128)} %broadcast_in_dim.78), calls=%async_computation.3 | async-start | bytes 1048576 | tf_op jit(solution)/shard_map/all_to_all | solution.py:150
  208.2 3.9 %copy-start.1 = (f32[32,32]{1,0:T(8,128)S(1)}, f32[32,32]{1,0:T(8,128)}, u32[]{:S(2)}) copy-start(f32[32,32]{1,0:T(8,128)} %copy-done) | copy-start | bytes 12292

commit v3 on v2

--- a/solution.py
+++ b/solution.py
@@ -16,18 +16,6 @@
 courant = 0.1
 diffusion = 0.08
 radius_share = 0.25
-
-
-def advance_once(field):
-    halos = []
-    for axis, dim in (("gx", 0), ("gy", 1)):
-        size, length = lax.axis_size(axis), field.shape[dim]
-        up = [(i, (i + 1) % size) for i in range(size)]
-        down = [(j, i) for i, j in up]
-        last = lax.slice_in_dim(field, length - 1, length, axis=dim)
-        initial = lax.slice_in_dim(field, 0, 1, axis=dim)
-        halos += [lax.ppermute(last, axis, up), lax.ppermute(initial, axis, down)]
-    return step(field, *halos)
 
 
 def gather_kernel(flag_ref, cell_ref, level_ref, coef_ref, field_ref, out_ref, chosen_ref):
@@ -76,42 +64,122 @@
     )(flags, cells, levels, coefs.reshape(-1), field)
 
 
-def step_kernel(field_ref, west_ref, east_ref, south_ref, north_ref, out_ref):
+def advect_update(c, w, e, s, n, width):
+    u = c[:, 0:width]
+    v = c[:, width:2 * width]
+    pu, mu = jnp.maximum(u, 0.0), jnp.minimum(u, 0.0)
+    pv, mv = jnp.maximum(v, 0.0), jnp.minimum(v, 0.0)
+    blocks = []
+    for b in range(3):
+        lanes = slice(b * width, (b + 1) * width)
+        cc, ww, ee, ss, nn = c[:, lanes], w[:, lanes], e[:, lanes], s[:, lanes], n[:, lanes]
+        flux = pu * (cc - ww) + mu * (ee - cc) + pv * (cc - ss) + mv * (nn - cc)
+        blocks.append(cc - courant * flux + diffusion * (ww + ee + (ss + nn) - 4.0 * cc))
+    return blocks
+
+
+def shifted(values, edge, shift):
+    count = values.shape[0]
+    row = lax.broadcasted_iota(jnp.int32, values.shape, 0)
+    fresh = 0 if shift == 1 else count - 1
+    return jnp.where(row == fresh, edge, pltpu.roll(values, shift % count, 0))
+
+
+def two_steps_kernel(
+    field_ref, west_ref, east_ref, south0_ref, south1_ref, north0_ref, north1_ref,
+    first_col_ref, last_col_ref, corner_ref, out_ref, mid_ref, ring_ref,
+):
     nx, ny, feat = field_ref.shape
     width = feat // 3
-    row_id = lax.broadcasted_iota(jnp.int32, (ny, width), 0)
-
-    def body(x, carry):
+
+    def store(ref, index, blocks):
+        for b in range(3):
+            ref[index, :, b * width:(b + 1) * width] = blocks[b]
+
+    def first_pass(x, carry):
         centre = field_ref[x]
-        west = jnp.where(x == 0, west_ref[0], field_ref[jnp.maximum(x - 1, 0)])
+        west = jnp.where(x == 0, west_ref[1], field_ref[jnp.maximum(x - 1, 0)])
         east = jnp.where(x == nx - 1, east_ref[0], field_ref[jnp.minimum(x + 1, nx - 1)])
-        south_edge = south_ref[x]
-        north_edge = north_ref[x]
-        u = centre[:, 0:width]
-        v = centre[:, width:2 * width]
-        pu, mu = jnp.maximum(u, 0.0), jnp.minimum(u, 0.0)
-        pv, mv = jnp.maximum(v, 0.0), jnp.minimum(v, 0.0)
-        for b in range(3):
-            lanes = slice(b * width, (b + 1) * width)
-            c = centre[:, lanes]
-            w = west[:, lanes]
-            e = east[:, lanes]
-            s = jnp.where(row_id == 0, south_edge[:, lanes], pltpu.roll(c, 1, 0))
-            n = jnp.where(row_id == ny - 1, north_edge[:, lanes], pltpu.roll(c, ny - 1, 0))
-            flux = pu * (c - w) + mu * (e - c) + pv * (c - s) + mv * (n - c)
-            out_ref[x, :, lanes] = c - courant * flux + diffusion * (w + e + (s + n) - 4.0 * c)
+        south = shifted(centre, south1_ref[pl.ds(x, 1), :], 1)
+        north = shifted(centre, north0_ref[pl.ds(x, 1), :], -1)
+        store(mid_ref, x, advect_update(centre, west, east, south, north, width))
         return carry
 
-    lax.fori_loop(0, nx, body, 0)
-
-def step(field, west, east, south, north):
+    lax.fori_loop(0, nx, first_pass, 0)
+    corner = corner_ref[...]
+    centre = west_ref[1]
+    ring_w = advect_update(centre, west_ref[0], field_ref[0], shifted(centre, corner[0:1], 1), shifted(centre, corner[1:2], -1), width)
+    centre = east_ref[0]
+    ring_e = advect_update(centre, field_ref[nx - 1], east_ref[1], shifted(centre, corner[2:3], 1), shifted(centre, corner[3:4], -1), width)
+    centre = south1_ref[...]
+    ring_s = advect_update(centre, shifted(centre, corner[0:1], 1), shifted(centre, corner[2:3], -1), south0_ref[...], first_col_ref[...], width)
+    centre = north0_ref[...]
+    ring_n = advect_update(centre, shifted(centre, corner[1:2], 1), shifted(centre, corner[3:4], -1), last_col_ref[...], north1_ref[...], width)
+    store(ring_ref, 0, ring_w)
+    store(ring_ref, 1, ring_e)
+    for b in range(3):
+        ring_ref[2, 0:nx, b * width:(b + 1) * width] = ring_s[b]
+        ring_ref[3, 0:nx, b * width:(b + 1) * width] = ring_n[b]
+
+    def second_pass(x, carry):
+        centre = mid_ref[x]
+        west = jnp.where(x == 0, ring_ref[0], mid_ref[jnp.maximum(x - 1, 0)])
+        east = jnp.where(x == nx - 1, ring_ref[1], mid_ref[jnp.minimum(x + 1, nx - 1)])
+        south = shifted(centre, ring_ref[2, pl.ds(x, 1), :], 1)
+        north = shifted(centre, ring_ref[3, pl.ds(x, 1), :], -1)
+        store(out_ref, x, advect_update(centre, west, east, south, north, width))
+        return carry
+
+    lax.fori_loop(0, nx, second_pass, 0)
+
+
+def two_steps(field, west, east, south0, south1, north0, north1, first_col, last_col, corner):
+    nx, ny, feat = field.shape
     vmem = pl.BlockSpec(memory_space=pltpu.VMEM)
     return pl.pallas_call(
-        step_kernel,
+        two_steps_kernel,
         out_shape=jax.ShapeDtypeStruct(field.shape, field.dtype),
-        in_specs=[vmem] * 5,
+        in_specs=[vmem] * 10,
         out_specs=vmem,
-    )(field, west, east, south, north)
+        scratch_shapes=[
+            pltpu.VMEM(field.shape, jnp.float32),
+            pltpu.VMEM((4, max(nx, ny), feat), jnp.float32),
+        ],
+    )(field, west, east, south0, south1, north0, north1, first_col, last_col, corner)
+
+
+def advance_twice(field):
+    nx, ny, feat = field.shape
+    sx, sy = lax.axis_size("gx"), lax.axis_size("gy")
+    up_x = [(i, (i + 1) % sx) for i in range(sx)]
+    down_x = [(j, i) for i, j in up_x]
+    up_y = [(i, (i + 1) % sy) for i in range(sy)]
+    down_y = [(j, i) for i, j in up_y]
+    west = lax.ppermute(field[nx - 2:], "gx", up_x)
+    east = lax.ppermute(field[:2], "gx", down_x)
+    south = lax.ppermute(field[:, ny - 2:], "gy", up_y)
+    north = lax.ppermute(field[:, :2], "gy", down_y)
+
+    def diagonal(piece, step_x, step_y):
+        pairs = [
+            (i * sy + j, ((i + step_x) % sx) * sy + (j + step_y) % sy)
+            for i in range(sx)
+            for j in range(sy)
+        ]
+        return lax.ppermute(piece, ("gx", "gy"), pairs)
+
+    corner = jnp.concatenate(
+        [
+            diagonal(field[nx - 1, ny - 1:], 1, 1),
+            diagonal(field[nx - 1, :1], 1, -1),
+            diagonal(field[0, ny - 1:], -1, 1),
+            diagonal(field[0, :1], -1, -1),
+        ]
+    )
+    return two_steps(
+        field, west, east, south[:, 0], south[:, 1], north[:, 0], north[:, 1],
+        field[:, 0], field[:, ny - 1], corner,
+    )
 
 
 def product(left, right):
@@ -227,9 +295,7 @@
     tile_east = lax.axis_index("gx")
     tile_north = lax.axis_index("gy")
     own_tile = tile_east * tiles_north + tile_north
-    field = state
-    for substep in range(2):
-        field = advance_once(field)
+    field = advance_twice(state)
     cells = field.reshape(span_east * span_north, features)
     width = features // COMP
     groups = width // ENS

time: 219 us -> 219 us (level); the launches traced: 223 us -> 215 us
  blocking collectives: 42.1 us -> 37.7 us
  waiting for transfers between devices: 39.7 us -> 44 us
  starting transfers between devices: 50.7 us -> 46.9 us
  Pallas kernels: 41.5 us -> 38.2 us
    all_to_all x1, blocking collectives: 42.1 us -> 37.7 us  [summed_everywhere(): parts = lax.all_to_all(rows, axes, 0, 0, tiled=True)]
    ppermute x8, waiting for transfers between devices: 0.32 us -> 4.63 us  [the longest x1 4.3 us: advance_twice(): south = lax.ppermute(field[:, ny - 2:], 'gy', up_y)]
    all_to_all x1, starting transfers between devices: 22.5 us -> 18.6 us  [summed_everywhere(): parts = lax.all_to_all(rows, axes, 0, 0, tiled=True)]
    pallas_call x2 -> x1, Pallas kernels: 13.5 us -> 10.2 us  [two_steps(): pl.pallas_call(two_steps_kernel, out_shape=jax.ShapeDtypeStruct(field.sha...]
    squeeze x0 -> x4, local copies, waits for them, and re-layouts: none -> 2.69 us  [the longest x1 0.77 us: advance_twice(): field[nx - 1, ny - 1:]]
  transfers between devices with their start and end apart: 11 -> 11, of which waited for: 4 -> 5; matrix products, arithmetic and copies ran while one was open for 9% -> 11% of each run, Pallas kernels for 5% -> 5%
where the time goes in v3:
time: 219 us; the launch traced here: 215 us
  starting transfers between devices  46.9 us (21%)
  waiting for transfers between devices  44 us (20%)
  Pallas kernels  38.2 us (17%)
  blocking collectives  37.7 us (17%)
  local copies, waits for them, and re-layouts  21 us (10%)
  matrix products  17.3 us (8%)
  other arithmetic  7.61 us (3%)
    all_to_all x1, blocking collectives, summed_everywhere(): parts = lax.all_to_all(rows, axes, 0, 0, tiled=True)  37.7 us
    pallas_call x2, Pallas kernels, gather_rows(): pl.pallas_call(gather_kernel, out_shape=jax.ShapeDtypeStruct((groups, cou...  22.2 us
    all_to_all x2, waiting for transfers between devices, summed_everywhere(): return lax.all_to_all(copies, axes, 0, 0, tiled=True)  19.7 us
    all_to_all x1, waiting for transfers between devices, summed_everywhere(): parts = lax.all_to_all(rows, axes, 0, 0, tiled=True)  19.7 us
    all_to_all x1, starting transfers between devices, summed_everywhere(): parts = lax.all_to_all(rows, axes, 0, 0, tiled=True)  18.6 us
    ppermute x4, starting transfers between devices, diagonal(): return lax.ppermute(piece, ('gx', 'gy'), pairs)  14.5 us
    dot_general x36, matrix products, product(): jnp.dot(left, right, precision=lax.Precision.HIGHEST, preferred_element_t...  11 us
    all_to_all x2, starting transfers between devices, summed_everywhere(): return lax.all_to_all(copies, axes, 0, 0, tiled=True)  10.7 us
  transfers between devices with their start and end apart: 11, of which 5 were waited for; matrix products, arithmetic and copies ran while one was open for 11% of the time, Pallas kernels for 5%

profile of v3, /device:TPU:1, one launch (start us, length us, event | category | flops | bytes accessed | tf_op | source)
XLA Modules:
  0.0 215.0 jit_solution(9424063027791559173)
XLA Ops:
  0.0 0.8 slice_bitcast_fusion.7
  0.8 5.7 %collective-permute-start.4 = (f32[1,384]{1,0:T(1,128)S(1)}, f32[1,384]{1,0:T(1,128)S(1)}, u32[]{:S(2)}, u32[]{:S(2)}) collective-permute-start(f32[1,384]{1,0:T(1,128)S(1)} %get-tuple-element.115), channel_id=1, source_target_pairs={{0,9},{1,10},{2,11},{3,12},{4,13},{5,14},{6,15},{7,8},{8,17},{9,18... | collective-permute-start | bytes 4616 | tf_op jit(solution)/shard_map/ppermute | solution.py:169
  6.5 2.5 %collective-permute-start.5 = (f32[1,384]{1,0:T(1,128)S(1)}, f32[1,384]{1,0:T(1,128)S(1)}, u32[]{:S(2)}, u32[]{:S(2)}) collective-permute-start(f32[1,384]{1,0:T(1,128)S(1)} %get-tuple-element.116), channel_id=1, source_target_pairs={{0,15},{1,8},{2,9},{3,10},{4,11},{5,12},{6,13},{7,14},{8,23},{9,16... | collective-permute-start | bytes 4616 | tf_op jit(solution)/shard_map/ppermute | solution.py:169
  9.0 6.3 %collective-permute-start.7 = (f32[1,384]{1,0:T(1,128)S(1)}, f32[1,384]{1,0:T(1,128)S(1)}, u32[]{:S(2)}, u32[]{:S(2)}) collective-permute-start(f32[1,384]{1,0:T(1,128)S(1)} %get-tuple-element.118), channel_id=1, source_target_pairs={{0,255},{1,248},{2,249},{3,250},{4,251},{5,252},{6,253},{7,254},{8... | collective-permute-start | bytes 4616 | tf_op jit(solution)/shard_map/ppermute | solution.py:169
  15.3 1.2 fusion.130
  16.6 1.2 fusion.129
  17.8 1.1 fusion.131
  18.9 0.8 compare_convert_fusion
  19.7 1.1 fusion.132
  20.8 1.5 slice_reduce_fusion.1
  22.3 0.6 fusion.133
  22.9 0.6 copy_bitcast_fusion
  24.2 0.6 mul.233.coef_ref
  24.9 1.4 collective-permute-start.2
  26.3 1.5 collective-permute-start.1
  28.4 0.6 slice_bitcast_fusion
  29.1 4.3 %collective-permute-done.2 = f32[32,2,384]{2,0,1:T(8,128)S(1)} collective-permute-done((f32[32,2,384]{2,0,1:T(8,128)S(1)}, f32[32,2,384]{2,0,1:T(8,128)S(1)}, u32[]{:S(2)}, u32[]{:S(2)}) %collective-permute-start.2) | collective-permute-done | bytes 98336 | tf_op jit(solution)/shard_map/ppermute | solution.py:160
  33.4 0.6 slice_bitcast_fusion.2
  35.0 10.2 %shard_map.82 = f32[32,64,384]{2,1,0:T(8,128)} custom-call(f32[32,64,384]{2,1,0:T(8,128)} %field_ref.1, f32[2,64,384]{2,1,0:T(8,128)} %copy-done.3, f32[2,64,384]{2,1,0:T(8,128)} %copy-done.4, f32[32,384]{1,0:T(8,128)} %get-tuple-element.130.south0_ref, f32[32,384]{1,0:T(8,128)} %get-tuple-element.129.south1_ref, f32[32,384]{1,0:T(8,128)} %get-tuple-element.128.north0_ref, ...), custom_call_target="tpu_custom_call" | custom-call | tf_op jit(solution)/shard_map/pallas_call | solution.py:139
  45.2 11.0 %shard_map.83 = f32[4,1024,128]{2,1,0:T(8,128)} custom-call(s32[4096]{0:T(1024)} %convert_element_type.102.flag_ref, s32[4096]{0:T(1024)} %bitcast.136, s32[4096]{0:T(1024)} %bitcast.138, f32[12288]{0:T(1024)} %mul.233.coef_ref, f32[2048,384]{1,0:T(8,128)} %bitcast.115), custom_call_target="tpu_custom_call" | custom-call | tf_op jit(solution)/shard_map/pallas_call | solution.py:58
  56.2 3.6 %fusion.127 = f32[1024,128,1]{1,0,2:T(8,128)} fusion(f32[4,1024,128]{2,1,0:T(8,128)} %shard_map.83, s32[128]{0:T(128)S(1)} %get-tuple-element.154, s32[128]{0:T(128)S(1)} %get-tuple-element.155, s32[128]{0:T(128)S(1)} %get-tuple-element.153, s32[128]{0:T(128)S(1)} %get-tuple-element.156, pred[128]{0:T(512)(128)(4,1)S(1)} %get-tuple-element.151, ...), kind=kOutput, calls=%fused_computation.214 | convolution fusion | flops 805699584 | bytes 2623744 | tf_op jit(solution)/shard_map/krl,klo->ro/dot_general | solution.py:309
  59.8 18.6 %all-to-all-start = ((f32[256,4,128]{2,1,0:T(4,128)}), f32[256,4,128]{2,1,0:T(4,128)S(1)}, u32[]{:S(2)}, u32[]{:S(2)}) async-start(f32[256,4,128]{2,1,0:T(4,128)} %bitcast.16), calls=%async_computation | async-start | bytes 1048576 | tf_op jit(solution)/shard_map/all_to_all | solution.py:215
  79.8 19.7 %all-to-all-done = f32[256,4,128]{2,1,0:T(4,128)S(1)} async-done(((f32[256,4,128]{2,1,0:T(4,128)}), f32[256,4,128]{2,1,0:T(4,128)S(1)}, u32[]{:S(2)}, u32[]{:S(2)}) %all-to-all-start) | async-done | bytes 524320 | tf_op jit(solution)/shard_map/all_to_all | solution.py:215
  99.8 0.9 broadcast_in_dim.70
  100.7 5.3 %all-to-all-start.1 = ((f32[256,4,128]{2,1,0:T(4,128)}), f32[256,4,128]{2,1,0:T(4,128)S(1)}, u32[]{:S(2)}, u32[]{:S(2)}) async-start(f32[256,4,128]{2,1,0:T(4,128)} %broadcast_in_dim.70), calls=%async_computation.1 | async-start | bytes 1048576 | tf_op jit(solution)/shard_map/all_to_all | solution.py:218
  108.8 0.6 convert_element_type.109.flag_ref
  109.5 0.6 mul.250.coef_ref
  110.1 11.2 %shard_map.84 = f32[4,1024,128]{2,1,0:T(8,128)} custom-call(s32[4096]{0:T(1024)} %convert_element_type.109.flag_ref, s32[4096]{0:T(1024)} %bitcast.135, s32[4096]{0:T(1024)} %bitcast.137, f32[12288]{0:T(1024)} %mul.250.coef_ref, f32[2048,384]{1,0:T(8,128)} %bitcast.116), custom_call_target="tpu_custom_call" | custom-call | tf_op jit(solution)/shard_map/pallas_call | solution.py:58
  121.3 2.8 %fusion.125 = f32[1024,128,1]{1,0,2:T(8,128)S(1)} fusion(f32[4,1024,128]{2,1,0:T(8,128)} %shard_map.84, s32[128]{0:T(128)S(1)} %get-tuple-element.154, s32[128]{0:T(128)S(1)} %get-tuple-element.155, s32[128]{0:T(128)S(1)} %get-tuple-element.153, s32[128]{0:T(128)S(1)} %get-tuple-element.156, pred[128]{0:T(512)(128)(4,1)S(1)} %get-tuple-element.151, ...), kind=kOutput, calls=%fused_computation.213 | convolution fusion | flops 805699584 | bytes 2623744 | tf_op jit(solution)/shard_map/krl,klo->ro/dot_general | solution.py:309
  124.0 2.9 %all-to-all-done.1 = f32[256,4,128]{2,1,0:T(4,128)S(1)} async-done(((f32[256,4,128]{2,1,0:T(4,128)}), f32[256,4,128]{2,1,0:T(4,128)S(1)}, u32[]{:S(2)}, u32[]{:S(2)}) %all-to-all-start.1) | async-done | bytes 524320 | tf_op jit(solution)/shard_map/all_to_all | solution.py:218
  126.9 0.8 multiply_reduce_fusion.1
  127.7 1.1 fusion.10
  128.9 0.6 reduce_max.18
  130.2 0.6 broadcast_divide_fusion.1
  130.8 2.2 %while.26 = (s32[]{:T(128)}, f32[32,32]{0,1:T(8,128)S(1)}, f32[32,32]{1,0:T(8,128)S(1)}, s32[]{:T(128)}) while((s32[]{:T(128)}, f32[32,32]{0,1:T(8,128)S(1)}, f32[32,32]{1,0:T(8,128)S(1)}, s32[]{:T(128)}) %tuple.84), condition=%wide.region_4.5_spmd.clone, body=%wide.region_3.4_spmd.clone.sunk | while | flops 1183746 | bytes 53301 | solution.py:279
  133.1 0.9 convolution_divide_fusion.1
  135.6 37.7 %all_to_all.33 = f32[256,4,128]{2,1,0:T(4,128)S(1)} all-to-all(f32[256,4,128]{2,1,0:T(4,128)S(1)} %copy.82), channel_id=1, replica_groups=mesh['gx'=32,'gy'=8] {'gx','gy'}, dimensions={0} | all-to-all | bytes 1048576 | tf_op jit(solution)/shard_map/all_to_all | solution.py:215
  173.6 0.9 broadcast_in_dim.78
  174.5 5.4 %all-to-all-start.3 = ((f32[256,4,128]{2,1,0:T(4,128)}), f32[256,4,128]{2,1,0:T(4,128)S(1)}, u32[]{:S(2)}, u32[]{:S(2)}) async-start(f32[256,4,128]{2,1,0:T(4,128)} %broadcast_in_dim.78), calls=%async_computation.3 | async-start | bytes 1048576 | tf_op jit(solution)/shard_map/all_to_all | solution.py:218
  183.9 16.8 %all-to-all-done.3 = f32[256,4,128]{2,1,0:T(4,128)S(1)} async-done(((f32[256,4,128]{2,1,0:T(4,128)}), f32[256,4,128]{2,1,0:T(4,128)S(1)}, u32[]{:S(2)}, u32[]{:S(2)}) %all-to-all-start.3) | async-done | bytes 524320 | tf_op jit(solution)/shard_map/all_to_all | solution.py:218
  200.7 0.8 multiply_reduce_fusion
  201.4 1.1 fusion.8
  202.6 0.6 reduce_max.19
  203.9 0.6 broadcast_divide_fusion
  204.6 2.2 %while.27 = (s32[]{:T(128)}, f32[32,32]{0,1:T(8,128)S(1)}, f32[32,32]{1,0:T(8,128)S(1)}, s32[]{:T(128)}) while((s32[]{:T(128)}, f32[32,32]{0,1:T(8,128)S(1)}, f32[32,32]{1,0:T(8,128)S(1)}, s32[]{:T(128)}) %tuple.83), condition=%wide.region_10.11_spmd.clone, body=%wide.region_9.10_spmd.clone.sunk | while | flops 1183746 | bytes 53301 | solution.py:279
  206.8 0.9 convolution_divide_fusion
  208.4 0.8 mul.268.mix_ref
  209.2 5.9 %shard_map.85 = f32[2048,384]{1,0:T(8,128)} custom-call(f32[2048,384]{1,0:T(8,128)} %bitcast.117, f32[128,128]{1,0:T(8,128)} %mul.268.mix_ref), custom_call_target="tpu_custom_call" | custom-call | tf_op jit(solution)/shard_map/pallas_call | solution.py:200
  (133 shorter events, 17.7 us)
Async XLA Ops:
  0.0 22.3 %copy-start.5 = (s32[2,4096]{1,0:T(2,128)S(1)}, s32[2,4096]{1,0:T(2,128)}, u32[]{:S(2)}) copy-start(s32[2,4096]{1,0:T(2,128)} %param.15) | copy-start | bytes 98308
  0.8 24.1 %collective-permute-start.4 = (f32[1,384]{1,0:T(1,128)S(1)}, f32[1,384]{1,0:T(1,128)S(1)}, u32[]{:S(2)}, u32[]{:S(2)}) collective-permute-start(f32[1,384]{1,0:T(1,128)S(1)} %get-tuple-element.115), channel_id=1, source_target_pairs={{0,9},{1,10},{2,11},{3,12},{4,13},{5,14},{6,15},{7,8},{8,17},{9,18... | collective-permute-start | bytes 4616 | tf_op jit(solution)/shard_map/ppermute | solution.py:169
  6.5 19.8 %collective-permute-start.5 = (f32[1,384]{1,0:T(1,128)S(1)}, f32[1,384]{1,0:T(1,128)S(1)}, u32[]{:S(2)}, u32[]{:S(2)}) collective-permute-start(f32[1,384]{1,0:T(1,128)S(1)} %get-tuple-element.116), channel_id=1, source_target_pairs={{0,15},{1,8},{2,9},{3,10},{4,11},{5,12},{6,13},{7,14},{8,23},{9,16... | collective-permute-start | bytes 4616 | tf_op jit(solution)/shard_map/ppermute | solution.py:169
  9.0 17.3 %collective-permute-start.6 = (f32[1,384]{1,0:T(1,128)S(1)}, f32[1,384]{1,0:T(1,128)S(1)}, u32[]{:S(2)}, u32[]{:S(2)}) collective-permute-start(f32[1,384]{1,0:T(1,128)S(1)} %get-tuple-element.117), channel_id=1, source_target_pairs={{0,249},{1,250},{2,251},{3,252},{4,253},{5,254},{6,255},{7,248},{8... | collective-permute-start | bytes 4616 | tf_op jit(solution)/shard_map/ppermute | solution.py:169
  9.0 18.8 %collective-permute-start.7 = (f32[1,384]{1,0:T(1,128)S(1)}, f32[1,384]{1,0:T(1,128)S(1)}, u32[]{:S(2)}, u32[]{:S(2)}) collective-permute-start(f32[1,384]{1,0:T(1,128)S(1)} %get-tuple-element.118), channel_id=1, source_target_pairs={{0,255},{1,248},{2,249},{3,250},{4,251},{5,252},{6,253},{7,254},{8... | collective-permute-start | bytes 4616 | tf_op jit(solution)/shard_map/ppermute | solution.py:169
  16.5 11.9 %collective-permute-start.3 = (f32[32,2,384]{2,0,1:T(8,128)S(1)}, f32[32,2,384]{2,0,1:T(8,128)S(1)}, u32[]{:S(2)}, u32[]{:S(2)}) collective-permute-start(f32[32,2,384]{2,0,1:T(8,128)S(1)} %copy.102), channel_id=1, source_target_pairs={{1,0},{2,1},{3,2},{4,3},{5,4},{6,5},{7,6},{0,7},{9,8},{10,9},{11,1... | collective-permute-start | bytes 294920 | tf_op jit(solution)/shard_map/ppermute | solution.py:161
  24.9 8.5 %collective-permute-start.2 = (f32[32,2,384]{2,0,1:T(8,128)S(1)}, f32[32,2,384]{2,0,1:T(8,128)S(1)}, u32[]{:S(2)}, u32[]{:S(2)}) collective-permute-start(f32[32,2,384]{2,0,1:T(8,128)S(1)} %copy.101), channel_id=1, source_target_pairs={{0,1},{1,2},{2,3},{3,4},{4,5},{5,6},{6,7},{7,0},{8,9},{9,10},{10,1... | collective-permute-start | bytes 294920 | tf_op jit(solution)/shard_map/ppermute | solution.py:160
  26.3 7.7 %collective-permute-start = (f32[2,64,384]{2,1,0:T(8,128)S(1)}, f32[2,64,384]{2,1,0:T(8,128)S(1)}, u32[]{:S(2)}, u32[]{:S(2)}) collective-permute-start(f32[2,64,384]{2,1,0:T(8,128)S(1)} %get-tuple-element.124), channel_id=1, source_target_pairs={{0,8},{8,16},{16,24},{24,32},{32,40},{40,48},{48,56},{56,64},{64,7... | collective-permute-start | bytes 589832 | tf_op jit(solution)/shard_map/ppermute | solution.py:158
  26.3 8.0 %collective-permute-start.1 = (f32[2,64,384]{2,1,0:T(8,128)S(1)}, f32[2,64,384]{2,1,0:T(8,128)S(1)}, u32[]{:S(2)}, u32[]{:S(2)}) collective-permute-start(f32[2,64,384]{2,1,0:T(8,128)S(1)} %get-tuple-element.123), channel_id=1, source_target_pairs={{8,0},{16,8},{24,16},{32,24},{40,32},{48,40},{56,48},{64,56},{72,6... | collective-permute-start | bytes 589832 | tf_op jit(solution)/shard_map/ppermute | solution.py:159
  34.0 0.7 copy-start.3
  34.3 0.7 copy-start.4
  59.8 39.7 %all-to-all-start = ((f32[256,4,128]{2,1,0:T(4,128)}), f32[256,4,128]{2,1,0:T(4,128)S(1)}, u32[]{:S(2)}, u32[]{:S(2)}) async-start(f32[256,4,128]{2,1,0:T(4,128)} %bitcast.16), calls=%async_computation | async-start | bytes 1048576 | tf_op jit(solution)/shard_map/all_to_all | solution.py:215
  78.3 27.7 %copy-start.8 = (s32[1,1,2,16]{3,2,1,0:T(2,128)S(1)}, s32[1,1,2,16]{3,2,1,0:T(2,128)}, u32[]{:S(2)}) copy-start(s32[1,1,2,16]{3,2,1,0:T(2,128)} %param.19) | copy-start | bytes 388
  79.6 26.9 %copy-start.6 = (f32[2,4096]{1,0:T(2,128)S(1)}, f32[2,4096]{1,0:T(2,128)}, u32[]{:S(2)}) copy-start(f32[2,4096]{1,0:T(2,128)} %param.17) | copy-start | bytes 98308
  79.6 26.9 %copy-start.7 = (f32[2,4096]{1,0:T(2,128)S(1)}, f32[2,4096]{1,0:T(2,128)}, u32[]{:S(2)}) copy-start(f32[2,4096]{1,0:T(2,128)} %param.18) | copy-start | bytes 98308
  100.7 26.3 %all-to-all-start.1 = ((f32[256,4,128]{2,1,0:T(4,128)}), f32[256,4,128]{2,1,0:T(4,128)S(1)}, u32[]{:S(2)}, u32[]{:S(2)}) async-start(f32[256,4,128]{2,1,0:T(4,128)} %broadcast_in_dim.70), calls=%async_computation.1 | async-start | bytes 1048576 | tf_op jit(solution)/shard_map/all_to_all | solution.py:218
  108.8 12.5 %copy-start = (f32[32,32]{1,0:T(8,128)}, f32[32,32]{1,0:T(8,128)S(1)}, u32[]{:S(2)}) copy-start(f32[32,32]{1,0:T(8,128)S(1)} %copy.76) | copy-start | bytes 12292
  127.7 3.1 %copy-start.2 = (f32[32,32]{1,0:T(8,128)S(1)}, f32[32,32]{1,0:T(8,128)}, u32[]{:S(2)}) copy-start(f32[32,32]{1,0:T(8,128)} %copy-done) | copy-start | bytes 12292
  174.5 26.2 %all-to-all-start.3 = ((f32[256,4,128]{2,1,0:T(4,128)}), f32[256,4,128]{2,1,0:T(4,128)S(1)}, u32[]{:S(2)}, u32[]{:S(2)}) async-start(f32[256,4,128]{2,1,0:T(4,128)} %broadcast_in_dim.78), calls=%async_computation.3 | async-start | bytes 1048576 | tf_op jit(solution)/shard_map/all_to_all | solution.py:218
  201.4 3.1 %copy-start.1 = (f32[32,32]{1,0:T(8,128)S(1)}, f32[32,32]{1,0:T(8,128)}, u32[]{:S(2)}) copy-start(f32[32,32]{1,0:T(8,128)} %copy-done) | copy-start | bytes 12292

commit v4 on v3

--- a/solution.py
+++ b/solution.py
@@ -157,27 +157,13 @@
     down_y = [(j, i) for i, j in up_y]
     west = lax.ppermute(field[nx - 2:], "gx", up_x)
     east = lax.ppermute(field[:2], "gx", down_x)
-    south = lax.ppermute(field[:, ny - 2:], "gy", up_y)
-    north = lax.ppermute(field[:, :2], "gy", down_y)
-
-    def diagonal(piece, step_x, step_y):
-        pairs = [
-            (i * sy + j, ((i + step_x) % sx) * sy + (j + step_y) % sy)
-            for i in range(sx)
-            for j in range(sy)
-        ]
-        return lax.ppermute(piece, ("gx", "gy"), pairs)
-
-    corner = jnp.concatenate(
-        [
-            diagonal(field[nx - 1, ny - 1:], 1, 1),
-            diagonal(field[nx - 1, :1], 1, -1),
-            diagonal(field[0, ny - 1:], -1, 1),
-            diagonal(field[0, :1], -1, -1),
-        ]
-    )
+    last_cols = jnp.concatenate([west[:, ny - 2:], field[:, ny - 2:], east[:, ny - 2:]])
+    first_cols = jnp.concatenate([west[:, :2], field[:, :2], east[:, :2]])
+    south = lax.ppermute(last_cols, "gy", up_y)
+    north = lax.ppermute(first_cols, "gy", down_y)
+    corner = jnp.stack([south[1, 1], north[1, 0], south[nx + 2, 1], north[nx + 2, 0]])
     return two_steps(
-        field, west, east, south[:, 0], south[:, 1], north[:, 0], north[:, 1],
+        field, west, east, south[2:nx + 2, 0], south[2:nx + 2, 1], north[2:nx + 2, 0], north[2:nx + 2, 1],
         field[:, 0], field[:, ny - 1], corner,
     )
 

time: 219 us -> 216 us (0.986); the launches traced: 215 us -> 220 us
  blocking collectives: 37.7 us -> 45.3 us
  starting transfers between devices: 46.9 us -> 44.2 us
    ppermute x6 -> x2, starting transfers between devices: 16.1 us -> 2.38 us  [the longest x1 2.3 us: advance_twice(): north = lax.ppermute(first_cols, 'gy', down_y)]
    all_to_all x1, starting transfers between devices: 18.6 us -> 26.7 us  [summed_everywhere(): parts = lax.all_to_all(rows, axes, 0, 0, tiled=True)]
    all_to_all x1, blocking collectives: 37.7 us -> 45.3 us  [summed_everywhere(): parts = lax.all_to_all(rows, axes, 0, 0, tiled=True)]
    ppermute x1, starting transfers between devices: 0.01 us -> 4.46 us  [advance_twice(): west = lax.ppermute(field[nx - 2:], 'gx', up_x)]
    ppermute x6 -> x2, waiting for transfers between devices: 4.32 us -> 4.43 us  [the longest x1 4.06 us: advance_twice(): south = lax.ppermute(last_cols, 'gy', up_y)]
  transfers between devices with their start and end apart: 11 -> 7, of which waited for: 5 -> 6; matrix products, arithmetic and copies ran while one was open for 11% -> 9% of each run, Pallas kernels for 5% -> 5%
where the time goes in v4:
time: 216 us; the launch traced here: 220 us
  waiting for transfers between devices  46 us (21%)
  blocking collectives  45.3 us (21%)
  starting transfers between devices  44.2 us (20%)
  Pallas kernels  38.4 us (18%)
  local copies, waits for them, and re-layouts  19.5 us (9%)
  matrix products  17.3 us (8%)
  other arithmetic  6.89 us (3%)
    all_to_all x1, blocking collectives, summed_everywhere(): parts = lax.all_to_all(rows, axes, 0, 0, tiled=True)  45.3 us
    all_to_all x1, starting transfers between devices, summed_everywhere(): parts = lax.all_to_all(rows, axes, 0, 0, tiled=True)  26.7 us
    pallas_call x2, Pallas kernels, gather_rows(): pl.pallas_call(gather_kernel, out_shape=jax.ShapeDtypeStruct((groups, cou...  22.3 us
    all_to_all x1, waiting for transfers between devices, summed_everywhere(): parts = lax.all_to_all(rows, axes, 0, 0, tiled=True)  19.7 us
    all_to_all x2, waiting for transfers between devices, summed_everywhere(): return lax.all_to_all(copies, axes, 0, 0, tiled=True)  19.7 us
    dot_general x36, matrix products, product(): jnp.dot(left, right, precision=lax.Precision.HIGHEST, preferred_element_t...  11 us
    all_to_all x2, starting transfers between devices, summed_everywhere(): return lax.all_to_all(copies, axes, 0, 0, tiled=True)  10.5 us
    pallas_call x1, Pallas kernels, two_steps(): pl.pallas_call(two_steps_kernel, out_shape=jax.ShapeDtypeStruct(field.sha...  10.2 us
  transfers between devices with their start and end apart: 7, of which 6 were waited for; matrix products, arithmetic and copies ran while one was open for 9% of the time, Pallas kernels for 5%

profile of v4, /device:TPU:1, one launch (start us, length us, event | category | flops | bytes accessed | tf_op | source)
XLA Modules:
  0.0 220.0 jit_solution(9052233448604743834)
XLA Ops:
  0.0 1.1 fusion.131
  1.3 4.5 %collective-permute-start = (f32[2,64,384]{2,0,1:T(2,128)S(1)}, f32[2,64,384]{2,0,1:T(2,128)S(1)}, u32[]{:S(2)}, u32[]{:S(2)}) collective-permute-start(f32[2,64,384]{2,0,1:T(2,128)S(1)} %copy.117), channel_id=1, source_target_pairs={{0,8},{8,16},{16,24},{24,32},{32,40},{40,48},{48,56},{56,64},{64,7... | collective-permute-start | bytes 589832 | tf_op jit(solution)/shard_map/ppermute | solution.py:158
  6.0 1.2 fusion.130
  7.2 1.2 fusion.129
  8.5 0.6 convert_element_type.102.flag_ref
  9.3 0.6 fusion.135
  9.9 0.6 copy_bitcast_fusion
  10.6 0.6 mul.233.coef_ref
  11.2 0.7 slice_reduce_fusion.1
  11.9 2.3 %collective-permute-done.1 = f32[2,64,384]{2,0,1:T(2,128)S(1)} collective-permute-done((f32[2,64,384]{2,0,1:T(2,128)S(1)}, f32[2,64,384]{2,0,1:T(2,128)S(1)}, u32[]{:S(2)}, u32[]{:S(2)}) %collective-permute-start.1) | collective-permute-done | bytes 196640 | tf_op jit(solution)/shard_map/ppermute | solution.py:159
  14.2 2.3 %collective-permute-start.3 = (f32[36,2,384]{2,0,1:T(8,128)S(1)}, f32[36,2,384]{2,0,1:T(8,128)S(1)}, u32[]{:S(2)}, u32[]{:S(2)}) collective-permute-start(f32[36,2,384]{2,0,1:T(8,128)S(1)} %pad_maximum_fusion.1), channel_id=1, source_target_pairs={{1,0},{2,1},{3,2},{4,3},{5,4},{6,5},{7,6},{0,7},{9,8},{10,9},{11,1... | collective-permute-start | bytes 331784 | tf_op jit(solution)/shard_map/ppermute | solution.py:163
  16.6 0.7 copy.79.west_ref
  17.3 0.7 copy.80.east_ref
  18.4 4.1 %collective-permute-done.2 = f32[36,2,384]{2,0,1:T(8,128)S(1)} collective-permute-done((f32[36,2,384]{2,0,1:T(8,128)S(1)}, f32[36,2,384]{2,0,1:T(8,128)S(1)}, u32[]{:S(2)}, u32[]{:S(2)}) %collective-permute-start.2) | collective-permute-done | bytes 110624 | tf_op jit(solution)/shard_map/ppermute | solution.py:162
  22.4 0.6 pad_maximum_fusion.2.corner_ref
  23.0 0.6 slice_bitcast_fusion
  23.7 0.6 slice_bitcast_fusion.2
  24.3 10.2 %shard_map.82 = f32[32,64,384]{2,1,0:T(8,128)} custom-call(f32[32,64,384]{2,1,0:T(8,128)} %field_ref.1, f32[2,64,384]{2,1,0:T(8,128)} %copy.79.west_ref, f32[2,64,384]{2,1,0:T(8,128)} %copy.80.east_ref, f32[32,384]{1,0:T(8,128)} %get-tuple-element.132.south0_ref, f32[32,384]{1,0:T(8,128)} %get-tuple-element.131.south1_ref, ...), custom_call_target="tpu_custom_call" | custom-call | tf_op jit(solution)/shard_map/pallas_call | solution.py:139
  34.5 11.0 %shard_map.83 = f32[4,1024,128]{2,1,0:T(8,128)} custom-call(s32[4096]{0:T(1024)} %convert_element_type.102.flag_ref, s32[4096]{0:T(1024)} %bitcast.136, s32[4096]{0:T(1024)} %bitcast.138, f32[12288]{0:T(1024)} %mul.233.coef_ref, f32[2048,384]{1,0:T(8,128)} %bitcast.115), custom_call_target="tpu_custom_call" | custom-call | tf_op jit(solution)/shard_map/pallas_call | solution.py:58
  45.5 3.6 %fusion.127 = f32[1024,128,1]{1,0,2:T(8,128)} fusion(f32[4,1024,128]{2,1,0:T(8,128)} %shard_map.83, s32[128]{0:T(128)S(1)} %get-tuple-element.158, s32[128]{0:T(128)S(1)} %get-tuple-element.159, s32[128]{0:T(128)S(1)} %get-tuple-element.157, s32[128]{0:T(128)S(1)} %get-tuple-element.160, pred[128]{0:T(512)(128)(4,1)S(1)} %get-tuple-element.155, ...), kind=kOutput, calls=%fused_computation.216 | convolution fusion | flops 805699584 | bytes 2623744 | tf_op jit(solution)/shard_map/krl,klo->ro/dot_general | solution.py:295
  49.1 26.7 %all-to-all-start = ((f32[256,4,128]{2,1,0:T(4,128)}), f32[256,4,128]{2,1,0:T(4,128)S(1)}, u32[]{:S(2)}, u32[]{:S(2)}) async-start(f32[256,4,128]{2,1,0:T(4,128)} %bitcast.16), calls=%async_computation | async-start | bytes 1048576 | tf_op jit(solution)/shard_map/all_to_all | solution.py:201
  77.3 19.7 %all-to-all-done = f32[256,4,128]{2,1,0:T(4,128)S(1)} async-done(((f32[256,4,128]{2,1,0:T(4,128)}), f32[256,4,128]{2,1,0:T(4,128)S(1)}, u32[]{:S(2)}, u32[]{:S(2)}) %all-to-all-start) | async-done | bytes 524320 | tf_op jit(solution)/shard_map/all_to_all | solution.py:201
  97.3 0.9 broadcast_in_dim.70
  98.2 5.2 %all-to-all-start.1 = ((f32[256,4,128]{2,1,0:T(4,128)}), f32[256,4,128]{2,1,0:T(4,128)S(1)}, u32[]{:S(2)}, u32[]{:S(2)}) async-start(f32[256,4,128]{2,1,0:T(4,128)} %broadcast_in_dim.70), calls=%async_computation.1 | async-start | bytes 1048576 | tf_op jit(solution)/shard_map/all_to_all | solution.py:204
  106.1 0.6 convert_element_type.109.flag_ref
  106.8 0.6 mul.250.coef_ref
  107.4 11.3 %shard_map.84 = f32[4,1024,128]{2,1,0:T(8,128)} custom-call(s32[4096]{0:T(1024)} %convert_element_type.109.flag_ref, s32[4096]{0:T(1024)} %bitcast.135, s32[4096]{0:T(1024)} %bitcast.137, f32[12288]{0:T(1024)} %mul.250.coef_ref, f32[2048,384]{1,0:T(8,128)} %bitcast.116), custom_call_target="tpu_custom_call" | custom-call | tf_op jit(solution)/shard_map/pallas_call | solution.py:58
  118.7 2.8 %fusion.125 = f32[1024,128,1]{1,0,2:T(8,128)S(1)} fusion(f32[4,1024,128]{2,1,0:T(8,128)} %shard_map.84, s32[128]{0:T(128)S(1)} %get-tuple-element.158, s32[128]{0:T(128)S(1)} %get-tuple-element.159, s32[128]{0:T(128)S(1)} %get-tuple-element.157, s32[128]{0:T(128)S(1)} %get-tuple-element.160, pred[128]{0:T(512)(128)(4,1)S(1)} %get-tuple-element.155, ...), kind=kOutput, calls=%fused_computation.215 | convolution fusion | flops 805699584 | bytes 2623744 | tf_op jit(solution)/shard_map/krl,klo->ro/dot_general | solution.py:295
  121.5 2.9 %all-to-all-done.1 = f32[256,4,128]{2,1,0:T(4,128)S(1)} async-done(((f32[256,4,128]{2,1,0:T(4,128)}), f32[256,4,128]{2,1,0:T(4,128)S(1)}, u32[]{:S(2)}, u32[]{:S(2)}) %all-to-all-start.1) | async-done | bytes 524320 | tf_op jit(solution)/shard_map/all_to_all | solution.py:204
  124.3 0.8 multiply_reduce_fusion.1
  125.1 1.1 fusion.10
  126.3 0.6 reduce_max.18
  127.6 0.6 broadcast_divide_fusion.1
  128.2 2.2 %while.26 = (s32[]{:T(128)}, f32[32,32]{0,1:T(8,128)S(1)}, f32[32,32]{1,0:T(8,128)S(1)}, s32[]{:T(128)}) while((s32[]{:T(128)}, f32[32,32]{0,1:T(8,128)S(1)}, f32[32,32]{1,0:T(8,128)S(1)}, s32[]{:T(128)}) %tuple.85), condition=%wide.region_4.5_spmd.clone, body=%wide.region_3.4_spmd.clone.sunk | while | flops 1183746 | bytes 53301 | solution.py:265
  130.5 0.9 convolution_divide_fusion.1
  132.1 0.6 fusion.6
  133.0 45.3 %all_to_all.33 = f32[256,4,128]{2,1,0:T(4,128)S(1)} all-to-all(f32[256,4,128]{2,1,0:T(4,128)S(1)} %copy.98), channel_id=1, replica_groups=mesh['gx'=32,'gy'=8] {'gx','gy'}, dimensions={0} | all-to-all | bytes 1048576 | tf_op jit(solution)/shard_map/all_to_all | solution.py:201
  178.5 0.9 broadcast_in_dim.78
  179.4 5.4 %all-to-all-start.3 = ((f32[256,4,128]{2,1,0:T(4,128)}), f32[256,4,128]{2,1,0:T(4,128)S(1)}, u32[]{:S(2)}, u32[]{:S(2)}) async-start(f32[256,4,128]{2,1,0:T(4,128)} %broadcast_in_dim.78), calls=%async_computation.3 | async-start | bytes 1048576 | tf_op jit(solution)/shard_map/all_to_all | solution.py:204
  188.8 16.8 %all-to-all-done.3 = f32[256,4,128]{2,1,0:T(4,128)S(1)} async-done(((f32[256,4,128]{2,1,0:T(4,128)}), f32[256,4,128]{2,1,0:T(4,128)S(1)}, u32[]{:S(2)}, u32[]{:S(2)}) %all-to-all-start.3) | async-done | bytes 524320 | tf_op jit(solution)/shard_map/all_to_all | solution.py:204
  205.6 0.8 multiply_reduce_fusion
  206.4 1.1 fusion.8
  207.5 0.6 reduce_max.19
  208.8 0.6 broadcast_divide_fusion
  209.5 2.2 %while.27 = (s32[]{:T(128)}, f32[32,32]{0,1:T(8,128)S(1)}, f32[32,32]{1,0:T(8,128)S(1)}, s32[]{:T(128)}) while((s32[]{:T(128)}, f32[32,32]{0,1:T(8,128)S(1)}, f32[32,32]{1,0:T(8,128)S(1)}, s32[]{:T(128)}) %tuple.84), condition=%wide.region_10.11_spmd.clone, body=%wide.region_9.10_spmd.clone.sunk | while | flops 1183746 | bytes 53301 | solution.py:265
  211.7 0.9 convolution_divide_fusion
  213.3 0.8 mul.268.mix_ref
  214.1 5.9 %shard_map.85 = f32[2048,384]{1,0:T(8,128)} custom-call(f32[2048,384]{1,0:T(8,128)} %bitcast.117, f32[128,128]{1,0:T(8,128)} %mul.268.mix_ref), custom_call_target="tpu_custom_call" | custom-call | tf_op jit(solution)/shard_map/pallas_call | solution.py:186
  (136 shorter events, 15.9 us)
Async XLA Ops:
  0.0 8.4 %copy-start.3 = (s32[2,4096]{1,0:T(2,128)S(1)}, s32[2,4096]{1,0:T(2,128)}, u32[]{:S(2)}) copy-start(s32[2,4096]{1,0:T(2,128)} %param.13) | copy-start | bytes 98308
  0.0 9.2 %copy-start.4 = (f32[2,3,4096]{2,0,1:T(2,128)S(1)}, f32[2,3,4096]{2,0,1:T(2,128)}, u32[]{:S(2)}) copy-start(f32[2,3,4096]{2,0,1:T(2,128)} %param.16) | copy-start | bytes 294916
  0.0 9.3 %copy-start.6 = (s32[2,4096]{1,0:T(2,128)S(1)}, s32[2,4096]{1,0:T(2,128)}, u32[]{:S(2)}) copy-start(s32[2,4096]{1,0:T(2,128)} %param.15) | copy-start | bytes 98308
  0.0 11.2 %copy-start.5 = (s32[2,4096]{1,0:T(2,128)S(1)}, s32[2,4096]{1,0:T(2,128)}, u32[]{:S(2)}) copy-start(s32[2,4096]{1,0:T(2,128)} %param.14) | copy-start | bytes 98308
  1.3 10.6 %collective-permute-start = (f32[2,64,384]{2,0,1:T(2,128)S(1)}, f32[2,64,384]{2,0,1:T(2,128)S(1)}, u32[]{:S(2)}, u32[]{:S(2)}) collective-permute-start(f32[2,64,384]{2,0,1:T(2,128)S(1)} %copy.117), channel_id=1, source_target_pairs={{0,8},{8,16},{16,24},{24,32},{32,40},{40,48},{48,56},{56,64},{64,7... | collective-permute-start | bytes 589832 | tf_op jit(solution)/shard_map/ppermute | solution.py:158
  5.9 8.3 %collective-permute-start.1 = (f32[2,64,384]{2,0,1:T(2,128)S(1)}, f32[2,64,384]{2,0,1:T(2,128)S(1)}, u32[]{:S(2)}, u32[]{:S(2)}) collective-permute-start(f32[2,64,384]{2,0,1:T(2,128)S(1)} %copy.118), channel_id=1, source_target_pairs={{8,0},{16,8},{24,16},{32,24},{40,32},{48,40},{56,48},{64,56},{72,6... | collective-permute-start | bytes 589832 | tf_op jit(solution)/shard_map/ppermute | solution.py:159
  14.2 4.2 %collective-permute-start.3 = (f32[36,2,384]{2,0,1:T(8,128)S(1)}, f32[36,2,384]{2,0,1:T(8,128)S(1)}, u32[]{:S(2)}, u32[]{:S(2)}) collective-permute-start(f32[36,2,384]{2,0,1:T(8,128)S(1)} %pad_maximum_fusion.1), channel_id=1, source_target_pairs={{1,0},{2,1},{3,2},{4,3},{5,4},{6,5},{7,6},{0,7},{9,8},{10,9},{11,1... | collective-permute-start | bytes 331784 | tf_op jit(solution)/shard_map/ppermute | solution.py:163
  16.5 5.9 %collective-permute-start.2 = (f32[36,2,384]{2,0,1:T(8,128)S(1)}, f32[36,2,384]{2,0,1:T(8,128)S(1)}, u32[]{:S(2)}, u32[]{:S(2)}) collective-permute-start(f32[36,2,384]{2,0,1:T(8,128)S(1)} %pad_maximum_fusion), channel_id=1, source_target_pairs={{0,1},{1,2},{2,3},{3,4},{4,5},{5,6},{6,7},{7,0},{8,9},{9,10},{10,1... | collective-permute-start | bytes 331784 | tf_op jit(solution)/shard_map/ppermute | solution.py:162
  49.1 47.9 %all-to-all-start = ((f32[256,4,128]{2,1,0:T(4,128)}), f32[256,4,128]{2,1,0:T(4,128)S(1)}, u32[]{:S(2)}, u32[]{:S(2)}) async-start(f32[256,4,128]{2,1,0:T(4,128)} %bitcast.16), calls=%async_computation | async-start | bytes 1048576 | tf_op jit(solution)/shard_map/all_to_all | solution.py:201
  75.8 27.5 %copy-start.9 = (s32[1,1,2,16]{3,2,1,0:T(2,128)S(1)}, s32[1,1,2,16]{3,2,1,0:T(2,128)}, u32[]{:S(2)}) copy-start(s32[1,1,2,16]{3,2,1,0:T(2,128)} %param.19) | copy-start | bytes 388
  77.1 26.7 %copy-start.7 = (f32[2,4096]{1,0:T(2,128)S(1)}, f32[2,4096]{1,0:T(2,128)}, u32[]{:S(2)}) copy-start(f32[2,4096]{1,0:T(2,128)} %param.17) | copy-start | bytes 98308
  77.1 26.7 %copy-start.8 = (f32[2,4096]{1,0:T(2,128)S(1)}, f32[2,4096]{1,0:T(2,128)}, u32[]{:S(2)}) copy-start(f32[2,4096]{1,0:T(2,128)} %param.18) | copy-start | bytes 98308
  98.2 26.2 %all-to-all-start.1 = ((f32[256,4,128]{2,1,0:T(4,128)}), f32[256,4,128]{2,1,0:T(4,128)S(1)}, u32[]{:S(2)}, u32[]{:S(2)}) async-start(f32[256,4,128]{2,1,0:T(4,128)} %broadcast_in_dim.70), calls=%async_computation.1 | async-start | bytes 1048576 | tf_op jit(solution)/shard_map/all_to_all | solution.py:204
  106.1 12.6 %copy-start = (f32[32,32]{1,0:T(8,128)}, f32[32,32]{1,0:T(8,128)S(1)}, u32[]{:S(2)}) copy-start(f32[32,32]{1,0:T(8,128)S(1)} %copy.92) | copy-start | bytes 12292
  125.1 3.1 %copy-start.2 = (f32[32,32]{1,0:T(8,128)S(1)}, f32[32,32]{1,0:T(8,128)}, u32[]{:S(2)}) copy-start(f32[32,32]{1,0:T(8,128)} %copy-done) | copy-start | bytes 12292
  179.4 26.2 %all-to-all-start.3 = ((f32[256,4,128]{2,1,0:T(4,128)}), f32[256,4,128]{2,1,0:T(4,128)S(1)}, u32[]{:S(2)}, u32[]{:S(2)}) async-start(f32[256,4,128]{2,1,0:T(4,128)} %broadcast_in_dim.78), calls=%async_computation.3 | async-start | bytes 1048576 | tf_op jit(solution)/shard_map/all_to_all | solution.py:204
  206.3 3.1 %copy-start.1 = (f32[32,32]{1,0:T(8,128)S(1)}, f32[32,32]{1,0:T(8,128)}, u32[]{:S(2)}) copy-start(f32[32,32]{1,0:T(8,128)} %copy-done) | copy-start | bytes 12292

commit v5 on v4

--- a/solution.py
+++ b/solution.py
@@ -18,18 +18,19 @@
 radius_share = 0.25
 
 
-def gather_kernel(flag_ref, cell_ref, level_ref, coef_ref, field_ref, out_ref, chosen_ref):
+def gather_kernel(slot_ref, taken_ref, cell_ref, level_ref, coef_ref, field_ref, out_ref, chosen_ref):
     count = cell_ref.shape[0]
     groups, rows, width = out_ref.shape
     lane_level = lax.broadcasted_iota(jnp.int32, (1, width), 1) // ENS
     sublane = lax.broadcasted_iota(jnp.int32, (8, width), 0)
     out_ref[...] = jnp.zeros(out_ref.shape, out_ref.dtype)
 
-    def choose(j, taken):
-        chosen_ref[taken] = j
-        return taken + flag_ref[j]
-
-    taken = lax.fori_loop(0, count, choose, 0, unroll=8)
+    def choose(j, carry):
+        chosen_ref[slot_ref[j]] = j
+        return carry
+
+    lax.fori_loop(0, count, choose, 0, unroll=8)
+    taken = taken_ref[0]
 
     def body(i, carry):
         j = chosen_ref[i]
@@ -50,6 +51,8 @@
 
 
 def gather_rows(flags, cells, levels, coefs, field):
+    slots = jnp.cumsum(flags) - flags
+    taken = jnp.sum(flags, keepdims=True)
     count = cells.shape[0]
     width = field.shape[1] // 3
     groups = width // ENS
@@ -58,10 +61,10 @@
     return pl.pallas_call(
         gather_kernel,
         out_shape=jax.ShapeDtypeStruct((groups, count // groups, width), jnp.float32),
-        in_specs=[smem, smem, smem, smem, vmem],
+        in_specs=[smem, smem, smem, smem, smem, vmem],
         out_specs=vmem,
         scratch_shapes=[pltpu.SMEM((count,), jnp.int32)],
-    )(flags, cells, levels, coefs.reshape(-1), field)
+    )(slots, taken, cells, levels, coefs.reshape(-1), field)
 
 
 def advect_update(c, w, e, s, n, width):

time: 216 us -> 215 us (level); the launches traced: 220 us -> 216 us
  waiting for transfers between devices: 46 us -> 43.5 us
  other arithmetic: 6.89 us -> 9.07 us
    all_to_all x1, starting transfers between devices: 26.7 us -> 23.5 us  [summed_everywhere(): parts = lax.all_to_all(rows, axes, 0, 0, tiled=True)]
    reduce_sum x0 -> x2, other arithmetic: none -> 2.67 us  [gather_rows(): taken = jnp.sum(flags, keepdims=True)]
  transfers between devices with their start and end apart: 7 -> 7, of which waited for: 6 -> 6; matrix products, arithmetic and copies ran while one was open for 9% -> 10% of each run, Pallas kernels for 5% -> 5%
where the time goes in v5:
time: 215 us; the launch traced here: 216 us
  waiting for transfers between devices  43.5 us (20%)
  blocking collectives  43.4 us (20%)
  starting transfers between devices  42.1 us (20%)
  Pallas kernels  38.4 us (18%)
  local copies, waits for them, and re-layouts  19.9 us (9%)
  matrix products  17.3 us (8%)
  other arithmetic  9.07 us (4%)
    all_to_all x1, blocking collectives, summed_everywhere(): parts = lax.all_to_all(rows, axes, 0, 0, tiled=True)  43.4 us
    all_to_all x1, starting transfers between devices, summed_everywhere(): parts = lax.all_to_all(rows, axes, 0, 0, tiled=True)  23.5 us
    pallas_call x2, Pallas kernels, gather_rows(): pl.pallas_call(gather_kernel, out_shape=jax.ShapeDtypeStruct((groups, cou...  22.3 us
    all_to_all x1, waiting for transfers between devices, summed_everywhere(): parts = lax.all_to_all(rows, axes, 0, 0, tiled=True)  19.5 us
    all_to_all x2, waiting for transfers between devices, summed_everywhere(): return lax.all_to_all(copies, axes, 0, 0, tiled=True)  18.5 us
    dot_general x36, matrix products, product(): jnp.dot(left, right, precision=lax.Precision.HIGHEST, preferred_element_t...  11 us
    all_to_all x2, starting transfers between devices, summed_everywhere(): return lax.all_to_all(copies, axes, 0, 0, tiled=True)  10.7 us
    pallas_call x1, Pallas kernels, two_steps(): pl.pallas_call(two_steps_kernel, out_shape=jax.ShapeDtypeStruct(field.sha...  10.2 us
  transfers between devices with their start and end apart: 7, of which 6 were waited for; matrix products, arithmetic and copies ran while one was open for 10% of the time, Pallas kernels for 5%

profile of v5, /device:TPU:1, one launch (start us, length us, event | category | flops | bytes accessed | tf_op | source)
XLA Modules:
  0.0 215.9 jit_solution(2824248392576618608)
XLA Ops:
  0.0 1.1 fusion.131
  1.3 4.5 %collective-permute-start = (f32[2,64,384]{2,0,1:T(2,128)S(1)}, f32[2,64,384]{2,0,1:T(2,128)S(1)}, u32[]{:S(2)}, u32[]{:S(2)}) collective-permute-start(f32[2,64,384]{2,0,1:T(2,128)S(1)} %copy.117), channel_id=1, source_target_pairs={{0,8},{8,16},{16,24},{24,32},{32,40},{40,48},{48,56},{56,64},{64,7... | collective-permute-start | bytes 589832 | tf_op jit(solution)/shard_map/ppermute | solution.py:161
  6.0 1.2 fusion.130
  7.2 1.2 fusion.129
  9.2 0.7 slice_reduce_fusion.3
  9.9 0.6 fusion.135
  10.6 0.6 copy_bitcast_fusion
  11.2 0.6 mul.233.coef_ref
  11.8 1.4 convert_reduce_fusion.1
  13.2 1.0 collective-permute-done.1
  14.2 3.2 %collective-permute-start.3 = (f32[36,2,384]{2,0,1:T(8,128)S(1)}, f32[36,2,384]{2,0,1:T(8,128)S(1)}, u32[]{:S(2)}, u32[]{:S(2)}) collective-permute-start(f32[36,2,384]{2,0,1:T(8,128)S(1)} %pad_maximum_fusion.1), channel_id=1, source_target_pairs={{1,0},{2,1},{3,2},{4,3},{5,4},{6,5},{7,6},{0,7},{9,8},{10,9},{11,1... | collective-permute-start | bytes 331784 | tf_op jit(solution)/shard_map/ppermute | solution.py:166
  17.5 0.7 copy.79.west_ref
  18.2 0.7 copy.80.east_ref
  19.3 4.1 %collective-permute-done.2 = f32[36,2,384]{2,0,1:T(8,128)S(1)} collective-permute-done((f32[36,2,384]{2,0,1:T(8,128)S(1)}, f32[36,2,384]{2,0,1:T(8,128)S(1)}, u32[]{:S(2)}, u32[]{:S(2)}) %collective-permute-start.2) | collective-permute-done | bytes 110624 | tf_op jit(solution)/shard_map/ppermute | solution.py:165
  23.3 0.6 pad_maximum_fusion.2.corner_ref
  23.9 0.6 slice_bitcast_fusion
  24.6 0.6 slice_bitcast_fusion.2
  25.2 10.2 %shard_map.82 = f32[32,64,384]{2,1,0:T(8,128)} custom-call(f32[32,64,384]{2,1,0:T(8,128)} %field_ref.1, f32[2,64,384]{2,1,0:T(8,128)} %copy.79.west_ref, f32[2,64,384]{2,1,0:T(8,128)} %copy.80.east_ref, f32[32,384]{1,0:T(8,128)} %get-tuple-element.132.south0_ref, f32[32,384]{1,0:T(8,128)} %get-tuple-element.131.south1_ref, ...), custom_call_target="tpu_custom_call" | custom-call | tf_op jit(solution)/shard_map/pallas_call | solution.py:142
  35.4 11.2 %shard_map.83 = f32[4,1024,128]{2,1,0:T(8,128)} custom-call(s32[4096]{0:T(1024)} %get-tuple-element.146.slot_ref, s32[1]{0:T(128)} %bitcast.14.taken_ref, s32[4096]{0:T(1024)} %bitcast.144, s32[4096]{0:T(1024)} %bitcast.146, f32[12288]{0:T(1024)} %mul.233.coef_ref, f32[2048,384]{1,0:T(8,128)} %bitcast.123), custom_call_target="tpu_custom_call" | custom-call | tf_op jit(solution)/shard_map/pallas_call | solution.py:61
  46.6 3.6 %fusion.127 = f32[1024,128,1]{1,0,2:T(8,128)} fusion(f32[4,1024,128]{2,1,0:T(8,128)} %shard_map.83, s32[128]{0:T(128)S(1)} %get-tuple-element.164, s32[128]{0:T(128)S(1)} %get-tuple-element.165, s32[128]{0:T(128)S(1)} %get-tuple-element.163, s32[128]{0:T(128)S(1)} %get-tuple-element.166, pred[128]{0:T(512)(128)(4,1)S(1)} %get-tuple-element.161, ...), kind=kOutput, calls=%fused_computation.224 | convolution fusion | flops 805699584 | bytes 2623744 | tf_op jit(solution)/shard_map/krl,klo->ro/dot_general | solution.py:298
  50.1 23.5 %all-to-all-start = ((f32[256,4,128]{2,1,0:T(4,128)}), f32[256,4,128]{2,1,0:T(4,128)S(1)}, u32[]{:S(2)}, u32[]{:S(2)}) async-start(f32[256,4,128]{2,1,0:T(4,128)} %bitcast.19), calls=%async_computation | async-start | bytes 1048576 | tf_op jit(solution)/shard_map/all_to_all | solution.py:204
  75.3 19.5 %all-to-all-done = f32[256,4,128]{2,1,0:T(4,128)S(1)} async-done(((f32[256,4,128]{2,1,0:T(4,128)}), f32[256,4,128]{2,1,0:T(4,128)S(1)}, u32[]{:S(2)}, u32[]{:S(2)}) %all-to-all-start) | async-done | bytes 524320 | tf_op jit(solution)/shard_map/all_to_all | solution.py:204
  95.1 0.9 broadcast_in_dim.77
  96.0 5.3 %all-to-all-start.1 = ((f32[256,4,128]{2,1,0:T(4,128)}), f32[256,4,128]{2,1,0:T(4,128)S(1)}, u32[]{:S(2)}, u32[]{:S(2)}) async-start(f32[256,4,128]{2,1,0:T(4,128)} %broadcast_in_dim.77), calls=%async_computation.1 | async-start | bytes 1048576 | tf_op jit(solution)/shard_map/all_to_all | solution.py:207
  104.4 0.6 mul.250.coef_ref
  105.2 1.3 convert_reduce_fusion
  106.5 11.1 %shard_map.84 = f32[4,1024,128]{2,1,0:T(8,128)} custom-call(s32[4096]{0:T(1024)} %get-tuple-element.144.slot_ref, s32[1]{0:T(128)} %bitcast.30.taken_ref, s32[4096]{0:T(1024)} %bitcast.143, s32[4096]{0:T(1024)} %bitcast.145, f32[12288]{0:T(1024)} %mul.250.coef_ref, f32[2048,384]{1,0:T(8,128)} %bitcast.124), custom_call_target="tpu_custom_call" | custom-call | tf_op jit(solution)/shard_map/pallas_call | solution.py:61
  117.6 2.8 %fusion.125 = f32[1024,128,1]{1,0,2:T(8,128)S(1)} fusion(f32[4,1024,128]{2,1,0:T(8,128)} %shard_map.84, s32[128]{0:T(128)S(1)} %get-tuple-element.164, s32[128]{0:T(128)S(1)} %get-tuple-element.165, s32[128]{0:T(128)S(1)} %get-tuple-element.163, s32[128]{0:T(128)S(1)} %get-tuple-element.166, pred[128]{0:T(512)(128)(4,1)S(1)} %get-tuple-element.161, ...), kind=kOutput, calls=%fused_computation.223 | convolution fusion | flops 805699584 | bytes 2623744 | tf_op jit(solution)/shard_map/krl,klo->ro/dot_general | solution.py:298
  120.4 1.7 all-to-all-done.1
  122.1 0.8 multiply_reduce_fusion.1
  122.9 1.1 fusion.10
  124.1 0.6 reduce_max.18
  125.4 0.6 broadcast_divide_fusion.1
  126.1 2.2 %while.26 = (s32[]{:T(128)}, f32[32,32]{0,1:T(8,128)S(1)}, f32[32,32]{1,0:T(8,128)S(1)}, s32[]{:T(128)}) while((s32[]{:T(128)}, f32[32,32]{0,1:T(8,128)S(1)}, f32[32,32]{1,0:T(8,128)S(1)}, s32[]{:T(128)}) %tuple.89), condition=%wide.region_7.8_spmd.clone, body=%wide.region_6.7_spmd.clone.sunk | while | flops 1183746 | bytes 53301 | solution.py:268
  128.3 0.9 convolution_divide_fusion.1
  129.9 0.6 fusion.6
  130.8 43.4 %all_to_all.33 = f32[256,4,128]{2,1,0:T(4,128)S(1)} all-to-all(f32[256,4,128]{2,1,0:T(4,128)S(1)} %copy.98), channel_id=1, replica_groups=mesh['gx'=32,'gy'=8] {'gx','gy'}, dimensions={0} | all-to-all | bytes 1048576 | tf_op jit(solution)/shard_map/all_to_all | solution.py:204
  174.5 0.9 broadcast_in_dim.86
  175.3 5.4 %all-to-all-start.3 = ((f32[256,4,128]{2,1,0:T(4,128)}), f32[256,4,128]{2,1,0:T(4,128)S(1)}, u32[]{:S(2)}, u32[]{:S(2)}) async-start(f32[256,4,128]{2,1,0:T(4,128)} %broadcast_in_dim.86), calls=%async_computation.3 | async-start | bytes 1048576 | tf_op jit(solution)/shard_map/all_to_all | solution.py:207
  184.7 16.8 %all-to-all-done.3 = f32[256,4,128]{2,1,0:T(4,128)S(1)} async-done(((f32[256,4,128]{2,1,0:T(4,128)}), f32[256,4,128]{2,1,0:T(4,128)S(1)}, u32[]{:S(2)}, u32[]{:S(2)}) %all-to-all-start.3) | async-done | bytes 524320 | tf_op jit(solution)/shard_map/all_to_all | solution.py:207
  201.5 0.8 multiply_reduce_fusion
  202.3 1.1 fusion.8
  203.5 0.6 reduce_max.19
  204.8 0.6 broadcast_divide_fusion
  205.4 2.2 %while.27 = (s32[]{:T(128)}, f32[32,32]{0,1:T(8,128)S(1)}, f32[32,32]{1,0:T(8,128)S(1)}, s32[]{:T(128)}) while((s32[]{:T(128)}, f32[32,32]{0,1:T(8,128)S(1)}, f32[32,32]{1,0:T(8,128)S(1)}, s32[]{:T(128)}) %tuple.88), condition=%wide.region_16.17_spmd.clone, body=%wide.region_15.16_spmd.clone.sunk | while | flops 1183746 | bytes 53301 | solution.py:268
  207.7 0.9 convolution_divide_fusion
  209.3 0.8 mul.268.mix_ref
  210.0 5.9 %shard_map.85 = f32[2048,384]{1,0:T(8,128)} custom-call(f32[2048,384]{1,0:T(8,128)} %bitcast.125, f32[128,128]{1,0:T(8,128)} %mul.268.mix_ref), custom_call_target="tpu_custom_call" | custom-call | tf_op jit(solution)/shard_map/pallas_call | solution.py:189
  (144 shorter events, 16.9 us)
Async XLA Ops:
  0.0 8.4 %copy-start.3 = (s32[2,4096]{1,0:T(2,128)S(1)}, s32[2,4096]{1,0:T(2,128)}, u32[]{:S(2)}) copy-start(s32[2,4096]{1,0:T(2,128)} %param.13) | copy-start | bytes 98308
  0.0 9.1 %copy-start.4 = (f32[2,3,4096]{2,0,1:T(2,128)S(1)}, f32[2,3,4096]{2,0,1:T(2,128)}, u32[]{:S(2)}) copy-start(f32[2,3,4096]{2,0,1:T(2,128)} %param.16) | copy-start | bytes 294916
  0.0 9.2 %copy-start.5 = (s32[2,4096]{1,0:T(2,128)S(1)}, s32[2,4096]{1,0:T(2,128)}, u32[]{:S(2)}) copy-start(s32[2,4096]{1,0:T(2,128)} %param.14) | copy-start | bytes 98308
  0.0 9.9 %copy-start.6 = (s32[2,4096]{1,0:T(2,128)S(1)}, s32[2,4096]{1,0:T(2,128)}, u32[]{:S(2)}) copy-start(s32[2,4096]{1,0:T(2,128)} %param.15) | copy-start | bytes 98308
  1.3 11.9 %collective-permute-start = (f32[2,64,384]{2,0,1:T(2,128)S(1)}, f32[2,64,384]{2,0,1:T(2,128)S(1)}, u32[]{:S(2)}, u32[]{:S(2)}) collective-permute-start(f32[2,64,384]{2,0,1:T(2,128)S(1)} %copy.117), channel_id=1, source_target_pairs={{0,8},{8,16},{16,24},{24,32},{32,40},{40,48},{48,56},{56,64},{64,7... | collective-permute-start | bytes 589832 | tf_op jit(solution)/shard_map/ppermute | solution.py:161
  5.9 8.3 %collective-permute-start.1 = (f32[2,64,384]{2,0,1:T(2,128)S(1)}, f32[2,64,384]{2,0,1:T(2,128)S(1)}, u32[]{:S(2)}, u32[]{:S(2)}) collective-permute-start(f32[2,64,384]{2,0,1:T(2,128)S(1)} %copy.118), channel_id=1, source_target_pairs={{8,0},{16,8},{24,16},{32,24},{40,32},{48,40},{56,48},{64,56},{72,6... | collective-permute-start | bytes 589832 | tf_op jit(solution)/shard_map/ppermute | solution.py:162
  14.2 5.1 %collective-permute-start.3 = (f32[36,2,384]{2,0,1:T(8,128)S(1)}, f32[36,2,384]{2,0,1:T(8,128)S(1)}, u32[]{:S(2)}, u32[]{:S(2)}) collective-permute-start(f32[36,2,384]{2,0,1:T(8,128)S(1)} %pad_maximum_fusion.1), channel_id=1, source_target_pairs={{1,0},{2,1},{3,2},{4,3},{5,4},{6,5},{7,6},{0,7},{9,8},{10,9},{11,1... | collective-permute-start | bytes 331784 | tf_op jit(solution)/shard_map/ppermute | solution.py:166
  17.4 5.9 %collective-permute-start.2 = (f32[36,2,384]{2,0,1:T(8,128)S(1)}, f32[36,2,384]{2,0,1:T(8,128)S(1)}, u32[]{:S(2)}, u32[]{:S(2)}) collective-permute-start(f32[36,2,384]{2,0,1:T(8,128)S(1)} %pad_maximum_fusion), channel_id=1, source_target_pairs={{0,1},{1,2},{2,3},{3,4},{4,5},{5,6},{6,7},{7,0},{8,9},{9,10},{10,1... | collective-permute-start | bytes 331784 | tf_op jit(solution)/shard_map/ppermute | solution.py:165
  50.1 25.0 %copy-start.9 = (s32[1,1,2,16]{3,2,1,0:T(2,128)S(1)}, s32[1,1,2,16]{3,2,1,0:T(2,128)}, u32[]{:S(2)}) copy-start(s32[1,1,2,16]{3,2,1,0:T(2,128)} %param.19) | copy-start | bytes 388
  50.1 44.7 %all-to-all-start = ((f32[256,4,128]{2,1,0:T(4,128)}), f32[256,4,128]{2,1,0:T(4,128)S(1)}, u32[]{:S(2)}, u32[]{:S(2)}) async-start(f32[256,4,128]{2,1,0:T(4,128)} %bitcast.19), calls=%async_computation | async-start | bytes 1048576 | tf_op jit(solution)/shard_map/all_to_all | solution.py:204
  74.9 26.8 %copy-start.7 = (f32[2,4096]{1,0:T(2,128)S(1)}, f32[2,4096]{1,0:T(2,128)}, u32[]{:S(2)}) copy-start(f32[2,4096]{1,0:T(2,128)} %param.17) | copy-start | bytes 98308
  74.9 26.8 %copy-start.8 = (f32[2,4096]{1,0:T(2,128)S(1)}, f32[2,4096]{1,0:T(2,128)}, u32[]{:S(2)}) copy-start(f32[2,4096]{1,0:T(2,128)} %param.18) | copy-start | bytes 98308
  96.0 26.2 %all-to-all-start.1 = ((f32[256,4,128]{2,1,0:T(4,128)}), f32[256,4,128]{2,1,0:T(4,128)S(1)}, u32[]{:S(2)}, u32[]{:S(2)}) async-start(f32[256,4,128]{2,1,0:T(4,128)} %broadcast_in_dim.77), calls=%async_computation.1 | async-start | bytes 1048576 | tf_op jit(solution)/shard_map/all_to_all | solution.py:207
  103.9 13.7 %copy-start = (f32[32,32]{1,0:T(8,128)}, f32[32,32]{1,0:T(8,128)S(1)}, u32[]{:S(2)}) copy-start(f32[32,32]{1,0:T(8,128)S(1)} %copy.92) | copy-start | bytes 12292
  122.9 3.1 %copy-start.2 = (f32[32,32]{1,0:T(8,128)S(1)}, f32[32,32]{1,0:T(8,128)}, u32[]{:S(2)}) copy-start(f32[32,32]{1,0:T(8,128)} %copy-done) | copy-start | bytes 12292
  175.3 26.2 %all-to-all-start.3 = ((f32[256,4,128]{2,1,0:T(4,128)}), f32[256,4,128]{2,1,0:T(4,128)S(1)}, u32[]{:S(2)}, u32[]{:S(2)}) async-start(f32[256,4,128]{2,1,0:T(4,128)} %broadcast_in_dim.86), calls=%async_computation.3 | async-start | bytes 1048576 | tf_op jit(solution)/shard_map/all_to_all | solution.py:207
  202.3 3.1 %copy-start.1 = (f32[32,32]{1,0:T(8,128)S(1)}, f32[32,32]{1,0:T(8,128)}, u32[]{:S(2)}) copy-start(f32[32,32]{1,0:T(8,128)} %copy-done) | copy-start | bytes 12292

commit v6 on v4

--- a/solution.py
+++ b/solution.py
@@ -20,8 +20,9 @@
 
 def gather_kernel(flag_ref, cell_ref, level_ref, coef_ref, field_ref, out_ref, chosen_ref):
     count = cell_ref.shape[0]
-    groups, rows, width = out_ref.shape
-    lane_level = lax.broadcasted_iota(jnp.int32, (1, width), 1) // ENS
+    rows, width = out_ref.shape
+    groups = width // ENS
+    lane_group = lax.broadcasted_iota(jnp.int32, (8, width), 1) // ENS
     sublane = lax.broadcasted_iota(jnp.int32, (8, width), 0)
     out_ref[...] = jnp.zeros(out_ref.shape, out_ref.dtype)
 
@@ -39,11 +40,13 @@
             + coef_ref[count + j] * picked[:, width:2 * width]
             + coef_ref[2 * count + j] * picked[:, 2 * width:3 * width]
         )
-        value = jnp.where(lane_level == level_ref[j], value, 0.0)
+        group = j % groups
+        turned = pltpu.roll(value, ((group - level_ref[j]) % groups) * ENS, 1)
         row = j // groups
         first = pl.multiple_of((row // 8) * 8, 8)
-        tile = out_ref[j % groups, pl.ds(first, 8), :]
-        out_ref[j % groups, pl.ds(first, 8), :] = jnp.where(sublane == row % 8, value, tile)
+        tile = out_ref[pl.ds(first, 8), :]
+        keep = (sublane == row % 8) & (lane_group == group)
+        out_ref[pl.ds(first, 8), :] = jnp.where(keep, turned, tile)
         return carry
 
     lax.fori_loop(0, taken, body, 0)
@@ -57,7 +60,7 @@
     vmem = pl.BlockSpec(memory_space=pltpu.VMEM)
     return pl.pallas_call(
         gather_kernel,
-        out_shape=jax.ShapeDtypeStruct((groups, count // groups, width), jnp.float32),
+        out_shape=jax.ShapeDtypeStruct((count // groups, width), jnp.float32),
         in_specs=[smem, smem, smem, smem, vmem],
         out_specs=vmem,
         scratch_shapes=[pltpu.SMEM((count,), jnp.int32)],
@@ -286,17 +289,6 @@
     width = features // COMP
     groups = width // ENS
     owned = (obs_owner == own_tile).astype(jnp.float32)
-    lane_in = lax.broadcasted_iota(jnp.int32, (groups, width, groups * ENS), 0)
-    level_lane = lax.broadcasted_iota(jnp.int32, (groups, width, groups * ENS), 1)
-    dense_lane = lax.broadcasted_iota(jnp.int32, (groups, width, groups * ENS), 2)
-    fold = ((lane_in == dense_lane // ENS) & (level_lane % ENS == dense_lane % ENS)).astype(jnp.float32)
-
-    def folded(spread):
-        return jnp.einsum(
-            "krl,klo->ro", spread, fold, precision=lax.Precision.HIGHEST,
-            preferred_element_type=jnp.float32,
-        )
-
     def observed(batch_index):
         masked_coefs = obs_coef[batch_index] * owned[batch_index][None, :]
         spread = gather_rows(
@@ -306,7 +298,7 @@
             masked_coefs,
             cells,
         )
-        return folded(spread)
+        return spread
 
     def mixing(local_terms, batch_index):
         predicted = summed_everywhere(local_terms)

time: 216 us -> 277 us (1.28); the launches traced: 220 us -> 277 us
  blocking collectives: 45.3 us -> 152 us
  starting transfers between devices: 44.2 us -> 18.6 us
  waiting for transfers between devices: 46 us -> 26.9 us
  matrix products: 17.3 us -> 11 us
    all_to_all x1 -> x2, blocking collectives: 45.3 us -> 152 us  [summed_everywhere(): parts = lax.all_to_all(rows, axes, 0, 0, tiled=True)]
    all_to_all x1 -> x0, starting transfers between devices: 26.7 us -> none  [summed_everywhere(): parts = lax.all_to_all(rows, axes, 0, 0, tiled=True)]
    all_to_all x1 -> x0, waiting for transfers between devices: 19.7 us -> none  [summed_everywhere(): parts = lax.all_to_all(rows, axes, 0, 0, tiled=True)]
    dot_general x2 -> x0, matrix products: 6.31 us -> none  [folded(): jnp.einsum('krl,klo->ro', spread, fold, precision=lax.Precision.HIGHEST,...]
  transfers between devices with their start and end apart: 7 -> 6, of which waited for: 6 -> 5; matrix products, arithmetic and copies ran while one was open for 9% -> 7% of each run, Pallas kernels for 5% -> 4%
where the time goes in v6:
time: 277 us
  blocking collectives  152 us (55%)
  Pallas kernels  37.4 us (14%)
  waiting for transfers between devices  26.9 us (10%)
  local copies, waits for them, and re-layouts  20.5 us (7%)
  starting transfers between devices  18.6 us (7%)
  matrix products  11 us (4%)
  other arithmetic  7.65 us (3%)
    all_to_all x2, blocking collectives, summed_everywhere(): parts = lax.all_to_all(rows, axes, 0, 0, tiled=True)  152 us
    all_to_all x2, waiting for transfers between devices, summed_everywhere(): return lax.all_to_all(copies, axes, 0, 0, tiled=True)  21.8 us
    pallas_call x2, Pallas kernels, gather_rows(): pl.pallas_call(gather_kernel, out_shape=jax.ShapeDtypeStruct((count // gr...  21.4 us
    dot_general x36, matrix products, product(): jnp.dot(left, right, precision=lax.Precision.HIGHEST, preferred_element_t...  11 us
    all_to_all x2, starting transfers between devices, summed_everywhere(): return lax.all_to_all(copies, axes, 0, 0, tiled=True)  10.3 us
    pallas_call x1, Pallas kernels, two_steps(): pl.pallas_call(two_steps_kernel, out_shape=jax.ShapeDtypeStruct(field.sha...  10.2 us
    pallas_call x1, Pallas kernels, mixed_once(): pl.pallas_call(mix_kernel, out_shape=jax.ShapeDtypeStruct(rows.shape, row...  5.86 us
  transfers between devices with their start and end apart: 6, of which 5 were waited for; matrix products, arithmetic and copies ran while one was open for 7% of the time, Pallas kernels for 4%

profile of v6, /device:TPU:1, one launch (start us, length us, event | category | flops | bytes accessed | tf_op | source)
XLA Modules:
  0.0 276.6 jit_solution(15813060768200814626)
XLA Ops:
  0.0 1.1 fusion.126
  1.2 4.5 %collective-permute-start = (f32[2,64,384]{2,0,1:T(2,128)S(1)}, f32[2,64,384]{2,0,1:T(2,128)S(1)}, u32[]{:S(2)}, u32[]{:S(2)}) collective-permute-start(f32[2,64,384]{2,0,1:T(2,128)S(1)} %copy.117), channel_id=1, source_target_pairs={{0,8},{8,16},{16,24},{24,32},{32,40},{40,48},{48,56},{56,64},{64,7... | collective-permute-start | bytes 589832 | tf_op jit(solution)/shard_map/ppermute | solution.py:161
  5.9 1.2 fusion.125
  7.1 1.2 fusion.124
  8.4 0.8 compare_convert_fusion
  9.2 0.6 convert_element_type.101.flag_ref
  9.8 1.1 fusion.129
  10.9 0.6 fusion.130
  11.6 0.6 copy_bitcast_fusion
  12.2 0.6 mul.233.coef_ref
  12.8 0.7 slice_reduce_fusion.1
  13.5 0.6 collective-permute-done.1
  14.2 3.6 %collective-permute-start.3 = (f32[36,2,384]{2,0,1:T(8,128)S(1)}, f32[36,2,384]{2,0,1:T(8,128)S(1)}, u32[]{:S(2)}, u32[]{:S(2)}) collective-permute-start(f32[36,2,384]{2,0,1:T(8,128)S(1)} %pad_maximum_fusion.1), channel_id=1, source_target_pairs={{1,0},{2,1},{3,2},{4,3},{5,4},{6,5},{7,6},{0,7},{9,8},{10,9},{11,1... | collective-permute-start | bytes 331784 | tf_op jit(solution)/shard_map/ppermute | solution.py:166
  17.9 0.7 copy.79.west_ref
  18.5 0.7 copy.80.east_ref
  19.6 4.1 %collective-permute-done.2 = f32[36,2,384]{2,0,1:T(8,128)S(1)} collective-permute-done((f32[36,2,384]{2,0,1:T(8,128)S(1)}, f32[36,2,384]{2,0,1:T(8,128)S(1)}, u32[]{:S(2)}, u32[]{:S(2)}) %collective-permute-start.2) | collective-permute-done | bytes 110624 | tf_op jit(solution)/shard_map/ppermute | solution.py:165
  23.7 0.6 pad_maximum_fusion.2.corner_ref
  24.3 0.6 slice_bitcast_fusion
  24.9 0.6 slice_bitcast_fusion.2
  25.6 10.2 %shard_map.82 = f32[32,64,384]{2,1,0:T(8,128)} custom-call(f32[32,64,384]{2,1,0:T(8,128)} %field_ref.1, f32[2,64,384]{2,1,0:T(8,128)} %copy.79.west_ref, f32[2,64,384]{2,1,0:T(8,128)} %copy.80.east_ref, f32[32,384]{1,0:T(8,128)} %get-tuple-element.132.south0_ref, f32[32,384]{1,0:T(8,128)} %get-tuple-element.131.south1_ref, ...), custom_call_target="tpu_custom_call" | custom-call | tf_op jit(solution)/shard_map/pallas_call | solution.py:142
  35.8 10.8 %shard_map.83 = f32[1024,128]{1,0:T(8,128)} custom-call(s32[4096]{0:T(1024)} %convert_element_type.101.flag_ref, s32[4096]{0:T(1024)} %bitcast.131, s32[4096]{0:T(1024)} %bitcast.133, f32[12288]{0:T(1024)} %mul.233.coef_ref, f32[2048,384]{1,0:T(8,128)} %bitcast.109), custom_call_target="tpu_custom_call" | custom-call | tf_op jit(solution)/shard_map/pallas_call | solution.py:61
  46.5 77.4 %all_to_all.33 = f32[256,4,128]{2,1,0:T(4,128)S(1)} all-to-all(f32[256,4,128]{2,1,0:T(4,128)} %bitcast.113), channel_id=1, replica_groups=mesh['gx'=32,'gy'=8] {'gx','gy'}, dimensions={0} | all-to-all | bytes 1048576 | tf_op jit(solution)/shard_map/all_to_all | solution.py:204
  124.2 0.9 broadcast_in_dim.70
  125.0 5.2 %all-to-all-start.1 = ((f32[256,4,128]{2,1,0:T(4,128)}), f32[256,4,128]{2,1,0:T(4,128)S(1)}, u32[]{:S(2)}, u32[]{:S(2)}) async-start(f32[256,4,128]{2,1,0:T(4,128)} %broadcast_in_dim.70), calls=%async_computation.1 | async-start | bytes 1048576 | tf_op jit(solution)/shard_map/all_to_all | solution.py:207
  131.0 0.5 squeeze.67
  134.5 0.6 convert_element_type.108.flag_ref
  135.2 0.6 mul.250.coef_ref
  135.8 10.6 %shard_map.84 = f32[1024,128]{1,0:T(8,128)} custom-call(s32[4096]{0:T(1024)} %convert_element_type.108.flag_ref, s32[4096]{0:T(1024)} %bitcast.130, s32[4096]{0:T(1024)} %bitcast.132, f32[12288]{0:T(1024)} %mul.250.coef_ref, f32[2048,384]{1,0:T(8,128)} %bitcast.110), custom_call_target="tpu_custom_call" | custom-call | tf_op jit(solution)/shard_map/pallas_call | solution.py:61
  146.4 4.8 %all-to-all-done.1 = f32[256,4,128]{2,1,0:T(4,128)S(1)} async-done(((f32[256,4,128]{2,1,0:T(4,128)}), f32[256,4,128]{2,1,0:T(4,128)S(1)}, u32[]{:S(2)}, u32[]{:S(2)}) %all-to-all-start.1) | async-done | bytes 524320 | tf_op jit(solution)/shard_map/all_to_all | solution.py:207
  151.2 0.8 multiply_reduce_fusion.1
  152.0 1.1 fusion.10
  153.2 0.6 reduce_max.18
  154.5 0.6 broadcast_divide_fusion.1
  155.2 2.2 while.26
  157.4 0.9 convolution_divide_fusion.1
  159.0 0.6 fusion.6
  159.9 75.0 %all_to_all.34 = f32[256,4,128]{2,1,0:T(4,128)S(1)} all-to-all(f32[256,4,128]{2,1,0:T(4,128)S(1)} %copy.98), channel_id=1, replica_groups=mesh['gx'=32,'gy'=8] {'gx','gy'}, dimensions={0} | all-to-all | bytes 1048576 | tf_op jit(solution)/shard_map/all_to_all | solution.py:204
  235.2 0.9 broadcast_in_dim.78
  236.0 5.2 %all-to-all-start.3 = ((f32[256,4,128]{2,1,0:T(4,128)}), f32[256,4,128]{2,1,0:T(4,128)S(1)}, u32[]{:S(2)}, u32[]{:S(2)}) async-start(f32[256,4,128]{2,1,0:T(4,128)} %broadcast_in_dim.78), calls=%async_computation.3 | async-start | bytes 1048576 | tf_op jit(solution)/shard_map/all_to_all | solution.py:207
  245.2 17.0 %all-to-all-done.3 = f32[256,4,128]{2,1,0:T(4,128)S(1)} async-done(((f32[256,4,128]{2,1,0:T(4,128)}), f32[256,4,128]{2,1,0:T(4,128)S(1)}, u32[]{:S(2)}, u32[]{:S(2)}) %all-to-all-start.3) | async-done | bytes 524320 | tf_op jit(solution)/shard_map/all_to_all | solution.py:207
  262.2 0.7 multiply_reduce_fusion
  263.0 1.1 fusion.8
  264.1 0.6 reduce_max.19
  265.4 0.6 broadcast_divide_fusion
  266.1 2.2 while.27
  268.4 0.9 convolution_divide_fusion
  269.9 0.8 mul.268.mix_ref
  270.7 5.9 %shard_map.85 = f32[2048,384]{1,0:T(8,128)} custom-call(f32[2048,384]{1,0:T(8,128)} %bitcast.111, f32[128,128]{1,0:T(8,128)} %mul.268.mix_ref), custom_call_target="tpu_custom_call" | custom-call | tf_op jit(solution)/shard_map/pallas_call | solution.py:189
  (132 shorter events, 15.2 us)
Async XLA Ops:
  0.0 12.8 %copy-start.4 = (s32[2,4096]{1,0:T(2,128)S(1)}, s32[2,4096]{1,0:T(2,128)}, u32[]{:S(2)}) copy-start(s32[2,4096]{1,0:T(2,128)} %param.13) | copy-start | bytes 98308
  0.0 10.9 %copy-start.6 = (s32[2,4096]{1,0:T(2,128)S(1)}, s32[2,4096]{1,0:T(2,128)}, u32[]{:S(2)}) copy-start(s32[2,4096]{1,0:T(2,128)} %param.15) | copy-start | bytes 98308
  0.0 12.8 %copy-start.5 = (s32[2,4096]{1,0:T(2,128)S(1)}, s32[2,4096]{1,0:T(2,128)}, u32[]{:S(2)}) copy-start(s32[2,4096]{1,0:T(2,128)} %param.14) | copy-start | bytes 98308
  1.2 12.3 %collective-permute-start = (f32[2,64,384]{2,0,1:T(2,128)S(1)}, f32[2,64,384]{2,0,1:T(2,128)S(1)}, u32[]{:S(2)}, u32[]{:S(2)}) collective-permute-start(f32[2,64,384]{2,0,1:T(2,128)S(1)} %copy.117), channel_id=1, source_target_pairs={{0,8},{8,16},{16,24},{24,32},{32,40},{40,48},{48,56},{56,64},{64,7... | collective-permute-start | bytes 589832 | tf_op jit(solution)/shard_map/ppermute | solution.py:161
  5.9 8.3 %collective-permute-start.1 = (f32[2,64,384]{2,0,1:T(2,128)S(1)}, f32[2,64,384]{2,0,1:T(2,128)S(1)}, u32[]{:S(2)}, u32[]{:S(2)}) collective-permute-start(f32[2,64,384]{2,0,1:T(2,128)S(1)} %copy.118), channel_id=1, source_target_pairs={{8,0},{16,8},{24,16},{32,24},{40,32},{48,40},{56,48},{64,56},{72,6... | collective-permute-start | bytes 589832 | tf_op jit(solution)/shard_map/ppermute | solution.py:162
  14.2 5.5 %collective-permute-start.3 = (f32[36,2,384]{2,0,1:T(8,128)S(1)}, f32[36,2,384]{2,0,1:T(8,128)S(1)}, u32[]{:S(2)}, u32[]{:S(2)}) collective-permute-start(f32[36,2,384]{2,0,1:T(8,128)S(1)} %pad_maximum_fusion.1), channel_id=1, source_target_pairs={{1,0},{2,1},{3,2},{4,3},{5,4},{6,5},{7,6},{0,7},{9,8},{10,9},{11,1... | collective-permute-start | bytes 331784 | tf_op jit(solution)/shard_map/ppermute | solution.py:166
  17.8 5.9 %collective-permute-start.2 = (f32[36,2,384]{2,0,1:T(8,128)S(1)}, f32[36,2,384]{2,0,1:T(8,128)S(1)}, u32[]{:S(2)}, u32[]{:S(2)}) collective-permute-start(f32[36,2,384]{2,0,1:T(8,128)S(1)} %pad_maximum_fusion), channel_id=1, source_target_pairs={{0,1},{1,2},{2,3},{3,4},{4,5},{5,6},{6,7},{7,0},{8,9},{9,10},{10,1... | collective-permute-start | bytes 331784 | tf_op jit(solution)/shard_map/ppermute | solution.py:165
  46.5 85.2 %copy-start.9 = (s32[1,1,2,16]{3,2,1,0:T(2,128)S(1)}, s32[1,1,2,16]{3,2,1,0:T(2,128)}, u32[]{:S(2)}) copy-start(s32[1,1,2,16]{3,2,1,0:T(2,128)} %param.19) | copy-start | bytes 388
  123.9 8.3 %copy-start.7 = (f32[2,4096]{1,0:T(2,128)S(1)}, f32[2,4096]{1,0:T(2,128)}, u32[]{:S(2)}) copy-start(f32[2,4096]{1,0:T(2,128)} %param.17) | copy-start | bytes 98308
  123.9 8.3 %copy-start.8 = (f32[2,4096]{1,0:T(2,128)S(1)}, f32[2,4096]{1,0:T(2,128)}, u32[]{:S(2)}) copy-start(f32[2,4096]{1,0:T(2,128)} %param.18) | copy-start | bytes 98308
  125.0 26.2 %all-to-all-start.1 = ((f32[256,4,128]{2,1,0:T(4,128)}), f32[256,4,128]{2,1,0:T(4,128)S(1)}, u32[]{:S(2)}, u32[]{:S(2)}) async-start(f32[256,4,128]{2,1,0:T(4,128)} %broadcast_in_dim.70), calls=%async_computation.1 | async-start | bytes 1048576 | tf_op jit(solution)/shard_map/all_to_all | solution.py:207
  134.5 17.5 %copy-start.1 = (f32[32,32]{1,0:T(8,128)}, f32[32,32]{1,0:T(8,128)S(1)}, u32[]{:S(2)}) copy-start(f32[32,32]{1,0:T(8,128)S(1)} %copy.92) | copy-start | bytes 12292
  152.0 7.0 %copy-start = (f32[1024,128]{1,0:T(8,128)S(1)}, f32[1024,128]{1,0:T(8,128)}, u32[]{:S(2)}) copy-start(f32[1024,128]{1,0:T(8,128)} %shard_map.84) | copy-start | bytes 1572868
  152.0 3.1 %copy-start.3 = (f32[32,32]{1,0:T(8,128)S(1)}, f32[32,32]{1,0:T(8,128)}, u32[]{:S(2)}) copy-start(f32[32,32]{1,0:T(8,128)} %copy-done.1) | copy-start | bytes 12292
  236.0 26.2 %all-to-all-start.3 = ((f32[256,4,128]{2,1,0:T(4,128)}), f32[256,4,128]{2,1,0:T(4,128)S(1)}, u32[]{:S(2)}, u32[]{:S(2)}) async-start(f32[256,4,128]{2,1,0:T(4,128)} %broadcast_in_dim.78), calls=%async_computation.3 | async-start | bytes 1048576 | tf_op jit(solution)/shard_map/all_to_all | solution.py:207
  262.2 3.9 %copy-start.2 = (f32[32,32]{1,0:T(8,128)S(1)}, f32[32,32]{1,0:T(8,128)}, u32[]{:S(2)}) copy-start(f32[32,32]{1,0:T(8,128)} %copy-done.1) | copy-start | bytes 12292

commit v7 on v6

--- a/solution.py
+++ b/solution.py
@@ -18,53 +18,51 @@
 radius_share = 0.25
 
 
-def gather_kernel(flag_ref, cell_ref, level_ref, coef_ref, field_ref, out_ref, chosen_ref):
+def gather_kernel(busy_ref, cell_ref, level_ref, coef_ref, field_ref, out_ref):
     count = cell_ref.shape[0]
-    rows, width = out_ref.shape
+    width = field_ref.shape[1] // 3
+    lane_level = lax.broadcasted_iota(jnp.int32, (1, width), 1) // ENS
+    sublane = lax.broadcasted_iota(jnp.int32, (8, width), 0)
     groups = width // ENS
-    lane_group = lax.broadcasted_iota(jnp.int32, (8, width), 1) // ENS
-    sublane = lax.broadcasted_iota(jnp.int32, (8, width), 0)
     out_ref[...] = jnp.zeros(out_ref.shape, out_ref.dtype)
 
-    def choose(j, taken):
-        chosen_ref[taken] = j
-        return taken + flag_ref[j]
-
-    taken = lax.fori_loop(0, count, choose, 0, unroll=8)
-
-    def body(i, carry):
-        j = chosen_ref[i]
-        picked = field_ref[pl.ds(cell_ref[j], 1), :]
-        value = (
-            coef_ref[j] * picked[:, 0:width]
-            + coef_ref[count + j] * picked[:, width:2 * width]
-            + coef_ref[2 * count + j] * picked[:, 2 * width:3 * width]
-        )
-        group = j % groups
-        turned = pltpu.roll(value, ((group - level_ref[j]) % groups) * ENS, 1)
-        row = j // groups
-        first = pl.multiple_of((row // 8) * 8, 8)
-        tile = out_ref[pl.ds(first, 8), :]
-        keep = (sublane == row % 8) & (lane_group == group)
-        out_ref[pl.ds(first, 8), :] = jnp.where(keep, turned, tile)
+    def body(block, carry):
+        @pl.when(busy_ref[block] > 0)
+        def _():
+            gathered = [jnp.zeros((8, width), jnp.float32) for k in range(groups)]
+            for i in range(8):
+                for k in range(groups):
+                    j = (block * 8 + i) * groups + k
+                    picked = field_ref[pl.ds(cell_ref[j], 1), :]
+                    value = (
+                        coef_ref[j] * picked[:, 0:width]
+                        + coef_ref[count + j] * picked[:, width:2 * width]
+                        + coef_ref[2 * count + j] * picked[:, 2 * width:3 * width]
+                    )
+                    value = jnp.where(lane_level == level_ref[j], value, 0.0)
+                    gathered[k] = jnp.where(sublane == i, value, gathered[k])
+            first = pl.multiple_of(block * 8, 8)
+            for k in range(groups):
+                out_ref[pl.ds(first, 8), k * width:(k + 1) * width] = gathered[k]
+
         return carry
 
-    lax.fori_loop(0, taken, body, 0)
+    lax.fori_loop(0, count // (8 * groups), body, 0)
 
 
 def gather_rows(flags, cells, levels, coefs, field):
     count = cells.shape[0]
     width = field.shape[1] // 3
     groups = width // ENS
+    busy = jnp.max(flags.reshape(-1, 8 * groups), axis=1)
     smem = pl.BlockSpec(memory_space=pltpu.SMEM)
     vmem = pl.BlockSpec(memory_space=pltpu.VMEM)
     return pl.pallas_call(
         gather_kernel,
-        out_shape=jax.ShapeDtypeStruct((count // groups, width), jnp.float32),
+        out_shape=jax.ShapeDtypeStruct((count // groups, groups * width), jnp.float32),
         in_specs=[smem, smem, smem, smem, vmem],
         out_specs=vmem,
-        scratch_shapes=[pltpu.SMEM((count,), jnp.int32)],
-    )(flags, cells, levels, coefs.reshape(-1), field)
+    )(busy, cells, levels, coefs.reshape(-1), field)
 
 
 def advect_update(c, w, e, s, n, width):
@@ -289,6 +287,12 @@
     width = features // COMP
     groups = width // ENS
     owned = (obs_owner == own_tile).astype(jnp.float32)
+    spread_lane = lax.broadcasted_iota(jnp.int32, (groups * width, groups * ENS), 0)
+    dense_lane = lax.broadcasted_iota(jnp.int32, (groups * width, groups * ENS), 1)
+    fold = (
+        (spread_lane // width == dense_lane // ENS) & (spread_lane % ENS == dense_lane % ENS)
+    ).astype(jnp.float32)
+
     def observed(batch_index):
         masked_coefs = obs_coef[batch_index] * owned[batch_index][None, :]
         spread = gather_rows(
@@ -298,7 +302,7 @@
             masked_coefs,
             cells,
         )
-        return spread
+        return product(spread, fold)
 
     def mixing(local_terms, batch_index):
         predicted = summed_everywhere(local_terms)

time: 277 us -> 207 us (0.75)
  blocking collectives: 152 us -> 40 us
  waiting for transfers between devices: 26.9 us -> 45.1 us
  starting transfers between devices: 18.6 us -> 36.7 us
  matrix products: 11 us -> 17.9 us
    all_to_all x2 -> x1, blocking collectives: 152 us -> 40 us  [summed_everywhere(): parts = lax.all_to_all(rows, axes, 0, 0, tiled=True)]
    all_to_all x0 -> x1, waiting for transfers between devices: none -> 19.7 us  [summed_everywhere(): parts = lax.all_to_all(rows, axes, 0, 0, tiled=True)]
    all_to_all x0 -> x1, starting transfers between devices: none -> 19.1 us  [summed_everywhere(): parts = lax.all_to_all(rows, axes, 0, 0, tiled=True)]
    dot_general x36 -> x38, matrix products: 11 us -> 17.9 us  [product(): jnp.dot(left, right, precision=lax.Precision.HIGHEST, preferred_element_t...]
    all_to_all x2, waiting for transfers between devices: 21.8 us -> 19 us  [summed_everywhere(): return lax.all_to_all(copies, axes, 0, 0, tiled=True)]
  transfers between devices with their start and end apart: 6 -> 7, of which waited for: 5 -> 6; matrix products, arithmetic and copies ran while one was open for 7% -> 10% of each run, Pallas kernels for 4% -> 5%
where the time goes in v7:
time: 207 us; the launch traced here: 209 us
  waiting for transfers between devices  45.1 us (22%)
  blocking collectives  40 us (19%)
  Pallas kernels  39.8 us (19%)
  starting transfers between devices  36.7 us (18%)
  local copies, waits for them, and re-layouts  19.6 us (9%)
  matrix products  17.9 us (9%)
  other arithmetic  7.16 us (3%)
    all_to_all x1, blocking collectives, summed_everywhere(): parts = lax.all_to_all(rows, axes, 0, 0, tiled=True)  40 us
    pallas_call x2, Pallas kernels, gather_rows(): pl.pallas_call(gather_kernel, out_shape=jax.ShapeDtypeStruct((count // gr...  23.8 us
    all_to_all x1, waiting for transfers between devices, summed_everywhere(): parts = lax.all_to_all(rows, axes, 0, 0, tiled=True)  19.7 us
    all_to_all x1, starting transfers between devices, summed_everywhere(): parts = lax.all_to_all(rows, axes, 0, 0, tiled=True)  19.1 us
    all_to_all x2, waiting for transfers between devices, summed_everywhere(): return lax.all_to_all(copies, axes, 0, 0, tiled=True)  19 us
    dot_general x38, matrix products, product(): jnp.dot(left, right, precision=lax.Precision.HIGHEST, preferred_element_t...  17.9 us
    all_to_all x2, starting transfers between devices, summed_everywhere(): return lax.all_to_all(copies, axes, 0, 0, tiled=True)  10.7 us
    pallas_call x1, Pallas kernels, two_steps(): pl.pallas_call(two_steps_kernel, out_shape=jax.ShapeDtypeStruct(field.sha...  10.2 us
  transfers between devices with their start and end apart: 7, of which 6 were waited for; matrix products, arithmetic and copies ran while one was open for 10% of the time, Pallas kernels for 5%

profile of v7, /device:TPU:1, one launch (start us, length us, event | category | flops | bytes accessed | tf_op | source)
XLA Modules:
  0.0 208.7 jit_solution(9767628834717698037)
XLA Ops:
  0.0 1.1 fusion.138
  1.3 4.5 %collective-permute-start = (f32[2,64,384]{2,0,1:T(2,128)S(1)}, f32[2,64,384]{2,0,1:T(2,128)S(1)}, u32[]{:S(2)}, u32[]{:S(2)}) collective-permute-start(f32[2,64,384]{2,0,1:T(2,128)S(1)} %copy.117), channel_id=1, source_target_pairs={{0,8},{8,16},{16,24},{24,32},{32,40},{40,48},{48,56},{56,64},{64,7... | collective-permute-start | bytes 589832 | tf_op jit(solution)/shard_map/ppermute | solution.py:159
  6.0 1.2 fusion.137
  7.2 1.2 fusion.136
  9.0 0.6 fusion.143
  9.6 0.6 copy_bitcast_fusion
  10.3 0.6 reduce_max.36.busy_ref
  10.8 0.6 mul.238.coef_ref
  11.5 0.6 slice_reduce_fusion.6
  12.1 2.0 collective-permute-done.1
  14.2 2.3 %collective-permute-start.3 = (f32[36,2,384]{2,0,1:T(8,128)S(1)}, f32[36,2,384]{2,0,1:T(8,128)S(1)}, u32[]{:S(2)}, u32[]{:S(2)}) collective-permute-start(f32[36,2,384]{2,0,1:T(8,128)S(1)} %pad_maximum_fusion.1), channel_id=1, source_target_pairs={{1,0},{2,1},{3,2},{4,3},{5,4},{6,5},{7,6},{0,7},{9,8},{10,9},{11,1... | collective-permute-start | bytes 331784 | tf_op jit(solution)/shard_map/ppermute | solution.py:164
  16.6 0.7 copy.79.west_ref
  17.3 0.7 copy.80.east_ref
  18.4 4.1 %collective-permute-done.2 = f32[36,2,384]{2,0,1:T(8,128)S(1)} collective-permute-done((f32[36,2,384]{2,0,1:T(8,128)S(1)}, f32[36,2,384]{2,0,1:T(8,128)S(1)}, u32[]{:S(2)}, u32[]{:S(2)}) %collective-permute-start.2) | collective-permute-done | bytes 110624 | tf_op jit(solution)/shard_map/ppermute | solution.py:163
  22.4 0.6 pad_maximum_fusion.2.corner_ref
  23.0 0.6 slice_bitcast_fusion
  23.7 0.6 slice_bitcast_fusion.2
  24.3 10.2 %shard_map.82 = f32[32,64,384]{2,1,0:T(8,128)} custom-call(f32[32,64,384]{2,1,0:T(8,128)} %field_ref.1, f32[2,64,384]{2,1,0:T(8,128)} %copy.79.west_ref, f32[2,64,384]{2,1,0:T(8,128)} %copy.80.east_ref, f32[32,384]{1,0:T(8,128)} %get-tuple-element.134.south0_ref, f32[32,384]{1,0:T(8,128)} %get-tuple-element.133.south1_ref, ...), custom_call_target="tpu_custom_call" | custom-call | tf_op jit(solution)/shard_map/pallas_call | solution.py:140
  34.5 12.5 %shard_map.83 = f32[1024,512]{1,0:T(8,128)} custom-call(s32[128]{0:T(128)} %reduce_max.36.busy_ref, s32[4096]{0:T(1024)} %bitcast.130, s32[4096]{0:T(1024)} %bitcast.129, f32[12288]{0:T(1024)} %mul.238.coef_ref, f32[2048,384]{1,0:T(8,128)} %bitcast.111), custom_call_target="tpu_custom_call" | custom-call | tf_op jit(solution)/shard_map/pallas_call | solution.py:60
  47.0 3.8 %fusion.134 = f32[1024,128]{1,0:T(8,128)} fusion(f32[1024,512]{1,0:T(8,128)} %shard_map.83, s32[128]{0:T(128)S(1)} %get-tuple-element.164, s32[128]{0:T(128)S(1)} %get-tuple-element.165, s32[512]{0:T(512)S(1)} %get-tuple-element.155, s32[512]{0:T(512)S(1)} %get-tuple-element.157, s32[128]{0:T(128)S(1)} %get-tuple-element.163, ...), kind=kOutput, calls=%fused_computation.230 | convolution fusion | flops 805765120 | bytes 2632960 | tf_op jit(solution)/shard_map/dot_general | solution.py:173
  50.8 19.1 %all-to-all-start = ((f32[256,4,128]{2,1,0:T(4,128)}), f32[256,4,128]{2,1,0:T(4,128)S(1)}, u32[]{:S(2)}, u32[]{:S(2)}) async-start(f32[256,4,128]{2,1,0:T(4,128)} %bitcast.15), calls=%async_computation | async-start | bytes 1048576 | tf_op jit(solution)/shard_map/all_to_all | solution.py:202
  71.4 19.7 %all-to-all-done = f32[256,4,128]{2,1,0:T(4,128)S(1)} async-done(((f32[256,4,128]{2,1,0:T(4,128)}), f32[256,4,128]{2,1,0:T(4,128)S(1)}, u32[]{:S(2)}, u32[]{:S(2)}) %all-to-all-start) | async-done | bytes 524320 | tf_op jit(solution)/shard_map/all_to_all | solution.py:202
  91.4 0.9 broadcast_in_dim.70
  92.2 5.3 %all-to-all-start.1 = ((f32[256,4,128]{2,1,0:T(4,128)}), f32[256,4,128]{2,1,0:T(4,128)S(1)}, u32[]{:S(2)}, u32[]{:S(2)}) async-start(f32[256,4,128]{2,1,0:T(4,128)} %broadcast_in_dim.70), calls=%async_computation.1 | async-start | bytes 1048576 | tf_op jit(solution)/shard_map/all_to_all | solution.py:205
  100.4 0.7 reduce_max.38.busy_ref
  101.2 0.6 mul.256.coef_ref
  101.8 11.3 %shard_map.84 = f32[1024,512]{1,0:T(8,128)} custom-call(s32[128]{0:T(128)} %reduce_max.38.busy_ref, s32[4096]{0:T(1024)} %bitcast.128, s32[4096]{0:T(1024)} %bitcast.127, f32[12288]{0:T(1024)} %mul.256.coef_ref, f32[2048,384]{1,0:T(8,128)} %bitcast.112), custom_call_target="tpu_custom_call" | custom-call | tf_op jit(solution)/shard_map/pallas_call | solution.py:60
  113.1 3.0 %fusion.132 = f32[1024,128]{1,0:T(8,128)S(1)} fusion(f32[1024,512]{1,0:T(8,128)} %shard_map.84, s32[128]{0:T(128)S(1)} %get-tuple-element.164, s32[128]{0:T(128)S(1)} %get-tuple-element.165, s32[512]{0:T(512)S(1)} %get-tuple-element.155, s32[512]{0:T(512)S(1)} %get-tuple-element.157, s32[128]{0:T(128)S(1)} %get-tuple-element.163, ...), kind=kOutput, calls=%fused_computation.229 | convolution fusion | flops 805765120 | bytes 2632960 | tf_op jit(solution)/shard_map/dot_general | solution.py:173
  116.2 2.2 %all-to-all-done.1 = f32[256,4,128]{2,1,0:T(4,128)S(1)} async-done(((f32[256,4,128]{2,1,0:T(4,128)}), f32[256,4,128]{2,1,0:T(4,128)S(1)}, u32[]{:S(2)}, u32[]{:S(2)}) %all-to-all-start.1) | async-done | bytes 524320 | tf_op jit(solution)/shard_map/all_to_all | solution.py:205
  118.4 0.8 multiply_reduce_fusion.1
  119.2 1.1 fusion.10
  120.3 0.6 reduce_max.37
  121.6 0.6 broadcast_divide_fusion.1
  122.3 2.2 %while.26 = (s32[]{:T(128)}, f32[32,32]{0,1:T(8,128)S(1)}, f32[32,32]{1,0:T(8,128)S(1)}, s32[]{:T(128)}) while((s32[]{:T(128)}, f32[32,32]{0,1:T(8,128)S(1)}, f32[32,32]{1,0:T(8,128)S(1)}, s32[]{:T(128)}) %tuple.87), condition=%wide.region_5.6_spmd.clone, body=%wide.region_4.5_spmd.clone.sunk | while | flops 1183746 | bytes 53301 | solution.py:266
  124.6 0.9 convolution_divide_fusion.1
  126.1 0.6 fusion.6
  127.1 40.0 %all_to_all.33 = f32[256,4,128]{2,1,0:T(4,128)S(1)} all-to-all(f32[256,4,128]{2,1,0:T(4,128)S(1)} %copy.98), channel_id=1, replica_groups=mesh['gx'=32,'gy'=8] {'gx','gy'}, dimensions={0} | all-to-all | bytes 1048576 | tf_op jit(solution)/shard_map/all_to_all | solution.py:202
  167.3 0.9 broadcast_in_dim.78
  168.2 5.4 %all-to-all-start.3 = ((f32[256,4,128]{2,1,0:T(4,128)}), f32[256,4,128]{2,1,0:T(4,128)S(1)}, u32[]{:S(2)}, u32[]{:S(2)}) async-start(f32[256,4,128]{2,1,0:T(4,128)} %broadcast_in_dim.78), calls=%async_computation.3 | async-start | bytes 1048576 | tf_op jit(solution)/shard_map/all_to_all | solution.py:205
  177.6 16.8 %all-to-all-done.3 = f32[256,4,128]{2,1,0:T(4,128)S(1)} async-done(((f32[256,4,128]{2,1,0:T(4,128)}), f32[256,4,128]{2,1,0:T(4,128)S(1)}, u32[]{:S(2)}, u32[]{:S(2)}) %all-to-all-start.3) | async-done | bytes 524320 | tf_op jit(solution)/shard_map/all_to_all | solution.py:205
  194.4 0.8 multiply_reduce_fusion
  195.1 1.1 fusion.8
  196.3 0.6 reduce_max.39
  197.6 0.6 broadcast_divide_fusion
  198.3 2.2 %while.27 = (s32[]{:T(128)}, f32[32,32]{0,1:T(8,128)S(1)}, f32[32,32]{1,0:T(8,128)S(1)}, s32[]{:T(128)}) while((s32[]{:T(128)}, f32[32,32]{0,1:T(8,128)S(1)}, f32[32,32]{1,0:T(8,128)S(1)}, s32[]{:T(128)}) %tuple.86), condition=%wide.region_12.13_spmd.clone, body=%wide.region_11.12_spmd.clone.sunk | while | flops 1183746 | bytes 53301 | solution.py:266
  200.5 0.9 convolution_divide_fusion
  202.1 0.8 mul.274.mix_ref
  202.9 5.9 %shard_map.85 = f32[2048,384]{1,0:T(8,128)} custom-call(f32[2048,384]{1,0:T(8,128)} %bitcast.113, f32[128,128]{1,0:T(8,128)} %mul.274.mix_ref), custom_call_target="tpu_custom_call" | custom-call | tf_op jit(solution)/shard_map/pallas_call | solution.py:187
  (142 shorter events, 16.2 us)
Async XLA Ops:
  0.0 8.4 %copy-start.3 = (s32[2,4096]{1,0:T(2,128)S(1)}, s32[2,4096]{1,0:T(2,128)}, u32[]{:S(2)}) copy-start(s32[2,4096]{1,0:T(2,128)} %param.13) | copy-start | bytes 98308
  0.0 8.9 %copy-start.4 = (f32[2,3,4096]{2,0,1:T(2,128)S(1)}, f32[2,3,4096]{2,0,1:T(2,128)}, u32[]{:S(2)}) copy-start(f32[2,3,4096]{2,0,1:T(2,128)} %param.16) | copy-start | bytes 294916
  0.0 9.0 %copy-start.6 = (s32[2,4096]{1,0:T(2,128)S(1)}, s32[2,4096]{1,0:T(2,128)}, u32[]{:S(2)}) copy-start(s32[2,4096]{1,0:T(2,128)} %param.15) | copy-start | bytes 98308
  0.0 11.5 %copy-start.5 = (s32[2,4096]{1,0:T(2,128)S(1)}, s32[2,4096]{1,0:T(2,128)}, u32[]{:S(2)}) copy-start(s32[2,4096]{1,0:T(2,128)} %param.14) | copy-start | bytes 98308
  1.3 10.8 %collective-permute-start = (f32[2,64,384]{2,0,1:T(2,128)S(1)}, f32[2,64,384]{2,0,1:T(2,128)S(1)}, u32[]{:S(2)}, u32[]{:S(2)}) collective-permute-start(f32[2,64,384]{2,0,1:T(2,128)S(1)} %copy.117), channel_id=1, source_target_pairs={{0,8},{8,16},{16,24},{24,32},{32,40},{40,48},{48,56},{56,64},{64,7... | collective-permute-start | bytes 589832 | tf_op jit(solution)/shard_map/ppermute | solution.py:159
  5.9 8.3 %collective-permute-start.1 = (f32[2,64,384]{2,0,1:T(2,128)S(1)}, f32[2,64,384]{2,0,1:T(2,128)S(1)}, u32[]{:S(2)}, u32[]{:S(2)}) collective-permute-start(f32[2,64,384]{2,0,1:T(2,128)S(1)} %copy.118), channel_id=1, source_target_pairs={{8,0},{16,8},{24,16},{32,24},{40,32},{48,40},{56,48},{64,56},{72,6... | collective-permute-start | bytes 589832 | tf_op jit(solution)/shard_map/ppermute | solution.py:160
  14.2 4.2 %collective-permute-start.3 = (f32[36,2,384]{2,0,1:T(8,128)S(1)}, f32[36,2,384]{2,0,1:T(8,128)S(1)}, u32[]{:S(2)}, u32[]{:S(2)}) collective-permute-start(f32[36,2,384]{2,0,1:T(8,128)S(1)} %pad_maximum_fusion.1), channel_id=1, source_target_pairs={{1,0},{2,1},{3,2},{4,3},{5,4},{6,5},{7,6},{0,7},{9,8},{10,9},{11,1... | collective-permute-start | bytes 331784 | tf_op jit(solution)/shard_map/ppermute | solution.py:164
  16.5 5.9 %collective-permute-start.2 = (f32[36,2,384]{2,0,1:T(8,128)S(1)}, f32[36,2,384]{2,0,1:T(8,128)S(1)}, u32[]{:S(2)}, u32[]{:S(2)}) collective-permute-start(f32[36,2,384]{2,0,1:T(8,128)S(1)} %pad_maximum_fusion), channel_id=1, source_target_pairs={{0,1},{1,2},{2,3},{3,4},{4,5},{5,6},{6,7},{7,0},{8,9},{9,10},{10,1... | collective-permute-start | bytes 331784 | tf_op jit(solution)/shard_map/ppermute | solution.py:163
  50.8 40.2 %all-to-all-start = ((f32[256,4,128]{2,1,0:T(4,128)}), f32[256,4,128]{2,1,0:T(4,128)S(1)}, u32[]{:S(2)}, u32[]{:S(2)}) async-start(f32[256,4,128]{2,1,0:T(4,128)} %bitcast.15), calls=%async_computation | async-start | bytes 1048576 | tf_op jit(solution)/shard_map/all_to_all | solution.py:202
  69.9 27.7 %copy-start.9 = (s32[1,1,2,16]{3,2,1,0:T(2,128)S(1)}, s32[1,1,2,16]{3,2,1,0:T(2,128)}, u32[]{:S(2)}) copy-start(s32[1,1,2,16]{3,2,1,0:T(2,128)} %param.19) | copy-start | bytes 388
  71.2 26.9 %copy-start.7 = (f32[2,4096]{1,0:T(2,128)S(1)}, f32[2,4096]{1,0:T(2,128)}, u32[]{:S(2)}) copy-start(f32[2,4096]{1,0:T(2,128)} %param.17) | copy-start | bytes 98308
  71.2 26.9 %copy-start.8 = (f32[2,4096]{1,0:T(2,128)S(1)}, f32[2,4096]{1,0:T(2,128)}, u32[]{:S(2)}) copy-start(f32[2,4096]{1,0:T(2,128)} %param.18) | copy-start | bytes 98308
  92.2 26.2 %all-to-all-start.1 = ((f32[256,4,128]{2,1,0:T(4,128)}), f32[256,4,128]{2,1,0:T(4,128)S(1)}, u32[]{:S(2)}, u32[]{:S(2)}) async-start(f32[256,4,128]{2,1,0:T(4,128)} %broadcast_in_dim.70), calls=%async_computation.1 | async-start | bytes 1048576 | tf_op jit(solution)/shard_map/all_to_all | solution.py:205
  100.4 12.8 %copy-start = (f32[32,32]{1,0:T(8,128)}, f32[32,32]{1,0:T(8,128)S(1)}, u32[]{:S(2)}) copy-start(f32[32,32]{1,0:T(8,128)S(1)} %copy.92) | copy-start | bytes 12292
  119.2 3.1 %copy-start.2 = (f32[32,32]{1,0:T(8,128)S(1)}, f32[32,32]{1,0:T(8,128)}, u32[]{:S(2)}) copy-start(f32[32,32]{1,0:T(8,128)} %copy-done) | copy-start | bytes 12292
  168.2 26.2 %all-to-all-start.3 = ((f32[256,4,128]{2,1,0:T(4,128)}), f32[256,4,128]{2,1,0:T(4,128)S(1)}, u32[]{:S(2)}, u32[]{:S(2)}) async-start(f32[256,4,128]{2,1,0:T(4,128)} %broadcast_in_dim.78), calls=%async_computation.3 | async-start | bytes 1048576 | tf_op jit(solution)/shard_map/all_to_all | solution.py:205
  195.1 3.1 %copy-start.1 = (f32[32,32]{1,0:T(8,128)S(1)}, f32[32,32]{1,0:T(8,128)}, u32[]{:S(2)}) copy-start(f32[32,32]{1,0:T(8,128)} %copy-done) | copy-start | bytes 12292

commit v8 on v7

--- a/solution.py
+++ b/solution.py
@@ -18,32 +18,38 @@
 radius_share = 0.25
 
 
-def gather_kernel(busy_ref, cell_ref, level_ref, coef_ref, field_ref, out_ref):
+def gather_kernel(busy_ref, row_busy_ref, cell_ref, level_ref, coef_ref, field_ref, out_ref, stage_ref):
     count = cell_ref.shape[0]
     width = field_ref.shape[1] // 3
     lane_level = lax.broadcasted_iota(jnp.int32, (1, width), 1) // ENS
-    sublane = lax.broadcasted_iota(jnp.int32, (8, width), 0)
     groups = width // ENS
     out_ref[...] = jnp.zeros(out_ref.shape, out_ref.dtype)
 
     def body(block, carry):
         @pl.when(busy_ref[block] > 0)
         def _():
-            gathered = [jnp.zeros((8, width), jnp.float32) for k in range(groups)]
             for i in range(8):
-                for k in range(groups):
-                    j = (block * 8 + i) * groups + k
-                    picked = field_ref[pl.ds(cell_ref[j], 1), :]
-                    value = (
-                        coef_ref[j] * picked[:, 0:width]
-                        + coef_ref[count + j] * picked[:, width:2 * width]
-                        + coef_ref[2 * count + j] * picked[:, 2 * width:3 * width]
-                    )
-                    value = jnp.where(lane_level == level_ref[j], value, 0.0)
-                    gathered[k] = jnp.where(sublane == i, value, gathered[k])
-            first = pl.multiple_of(block * 8, 8)
-            for k in range(groups):
-                out_ref[pl.ds(first, 8), k * width:(k + 1) * width] = gathered[k]
+                row = block * 8 + i
+
+                @pl.when(row_busy_ref[row] > 0)
+                def _():
+                    for k in range(groups):
+                        j = row * groups + k
+                        picked = field_ref[pl.ds(cell_ref[j], 1), :]
+                        value = (
+                            coef_ref[j] * picked[:, 0:width]
+                            + coef_ref[count + j] * picked[:, width:2 * width]
+                            + coef_ref[2 * count + j] * picked[:, 2 * width:3 * width]
+                        )
+                        stage_ref[i:i + 1, k * width:(k + 1) * width] = jnp.where(
+                            lane_level == level_ref[j], value, 0.0
+                        )
+
+                @pl.when(row_busy_ref[row] == 0)
+                def _():
+                    stage_ref[i:i + 1, :] = jnp.zeros((1, groups * width), jnp.float32)
+
+            out_ref[pl.ds(pl.multiple_of(block * 8, 8), 8), :] = stage_ref[...]
 
         return carry
 
@@ -54,15 +60,17 @@
     count = cells.shape[0]
     width = field.shape[1] // 3
     groups = width // ENS
-    busy = jnp.max(flags.reshape(-1, 8 * groups), axis=1)
+    row_busy = jnp.max(flags.reshape(-1, groups), axis=1)
+    busy = jnp.max(row_busy.reshape(-1, 8), axis=1)
     smem = pl.BlockSpec(memory_space=pltpu.SMEM)
     vmem = pl.BlockSpec(memory_space=pltpu.VMEM)
     return pl.pallas_call(
         gather_kernel,
         out_shape=jax.ShapeDtypeStruct((count // groups, groups * width), jnp.float32),
-        in_specs=[smem, smem, smem, smem, vmem],
+        in_specs=[smem, smem, smem, smem, smem, vmem],
         out_specs=vmem,
-    )(busy, cells, levels, coefs.reshape(-1), field)
+        scratch_shapes=[pltpu.VMEM((8, groups * width), jnp.float32)],
+    )(busy, row_busy, cells, levels, coefs.reshape(-1), field)
 
 
 def advect_update(c, w, e, s, n, width):

time: 207 us -> 219 us (1.058)
  starting transfers between devices: 36.7 us -> 47.5 us
  Pallas kernels: 39.8 us -> 29.8 us
  blocking collectives: 40 us -> 47.1 us
  waiting for transfers between devices: 45.1 us -> 47.7 us
    all_to_all x1, starting transfers between devices: 19.1 us -> 29.2 us  [summed_everywhere(): parts = lax.all_to_all(rows, axes, 0, 0, tiled=True)]
    pallas_call x2, Pallas kernels: 23.8 us -> 13.7 us  [gather_rows(): pl.pallas_call(gather_kernel, out_shape=jax.ShapeDtypeStruct((count // gr...]
    all_to_all x1, blocking collectives: 40 us -> 47.1 us  [summed_everywhere(): parts = lax.all_to_all(rows, axes, 0, 0, tiled=True)]
    all_to_all x2, waiting for transfers between devices: 19 us -> 22.4 us  [summed_everywhere(): return lax.all_to_all(copies, axes, 0, 0, tiled=True)]
  transfers between devices with their start and end apart: 7 -> 7, of which waited for: 6 -> 6; matrix products, arithmetic and copies ran while one was open for 10% -> 10% of each run, Pallas kernels for 5% -> 3%
where the time goes in v8:
time: 219 us; the launch traced here: 221 us
  waiting for transfers between devices  47.7 us (22%)
  starting transfers between devices  47.5 us (22%)
  blocking collectives  47.1 us (22%)
  Pallas kernels  29.8 us (14%)
  local copies, waits for them, and re-layouts  20.7 us (9%)
  matrix products  17.9 us (8%)
  other arithmetic  7.56 us (3%)
    all_to_all x1, blocking collectives, summed_everywhere(): parts = lax.all_to_all(rows, axes, 0, 0, tiled=True)  47.1 us
    all_to_all x1, starting transfers between devices, summed_everywhere(): parts = lax.all_to_all(rows, axes, 0, 0, tiled=True)  29.2 us
    all_to_all x2, waiting for transfers between devices, summed_everywhere(): return lax.all_to_all(copies, axes, 0, 0, tiled=True)  22.4 us
    all_to_all x1, waiting for transfers between devices, summed_everywhere(): parts = lax.all_to_all(rows, axes, 0, 0, tiled=True)  19.7 us
    dot_general x38, matrix products, product(): jnp.dot(left, right, precision=lax.Precision.HIGHEST, preferred_element_t...  17.9 us
    pallas_call x2, Pallas kernels, gather_rows(): pl.pallas_call(gather_kernel, out_shape=jax.ShapeDtypeStruct((count // gr...  13.7 us
    all_to_all x2, starting transfers between devices, summed_everywhere(): return lax.all_to_all(copies, axes, 0, 0, tiled=True)  10.7 us
    pallas_call x1, Pallas kernels, two_steps(): pl.pallas_call(two_steps_kernel, out_shape=jax.ShapeDtypeStruct(field.sha...  10.2 us
  transfers between devices with their start and end apart: 7, of which 6 were waited for; matrix products, arithmetic and copies ran while one was open for 10% of the time, Pallas kernels for 3%

profile of v8, /device:TPU:1, one launch (start us, length us, event | category | flops | bytes accessed | tf_op | source)
XLA Modules:
  0.0 220.7 jit_solution(9134222017668692315)
XLA Ops:
  0.0 1.1 fusion.138
  1.3 4.5 %collective-permute-start = (f32[2,64,384]{2,0,1:T(2,128)S(1)}, f32[2,64,384]{2,0,1:T(2,128)S(1)}, u32[]{:S(2)}, u32[]{:S(2)}) collective-permute-start(f32[2,64,384]{2,0,1:T(2,128)S(1)} %copy.117), channel_id=1, source_target_pairs={{0,8},{8,16},{16,24},{24,32},{32,40},{40,48},{48,56},{56,64},{64,7... | collective-permute-start | bytes 589832 | tf_op jit(solution)/shard_map/ppermute | solution.py:167
  6.0 1.2 fusion.137
  7.2 1.2 fusion.136
  9.6 0.6 reduce_max.55.busy_ref
  10.4 0.6 fusion.143
  11.0 0.6 copy_bitcast_fusion
  11.7 0.6 mul.238.coef_ref
  12.3 0.6 slice_reduce_fusion.6
  12.9 1.2 collective-permute-done.1
  14.2 2.9 %collective-permute-start.3 = (f32[36,2,384]{2,0,1:T(8,128)S(1)}, f32[36,2,384]{2,0,1:T(8,128)S(1)}, u32[]{:S(2)}, u32[]{:S(2)}) collective-permute-start(f32[36,2,384]{2,0,1:T(8,128)S(1)} %pad_maximum_fusion.1), channel_id=1, source_target_pairs={{1,0},{2,1},{3,2},{4,3},{5,4},{6,5},{7,6},{0,7},{9,8},{10,9},{11,1... | collective-permute-start | bytes 331784 | tf_op jit(solution)/shard_map/ppermute | solution.py:172
  17.2 0.7 copy.79.west_ref
  17.9 0.7 copy.80.east_ref
  19.0 4.1 %collective-permute-done.2 = f32[36,2,384]{2,0,1:T(8,128)S(1)} collective-permute-done((f32[36,2,384]{2,0,1:T(8,128)S(1)}, f32[36,2,384]{2,0,1:T(8,128)S(1)}, u32[]{:S(2)}, u32[]{:S(2)}) %collective-permute-start.2) | collective-permute-done | bytes 110624 | tf_op jit(solution)/shard_map/ppermute | solution.py:171
  23.1 0.6 pad_maximum_fusion.2.corner_ref
  23.7 0.6 slice_bitcast_fusion
  24.3 0.6 slice_bitcast_fusion.2
  25.0 10.2 %shard_map.82 = f32[32,64,384]{2,1,0:T(8,128)} custom-call(f32[32,64,384]{2,1,0:T(8,128)} %field_ref.1, f32[2,64,384]{2,1,0:T(8,128)} %copy.79.west_ref, f32[2,64,384]{2,1,0:T(8,128)} %copy.80.east_ref, f32[32,384]{1,0:T(8,128)} %get-tuple-element.134.south0_ref, f32[32,384]{1,0:T(8,128)} %get-tuple-element.133.south1_ref, ...), custom_call_target="tpu_custom_call" | custom-call | tf_op jit(solution)/shard_map/pallas_call | solution.py:148
  35.1 6.5 %shard_map.83 = f32[1024,512]{1,0:T(8,128)} custom-call(s32[128]{0:T(128)} %reduce_max.55.busy_ref, s32[1024]{0:T(1024)} %copy-done.5, s32[4096]{0:T(1024)} %bitcast.130, s32[4096]{0:T(1024)} %bitcast.129, f32[12288]{0:T(1024)} %mul.238.coef_ref, f32[2048,384]{1,0:T(8,128)} %bitcast.111), custom_call_target="tpu_custom_call" | custom-call | tf_op jit(solution)/shard_map/pallas_call | solution.py:67
  41.7 3.8 %fusion.134 = f32[1024,128]{1,0:T(8,128)} fusion(f32[1024,512]{1,0:T(8,128)} %shard_map.83, s32[128]{0:T(128)S(1)} %get-tuple-element.164, s32[128]{0:T(128)S(1)} %get-tuple-element.165, s32[512]{0:T(512)S(1)} %get-tuple-element.155, s32[512]{0:T(512)S(1)} %get-tuple-element.157, s32[128]{0:T(128)S(1)} %get-tuple-element.163, ...), kind=kOutput, calls=%fused_computation.230 | convolution fusion | flops 805765120 | bytes 2632960 | tf_op jit(solution)/shard_map/dot_general | solution.py:181
  45.5 29.2 %all-to-all-start = ((f32[256,4,128]{2,1,0:T(4,128)}), f32[256,4,128]{2,1,0:T(4,128)S(1)}, u32[]{:S(2)}, u32[]{:S(2)}) async-start(f32[256,4,128]{2,1,0:T(4,128)} %bitcast.15), calls=%async_computation | async-start | bytes 1048576 | tf_op jit(solution)/shard_map/all_to_all | solution.py:210
  76.3 19.7 %all-to-all-done = f32[256,4,128]{2,1,0:T(4,128)S(1)} async-done(((f32[256,4,128]{2,1,0:T(4,128)}), f32[256,4,128]{2,1,0:T(4,128)S(1)}, u32[]{:S(2)}, u32[]{:S(2)}) %all-to-all-start) | async-done | bytes 524320 | tf_op jit(solution)/shard_map/all_to_all | solution.py:210
  96.2 0.9 broadcast_in_dim.70
  97.1 5.3 %all-to-all-start.1 = ((f32[256,4,128]{2,1,0:T(4,128)}), f32[256,4,128]{2,1,0:T(4,128)S(1)}, u32[]{:S(2)}, u32[]{:S(2)}) async-start(f32[256,4,128]{2,1,0:T(4,128)} %broadcast_in_dim.70), calls=%async_computation.1 | async-start | bytes 1048576 | tf_op jit(solution)/shard_map/all_to_all | solution.py:213
  106.1 0.6 reduce_max.58.busy_ref
  106.8 0.6 mul.256.coef_ref
  107.4 7.2 %shard_map.84 = f32[1024,512]{1,0:T(8,128)} custom-call(s32[128]{0:T(128)} %reduce_max.58.busy_ref, s32[1024]{0:T(1024)} %copy-done.6, s32[4096]{0:T(1024)} %bitcast.128, s32[4096]{0:T(1024)} %bitcast.127, f32[12288]{0:T(1024)} %mul.256.coef_ref, f32[2048,384]{1,0:T(8,128)} %bitcast.112), custom_call_target="tpu_custom_call" | custom-call | tf_op jit(solution)/shard_map/pallas_call | solution.py:67
  114.6 3.0 %fusion.132 = f32[1024,128]{1,0:T(8,128)S(1)} fusion(f32[1024,512]{1,0:T(8,128)} %shard_map.84, s32[128]{0:T(128)S(1)} %get-tuple-element.164, s32[128]{0:T(128)S(1)} %get-tuple-element.165, s32[512]{0:T(512)S(1)} %get-tuple-element.155, s32[512]{0:T(512)S(1)} %get-tuple-element.157, s32[128]{0:T(128)S(1)} %get-tuple-element.163, ...), kind=kOutput, calls=%fused_computation.229 | convolution fusion | flops 805765120 | bytes 2632960 | tf_op jit(solution)/shard_map/dot_general | solution.py:181
  117.6 5.6 %all-to-all-done.1 = f32[256,4,128]{2,1,0:T(4,128)S(1)} async-done(((f32[256,4,128]{2,1,0:T(4,128)}), f32[256,4,128]{2,1,0:T(4,128)S(1)}, u32[]{:S(2)}, u32[]{:S(2)}) %all-to-all-start.1) | async-done | bytes 524320 | tf_op jit(solution)/shard_map/all_to_all | solution.py:213
  123.2 0.8 multiply_reduce_fusion.1
  124.0 1.1 fusion.10
  125.2 0.6 reduce_max.56
  126.5 0.6 broadcast_divide_fusion.1
  127.2 2.2 %while.26 = (s32[]{:T(128)}, f32[32,32]{0,1:T(8,128)S(1)}, f32[32,32]{1,0:T(8,128)S(1)}, s32[]{:T(128)}) while((s32[]{:T(128)}, f32[32,32]{0,1:T(8,128)S(1)}, f32[32,32]{1,0:T(8,128)S(1)}, s32[]{:T(128)}) %tuple.87), condition=%wide.region_6.7_spmd.clone, body=%wide.region_5.6_spmd.clone.sunk | while | flops 1183746 | bytes 53301 | solution.py:274
  129.4 0.9 convolution_divide_fusion.1
  131.0 0.6 fusion.6
  131.9 47.1 %all_to_all.33 = f32[256,4,128]{2,1,0:T(4,128)S(1)} all-to-all(f32[256,4,128]{2,1,0:T(4,128)S(1)} %copy.98), channel_id=1, replica_groups=mesh['gx'=32,'gy'=8] {'gx','gy'}, dimensions={0} | all-to-all | bytes 1048576 | tf_op jit(solution)/shard_map/all_to_all | solution.py:210
  179.3 0.9 broadcast_in_dim.78
  180.2 5.4 %all-to-all-start.3 = ((f32[256,4,128]{2,1,0:T(4,128)}), f32[256,4,128]{2,1,0:T(4,128)S(1)}, u32[]{:S(2)}, u32[]{:S(2)}) async-start(f32[256,4,128]{2,1,0:T(4,128)} %broadcast_in_dim.78), calls=%async_computation.3 | async-start | bytes 1048576 | tf_op jit(solution)/shard_map/all_to_all | solution.py:213
  189.6 16.8 %all-to-all-done.3 = f32[256,4,128]{2,1,0:T(4,128)S(1)} async-done(((f32[256,4,128]{2,1,0:T(4,128)}), f32[256,4,128]{2,1,0:T(4,128)S(1)}, u32[]{:S(2)}, u32[]{:S(2)}) %all-to-all-start.3) | async-done | bytes 524320 | tf_op jit(solution)/shard_map/all_to_all | solution.py:213
  206.4 0.8 multiply_reduce_fusion
  207.1 1.1 fusion.8
  208.3 0.6 reduce_max.59
  209.6 0.6 broadcast_divide_fusion
  210.3 2.2 %while.27 = (s32[]{:T(128)}, f32[32,32]{0,1:T(8,128)S(1)}, f32[32,32]{1,0:T(8,128)S(1)}, s32[]{:T(128)}) while((s32[]{:T(128)}, f32[32,32]{0,1:T(8,128)S(1)}, f32[32,32]{1,0:T(8,128)S(1)}, s32[]{:T(128)}) %tuple.86), condition=%wide.region_14.15_spmd.clone, body=%wide.region_13.14_spmd.clone.sunk | while | flops 1183746 | bytes 53301 | solution.py:274
  212.5 0.9 convolution_divide_fusion
  214.1 0.8 mul.274.mix_ref
  214.9 5.9 %shard_map.85 = f32[2048,384]{1,0:T(8,128)} custom-call(f32[2048,384]{1,0:T(8,128)} %bitcast.113, f32[128,128]{1,0:T(8,128)} %mul.274.mix_ref), custom_call_target="tpu_custom_call" | custom-call | tf_op jit(solution)/shard_map/pallas_call | solution.py:195
  (150 shorter events, 17.7 us)
Async XLA Ops:
  0.0 8.4 %copy-start.3 = (s32[2,4096]{1,0:T(2,128)S(1)}, s32[2,4096]{1,0:T(2,128)}, u32[]{:S(2)}) copy-start(s32[2,4096]{1,0:T(2,128)} %param.13) | copy-start | bytes 98308
  0.0 10.3 %copy-start.4 = (f32[2,3,4096]{2,0,1:T(2,128)S(1)}, f32[2,3,4096]{2,0,1:T(2,128)}, u32[]{:S(2)}) copy-start(f32[2,3,4096]{2,0,1:T(2,128)} %param.16) | copy-start | bytes 294916
  0.0 10.4 %copy-start.8 = (s32[2,4096]{1,0:T(2,128)S(1)}, s32[2,4096]{1,0:T(2,128)}, u32[]{:S(2)}) copy-start(s32[2,4096]{1,0:T(2,128)} %param.15) | copy-start | bytes 98308
  1.1 11.2 %copy-start.7 = (s32[2,4096]{1,0:T(2,128)S(1)}, s32[2,4096]{1,0:T(2,128)}, u32[]{:S(2)}) copy-start(s32[2,4096]{1,0:T(2,128)} %param.14) | copy-start | bytes 98308
  1.3 11.7 %collective-permute-start = (f32[2,64,384]{2,0,1:T(2,128)S(1)}, f32[2,64,384]{2,0,1:T(2,128)S(1)}, u32[]{:S(2)}, u32[]{:S(2)}) collective-permute-start(f32[2,64,384]{2,0,1:T(2,128)S(1)} %copy.117), channel_id=1, source_target_pairs={{0,8},{8,16},{16,24},{24,32},{32,40},{40,48},{48,56},{56,64},{64,7... | collective-permute-start | bytes 589832 | tf_op jit(solution)/shard_map/ppermute | solution.py:167
  5.9 8.3 %collective-permute-start.1 = (f32[2,64,384]{2,0,1:T(2,128)S(1)}, f32[2,64,384]{2,0,1:T(2,128)S(1)}, u32[]{:S(2)}, u32[]{:S(2)}) collective-permute-start(f32[2,64,384]{2,0,1:T(2,128)S(1)} %copy.118), channel_id=1, source_target_pairs={{8,0},{16,8},{24,16},{32,24},{40,32},{48,40},{56,48},{64,56},{72,6... | collective-permute-start | bytes 589832 | tf_op jit(solution)/shard_map/ppermute | solution.py:168
  9.5 25.7 %copy-start.5 = (s32[1024]{0:T(1024)}, s32[1024]{0:T(1024)S(1)}, u32[]{:S(2)}) copy-start(s32[1024]{0:T(1024)S(1)} %reduce_max.54.row_busy_ref) | copy-start | bytes 12292
  14.2 4.8 %collective-permute-start.3 = (f32[36,2,384]{2,0,1:T(8,128)S(1)}, f32[36,2,384]{2,0,1:T(8,128)S(1)}, u32[]{:S(2)}, u32[]{:S(2)}) collective-permute-start(f32[36,2,384]{2,0,1:T(8,128)S(1)} %pad_maximum_fusion.1), channel_id=1, source_target_pairs={{1,0},{2,1},{3,2},{4,3},{5,4},{6,5},{7,6},{0,7},{9,8},{10,9},{11,1... | collective-permute-start | bytes 331784 | tf_op jit(solution)/shard_map/ppermute | solution.py:172
  17.2 5.9 %collective-permute-start.2 = (f32[36,2,384]{2,0,1:T(8,128)S(1)}, f32[36,2,384]{2,0,1:T(8,128)S(1)}, u32[]{:S(2)}, u32[]{:S(2)}) collective-permute-start(f32[36,2,384]{2,0,1:T(8,128)S(1)} %pad_maximum_fusion), channel_id=1, source_target_pairs={{0,1},{1,2},{2,3},{3,4},{4,5},{5,6},{6,7},{7,0},{8,9},{9,10},{10,1... | collective-permute-start | bytes 331784 | tf_op jit(solution)/shard_map/ppermute | solution.py:171
  45.5 50.4 %all-to-all-start = ((f32[256,4,128]{2,1,0:T(4,128)}), f32[256,4,128]{2,1,0:T(4,128)S(1)}, u32[]{:S(2)}, u32[]{:S(2)}) async-start(f32[256,4,128]{2,1,0:T(4,128)} %bitcast.15), calls=%async_computation | async-start | bytes 1048576 | tf_op jit(solution)/shard_map/all_to_all | solution.py:210
  74.8 27.7 %copy-start.11 = (s32[1,1,2,16]{3,2,1,0:T(2,128)S(1)}, s32[1,1,2,16]{3,2,1,0:T(2,128)}, u32[]{:S(2)}) copy-start(s32[1,1,2,16]{3,2,1,0:T(2,128)} %param.19) | copy-start | bytes 388
  76.0 26.9 %copy-start.9 = (f32[2,4096]{1,0:T(2,128)S(1)}, f32[2,4096]{1,0:T(2,128)}, u32[]{:S(2)}) copy-start(f32[2,4096]{1,0:T(2,128)} %param.17) | copy-start | bytes 98308
  76.1 26.9 %copy-start.10 = (f32[2,4096]{1,0:T(2,128)S(1)}, f32[2,4096]{1,0:T(2,128)}, u32[]{:S(2)}) copy-start(f32[2,4096]{1,0:T(2,128)} %param.18) | copy-start | bytes 98308
  97.1 26.2 %all-to-all-start.1 = ((f32[256,4,128]{2,1,0:T(4,128)}), f32[256,4,128]{2,1,0:T(4,128)S(1)}, u32[]{:S(2)}, u32[]{:S(2)}) async-start(f32[256,4,128]{2,1,0:T(4,128)} %broadcast_in_dim.70), calls=%async_computation.1 | async-start | bytes 1048576 | tf_op jit(solution)/shard_map/all_to_all | solution.py:213
  105.2 9.4 %copy-start = (f32[32,32]{1,0:T(8,128)}, f32[32,32]{1,0:T(8,128)S(1)}, u32[]{:S(2)}) copy-start(f32[32,32]{1,0:T(8,128)S(1)} %copy.92) | copy-start | bytes 12292
  106.0 1.4 copy-start.6
  124.0 3.1 %copy-start.2 = (f32[32,32]{1,0:T(8,128)S(1)}, f32[32,32]{1,0:T(8,128)}, u32[]{:S(2)}) copy-start(f32[32,32]{1,0:T(8,128)} %copy-done) | copy-start | bytes 12292
  180.2 26.2 %all-to-all-start.3 = ((f32[256,4,128]{2,1,0:T(4,128)}), f32[256,4,128]{2,1,0:T(4,128)S(1)}, u32[]{:S(2)}, u32[]{:S(2)}) async-start(f32[256,4,128]{2,1,0:T(4,128)} %broadcast_in_dim.78), calls=%async_computation.3 | async-start | bytes 1048576 | tf_op jit(solution)/shard_map/all_to_all | solution.py:213
  207.1 3.1 %copy-start.1 = (f32[32,32]{1,0:T(8,128)S(1)}, f32[32,32]{1,0:T(8,128)}, u32[]{:S(2)}) copy-start(f32[32,32]{1,0:T(8,128)} %copy-done) | copy-start | bytes 12292

commit v9 on v7

--- a/solution.py
+++ b/solution.py
@@ -18,13 +18,13 @@
 radius_share = 0.25
 
 
-def gather_kernel(busy_ref, cell_ref, level_ref, coef_ref, field_ref, out_ref):
+def gather_kernel(busy_ref, cell_ref, level_ref, coef_ref, field_ref, fold_ref, out_ref, spread_ref):
     count = cell_ref.shape[0]
     width = field_ref.shape[1] // 3
     lane_level = lax.broadcasted_iota(jnp.int32, (1, width), 1) // ENS
     sublane = lax.broadcasted_iota(jnp.int32, (8, width), 0)
     groups = width // ENS
-    out_ref[...] = jnp.zeros(out_ref.shape, out_ref.dtype)
+    spread_ref[...] = jnp.zeros(spread_ref.shape, spread_ref.dtype)
 
     def body(block, carry):
         @pl.when(busy_ref[block] > 0)
@@ -43,14 +43,15 @@
                     gathered[k] = jnp.where(sublane == i, value, gathered[k])
             first = pl.multiple_of(block * 8, 8)
             for k in range(groups):
-                out_ref[pl.ds(first, 8), k * width:(k + 1) * width] = gathered[k]
+                spread_ref[pl.ds(first, 8), k * width:(k + 1) * width] = gathered[k]
 
         return carry
 
     lax.fori_loop(0, count // (8 * groups), body, 0)
-
-
-def gather_rows(flags, cells, levels, coefs, field):
+    out_ref[...] = product(spread_ref[...], fold_ref[...])
+
+
+def gather_rows(flags, cells, levels, coefs, field, fold):
     count = cells.shape[0]
     width = field.shape[1] // 3
     groups = width // ENS
@@ -59,10 +60,11 @@
     vmem = pl.BlockSpec(memory_space=pltpu.VMEM)
     return pl.pallas_call(
         gather_kernel,
-        out_shape=jax.ShapeDtypeStruct((count // groups, groups * width), jnp.float32),
-        in_specs=[smem, smem, smem, smem, vmem],
+        out_shape=jax.ShapeDtypeStruct((count // groups, width), jnp.float32),
+        in_specs=[smem, smem, smem, smem, vmem, vmem],
         out_specs=vmem,
-    )(busy, cells, levels, coefs.reshape(-1), field)
+        scratch_shapes=[pltpu.VMEM((count // groups, groups * width), jnp.float32)],
+    )(busy, cells, levels, coefs.reshape(-1), field, fold)
 
 
 def advect_update(c, w, e, s, n, width):
@@ -301,8 +303,9 @@
             obs_level[batch_index],
             masked_coefs,
             cells,
+            fold,
         )
-        return product(spread, fold)
+        return spread
 
     def mixing(local_terms, batch_index):
         predicted = summed_everywhere(local_terms)

time: 207 us -> 206 us (level); the launches traced: 209 us -> 204 us
  blocking collectives: 40 us -> 81.5 us
  starting transfers between devices: 36.7 us -> 19.5 us
  waiting for transfers between devices: 45.1 us -> 28.9 us
  Pallas kernels: 39.8 us -> 30.8 us
  matrix products: 17.9 us -> 11 us
  other arithmetic: 7.16 us -> 10.1 us
    all_to_all x1 -> x2, blocking collectives: 40 us -> 81.5 us  [summed_everywhere(): parts = lax.all_to_all(rows, axes, 0, 0, tiled=True)]
    all_to_all x1 -> x0, waiting for transfers between devices: 19.7 us -> none  [summed_everywhere(): parts = lax.all_to_all(rows, axes, 0, 0, tiled=True)]
    all_to_all x1 -> x0, starting transfers between devices: 19.1 us -> none  [summed_everywhere(): parts = lax.all_to_all(rows, axes, 0, 0, tiled=True)]
    pallas_call x2, Pallas kernels: 23.8 us -> 14.8 us  [gather_rows(): pl.pallas_call(gather_kernel, out_shape=jax.ShapeDtypeStruct((count // gr...]
    dot_general x38 -> x36, matrix products: 17.9 us -> 11 us  [product(): jnp.dot(left, right, precision=lax.Precision.HIGHEST, preferred_element_t...]
    all_to_all x2, waiting for transfers between devices: 19 us -> 24.5 us  [summed_everywhere(): return lax.all_to_all(copies, axes, 0, 0, tiled=True)]
  transfers between devices with their start and end apart: 7 -> 6, of which waited for: 6 -> 4; matrix products, arithmetic and copies ran while one was open for 10% -> 10% of each run, Pallas kernels for 5% -> 4%
where the time goes in v9:
time: 206 us; the launch traced here: 204 us
  blocking collectives  81.5 us (40%)
  Pallas kernels  30.8 us (15%)
  waiting for transfers between devices  28.9 us (14%)
  local copies, waits for them, and re-layouts  19.6 us (10%)
  starting transfers between devices  19.5 us (9%)
  matrix products  11 us (5%)
  other arithmetic  10.1 us (5%)
    all_to_all x2, blocking collectives, summed_everywhere(): parts = lax.all_to_all(rows, axes, 0, 0, tiled=True)  81.5 us
    all_to_all x2, waiting for transfers between devices, summed_everywhere(): return lax.all_to_all(copies, axes, 0, 0, tiled=True)  24.5 us
    pallas_call x2, Pallas kernels, gather_rows(): pl.pallas_call(gather_kernel, out_shape=jax.ShapeDtypeStruct((count // gr...  14.8 us
    dot_general x36, matrix products, product(): jnp.dot(left, right, precision=lax.Precision.HIGHEST, preferred_element_t...  11 us
    all_to_all x2, starting transfers between devices, summed_everywhere(): return lax.all_to_all(copies, axes, 0, 0, tiled=True)  10.7 us
    pallas_call x1, Pallas kernels, two_steps(): pl.pallas_call(two_steps_kernel, out_shape=jax.ShapeDtypeStruct(field.sha...  10.2 us
    pallas_call x1, Pallas kernels, mixed_once(): pl.pallas_call(mix_kernel, out_shape=jax.ShapeDtypeStruct(rows.shape, row...  5.86 us
    ppermute x1, starting transfers between devices, advance_twice(): west = lax.ppermute(field[nx - 2:], 'gx', up_x)  4.46 us
  transfers between devices with their start and end apart: 6, of which 4 were waited for; matrix products, arithmetic and copies ran while one was open for 10% of the time, Pallas kernels for 4%

profile of v9, /device:TPU:1, one launch (start us, length us, event | category | flops | bytes accessed | tf_op | source)
XLA Modules:
  0.0 203.8 jit_solution(17969687718810826215)
XLA Ops:
  0.0 1.1 fusion.135
  1.3 4.5 %collective-permute-start = (f32[2,64,384]{2,0,1:T(2,128)S(1)}, f32[2,64,384]{2,0,1:T(2,128)S(1)}, u32[]{:S(2)}, u32[]{:S(2)}) collective-permute-start(f32[2,64,384]{2,0,1:T(2,128)S(1)} %copy.117), channel_id=1, source_target_pairs={{0,8},{8,16},{16,24},{24,32},{32,40},{40,48},{48,56},{56,64},{64,7... | collective-permute-start | bytes 589832 | tf_op jit(solution)/shard_map/ppermute | solution.py:161
  6.0 1.2 fusion.134
  7.2 1.2 fusion.133
  8.4 0.8 compare_convert_fusion
  9.2 1.0 slice_reduce_fusion.1
  10.5 0.6 fusion.140
  11.2 0.6 copy_bitcast_fusion
  11.8 0.7 reduce_max.36.busy_ref
  12.5 0.6 mul.238.coef_ref
  13.1 1.2 fusion.13.fold_ref
  14.4 0.6 slice_reduce_fusion.6
  15.1 4.2 %collective-permute-start.3 = (f32[36,2,384]{2,0,1:T(8,128)S(1)}, f32[36,2,384]{2,0,1:T(8,128)S(1)}, u32[]{:S(2)}, u32[]{:S(2)}) collective-permute-start(f32[36,2,384]{2,0,1:T(8,128)S(1)} %pad_maximum_fusion.1), channel_id=1, source_target_pairs={{1,0},{2,1},{3,2},{4,3},{5,4},{6,5},{7,6},{0,7},{9,8},{10,9},{11,1... | collective-permute-start | bytes 331784 | tf_op jit(solution)/shard_map/ppermute | solution.py:166
  19.3 0.7 copy.79.west_ref
  20.0 0.7 copy.80.east_ref
  21.1 4.1 %collective-permute-done.2 = f32[36,2,384]{2,0,1:T(8,128)S(1)} collective-permute-done((f32[36,2,384]{2,0,1:T(8,128)S(1)}, f32[36,2,384]{2,0,1:T(8,128)S(1)}, u32[]{:S(2)}, u32[]{:S(2)}) %collective-permute-start.2) | collective-permute-done | bytes 110624 | tf_op jit(solution)/shard_map/ppermute | solution.py:165
  25.2 0.6 pad_maximum_fusion.2.corner_ref
  25.8 0.6 slice_bitcast_fusion
  26.4 0.6 slice_bitcast_fusion.2
  27.1 10.2 %shard_map.82 = f32[32,64,384]{2,1,0:T(8,128)} custom-call(f32[32,64,384]{2,1,0:T(8,128)} %field_ref.1, f32[2,64,384]{2,1,0:T(8,128)} %copy.79.west_ref, f32[2,64,384]{2,1,0:T(8,128)} %copy.80.east_ref, f32[32,384]{1,0:T(8,128)} %get-tuple-element.134.south0_ref, f32[32,384]{1,0:T(8,128)} %get-tuple-element.133.south1_ref, ...), custom_call_target="tpu_custom_call" | custom-call | tf_op jit(solution)/shard_map/pallas_call | solution.py:142
  37.2 7.4 %shard_map.83 = f32[1024,128]{1,0:T(8,128)} custom-call(s32[128]{0:T(128)} %reduce_max.36.busy_ref, s32[4096]{0:T(1024)} %bitcast.129, s32[4096]{0:T(1024)} %bitcast.128, f32[12288]{0:T(1024)} %mul.238.coef_ref, f32[2048,384]{1,0:T(8,128)} %bitcast.109, f32[512,128]{1,0:T(8,128)} %fusion.13.fold_ref), custom_call_target="tpu_custom_call" | custom-call | tf_op jit(solution)/shard_map/pallas_call | solution.py:61
  44.7 43.3 %all_to_all.33 = f32[256,4,128]{2,1,0:T(4,128)S(1)} all-to-all(f32[256,4,128]{2,1,0:T(4,128)} %bitcast.113), channel_id=1, replica_groups=mesh['gx'=32,'gy'=8] {'gx','gy'}, dimensions={0} | all-to-all | bytes 1048576 | tf_op jit(solution)/shard_map/all_to_all | solution.py:204
  88.2 0.9 broadcast_in_dim.70
  89.1 5.4 %all-to-all-start.1 = ((f32[256,4,128]{2,1,0:T(4,128)}), f32[256,4,128]{2,1,0:T(4,128)S(1)}, u32[]{:S(2)}, u32[]{:S(2)}) async-start(f32[256,4,128]{2,1,0:T(4,128)} %broadcast_in_dim.70), calls=%async_computation.1 | async-start | bytes 1048576 | tf_op jit(solution)/shard_map/all_to_all | solution.py:207
  98.8 0.7 reduce_max.38.busy_ref
  99.5 0.6 mul.256.coef_ref
  100.2 7.4 %shard_map.84 = f32[1024,128]{1,0:T(8,128)} custom-call(s32[128]{0:T(128)} %reduce_max.38.busy_ref, s32[4096]{0:T(1024)} %bitcast.127, s32[4096]{0:T(1024)} %bitcast.126, f32[12288]{0:T(1024)} %mul.256.coef_ref, f32[2048,384]{1,0:T(8,128)} %bitcast.110, f32[512,128]{1,0:T(8,128)} %fusion.13.fold_ref), custom_call_target="tpu_custom_call" | custom-call | tf_op jit(solution)/shard_map/pallas_call | solution.py:61
  107.6 7.7 %all-to-all-done.1 = f32[256,4,128]{2,1,0:T(4,128)S(1)} async-done(((f32[256,4,128]{2,1,0:T(4,128)}), f32[256,4,128]{2,1,0:T(4,128)S(1)}, u32[]{:S(2)}, u32[]{:S(2)}) %all-to-all-start.1) | async-done | bytes 524320 | tf_op jit(solution)/shard_map/all_to_all | solution.py:207
  115.3 0.8 multiply_reduce_fusion.1
  116.0 1.1 fusion.10
  117.2 0.6 reduce_max.37
  118.5 0.6 broadcast_divide_fusion.1
  119.2 2.2 %while.26 = (s32[]{:T(128)}, f32[32,32]{0,1:T(8,128)S(1)}, f32[32,32]{1,0:T(8,128)S(1)}, s32[]{:T(128)}) while((s32[]{:T(128)}, f32[32,32]{0,1:T(8,128)S(1)}, f32[32,32]{1,0:T(8,128)S(1)}, s32[]{:T(128)}) %tuple.87), condition=%wide.region_5.6_spmd.clone, body=%wide.region_4.5_spmd.clone.sunk | while | flops 1183746 | bytes 53301 | solution.py:268
  121.4 0.9 convolution_divide_fusion.1
  123.0 0.6 fusion.6
  123.9 38.2 %all_to_all.34 = f32[256,4,128]{2,1,0:T(4,128)S(1)} all-to-all(f32[256,4,128]{2,1,0:T(4,128)S(1)} %copy.98), channel_id=1, replica_groups=mesh['gx'=32,'gy'=8] {'gx','gy'}, dimensions={0} | all-to-all | bytes 1048576 | tf_op jit(solution)/shard_map/all_to_all | solution.py:204
  162.4 0.9 broadcast_in_dim.78
  163.3 5.4 %all-to-all-start.3 = ((f32[256,4,128]{2,1,0:T(4,128)}), f32[256,4,128]{2,1,0:T(4,128)S(1)}, u32[]{:S(2)}, u32[]{:S(2)}) async-start(f32[256,4,128]{2,1,0:T(4,128)} %broadcast_in_dim.78), calls=%async_computation.3 | async-start | bytes 1048576 | tf_op jit(solution)/shard_map/all_to_all | solution.py:207
  169.4 0.5 squeeze.67
  172.7 16.8 %all-to-all-done.3 = f32[256,4,128]{2,1,0:T(4,128)S(1)} async-done(((f32[256,4,128]{2,1,0:T(4,128)}), f32[256,4,128]{2,1,0:T(4,128)S(1)}, u32[]{:S(2)}, u32[]{:S(2)}) %all-to-all-start.3) | async-done | bytes 524320 | tf_op jit(solution)/shard_map/all_to_all | solution.py:207
  189.5 0.8 multiply_reduce_fusion
  190.2 1.1 fusion.8
  191.4 0.6 reduce_max.39
  192.7 0.6 broadcast_divide_fusion
  193.4 2.2 %while.27 = (s32[]{:T(128)}, f32[32,32]{0,1:T(8,128)S(1)}, f32[32,32]{1,0:T(8,128)S(1)}, s32[]{:T(128)}) while((s32[]{:T(128)}, f32[32,32]{0,1:T(8,128)S(1)}, f32[32,32]{1,0:T(8,128)S(1)}, s32[]{:T(128)}) %tuple.86), condition=%wide.region_12.13_spmd.clone, body=%wide.region_11.12_spmd.clone.sunk | while | flops 1183746 | bytes 53301 | solution.py:268
  195.6 0.9 convolution_divide_fusion
  197.2 0.8 mul.274.mix_ref
  198.0 5.9 %shard_map.85 = f32[2048,384]{1,0:T(8,128)} custom-call(f32[2048,384]{1,0:T(8,128)} %bitcast.111, f32[128,128]{1,0:T(8,128)} %mul.274.mix_ref), custom_call_target="tpu_custom_call" | custom-call | tf_op jit(solution)/shard_map/pallas_call | solution.py:189
  (140 shorter events, 15.5 us)
Async XLA Ops:
  0.0 10.4 %copy-start.4 = (f32[2,3,4096]{2,0,1:T(2,128)S(1)}, f32[2,3,4096]{2,0,1:T(2,128)}, u32[]{:S(2)}) copy-start(f32[2,3,4096]{2,0,1:T(2,128)} %param.16) | copy-start | bytes 294916
  0.0 10.5 %copy-start.6 = (s32[2,4096]{1,0:T(2,128)S(1)}, s32[2,4096]{1,0:T(2,128)}, u32[]{:S(2)}) copy-start(s32[2,4096]{1,0:T(2,128)} %param.15) | copy-start | bytes 98308
  0.0 14.4 %copy-start.5 = (s32[2,4096]{1,0:T(2,128)S(1)}, s32[2,4096]{1,0:T(2,128)}, u32[]{:S(2)}) copy-start(s32[2,4096]{1,0:T(2,128)} %param.14) | copy-start | bytes 98308
  1.3 13.8 %collective-permute-start = (f32[2,64,384]{2,0,1:T(2,128)S(1)}, f32[2,64,384]{2,0,1:T(2,128)S(1)}, u32[]{:S(2)}, u32[]{:S(2)}) collective-permute-start(f32[2,64,384]{2,0,1:T(2,128)S(1)} %copy.117), channel_id=1, source_target_pairs={{0,8},{8,16},{16,24},{24,32},{32,40},{40,48},{48,56},{56,64},{64,7... | collective-permute-start | bytes 589832 | tf_op jit(solution)/shard_map/ppermute | solution.py:161
  5.9 9.2 %collective-permute-start.1 = (f32[2,64,384]{2,0,1:T(2,128)S(1)}, f32[2,64,384]{2,0,1:T(2,128)S(1)}, u32[]{:S(2)}, u32[]{:S(2)}) collective-permute-start(f32[2,64,384]{2,0,1:T(2,128)S(1)} %copy.118), channel_id=1, source_target_pairs={{8,0},{16,8},{24,16},{32,24},{40,32},{48,40},{56,48},{64,56},{72,6... | collective-permute-start | bytes 589832 | tf_op jit(solution)/shard_map/ppermute | solution.py:162
  15.1 6.0 %collective-permute-start.3 = (f32[36,2,384]{2,0,1:T(8,128)S(1)}, f32[36,2,384]{2,0,1:T(8,128)S(1)}, u32[]{:S(2)}, u32[]{:S(2)}) collective-permute-start(f32[36,2,384]{2,0,1:T(8,128)S(1)} %pad_maximum_fusion.1), channel_id=1, source_target_pairs={{1,0},{2,1},{3,2},{4,3},{5,4},{6,5},{7,6},{0,7},{9,8},{10,9},{11,1... | collective-permute-start | bytes 331784 | tf_op jit(solution)/shard_map/ppermute | solution.py:166
  19.3 5.9 %collective-permute-start.2 = (f32[36,2,384]{2,0,1:T(8,128)S(1)}, f32[36,2,384]{2,0,1:T(8,128)S(1)}, u32[]{:S(2)}, u32[]{:S(2)}) collective-permute-start(f32[36,2,384]{2,0,1:T(8,128)S(1)} %pad_maximum_fusion), channel_id=1, source_target_pairs={{0,1},{1,2},{2,3},{3,4},{4,5},{5,6},{6,7},{7,0},{8,9},{9,10},{10,1... | collective-permute-start | bytes 331784 | tf_op jit(solution)/shard_map/ppermute | solution.py:165
  44.6 51.3 %copy-start.9 = (s32[1,1,2,16]{3,2,1,0:T(2,128)S(1)}, s32[1,1,2,16]{3,2,1,0:T(2,128)}, u32[]{:S(2)}) copy-start(s32[1,1,2,16]{3,2,1,0:T(2,128)} %param.19) | copy-start | bytes 388
  87.9 8.5 %copy-start.7 = (f32[2,4096]{1,0:T(2,128)S(1)}, f32[2,4096]{1,0:T(2,128)}, u32[]{:S(2)}) copy-start(f32[2,4096]{1,0:T(2,128)} %param.17) | copy-start | bytes 98308
  87.9 8.5 %copy-start.8 = (f32[2,4096]{1,0:T(2,128)S(1)}, f32[2,4096]{1,0:T(2,128)}, u32[]{:S(2)}) copy-start(f32[2,4096]{1,0:T(2,128)} %param.18) | copy-start | bytes 98308
  89.1 26.2 %all-to-all-start.1 = ((f32[256,4,128]{2,1,0:T(4,128)}), f32[256,4,128]{2,1,0:T(4,128)S(1)}, u32[]{:S(2)}, u32[]{:S(2)}) async-start(f32[256,4,128]{2,1,0:T(4,128)} %broadcast_in_dim.70), calls=%async_computation.1 | async-start | bytes 1048576 | tf_op jit(solution)/shard_map/all_to_all | solution.py:207
  98.7 17.3 %copy-start.1 = (f32[32,32]{1,0:T(8,128)}, f32[32,32]{1,0:T(8,128)S(1)}, u32[]{:S(2)}) copy-start(f32[32,32]{1,0:T(8,128)S(1)} %copy.92) | copy-start | bytes 12292
  116.0 7.0 %copy-start = (f32[1024,128]{1,0:T(8,128)S(1)}, f32[1024,128]{1,0:T(8,128)}, u32[]{:S(2)}) copy-start(f32[1024,128]{1,0:T(8,128)} %shard_map.84) | copy-start | bytes 1572868
  116.0 3.1 %copy-start.3 = (f32[32,32]{1,0:T(8,128)S(1)}, f32[32,32]{1,0:T(8,128)}, u32[]{:S(2)}) copy-start(f32[32,32]{1,0:T(8,128)} %copy-done.1) | copy-start | bytes 12292
  163.3 26.2 %all-to-all-start.3 = ((f32[256,4,128]{2,1,0:T(4,128)}), f32[256,4,128]{2,1,0:T(4,128)S(1)}, u32[]{:S(2)}, u32[]{:S(2)}) async-start(f32[256,4,128]{2,1,0:T(4,128)} %broadcast_in_dim.78), calls=%async_computation.3 | async-start | bytes 1048576 | tf_op jit(solution)/shard_map/all_to_all | solution.py:207
  189.5 3.9 %copy-start.2 = (f32[32,32]{1,0:T(8,128)S(1)}, f32[32,32]{1,0:T(8,128)}, u32[]{:S(2)}) copy-start(f32[32,32]{1,0:T(8,128)} %copy-done.1) | copy-start | bytes 12292

commit v10 on v9

--- a/solution.py
+++ b/solution.py
@@ -185,7 +185,7 @@
 def mixed_once(rows, mix):
     count, features = rows.shape
     width = mix.shape[0]
-    tile = 512
+    tile = 1024
     return pl.pallas_call(
         mix_kernel,
         out_shape=jax.ShapeDtypeStruct(rows.shape, rows.dtype),
@@ -265,7 +265,7 @@
         middle = 1.5 * unit_matrix - 0.5 * product(inverse_root, approach)
         return (product(approach, middle), product(middle, inverse_root))
 
-    approach, inverse_root = lax.fori_loop(0, NSIT, refine, (system / row_bound, unit_matrix))
+    approach, inverse_root = lax.fori_loop(0, NSIT, refine, (system / row_bound, unit_matrix), unroll=True)
     inverse = product(inverse_root, inverse_root) / row_bound
     weights = product(inverse, projection[:, None])[:, 0]
     centring = unit_matrix - 1.0 / members

time: 206 us -> 206 us (level); the launches traced: 204 us -> 209 us
  blocking collectives: 81.5 us -> 86.4 us
  matrix products: 11 us -> 13.7 us
    all_to_all x2, blocking collectives: 81.5 us -> 86.4 us  [summed_everywhere(): parts = lax.all_to_all(rows, axes, 0, 0, tiled=True)]
    dot_general x36 -> x34, matrix products: 11 us -> 13.7 us  [product(): jnp.dot(left, right, precision=lax.Precision.HIGHEST, preferred_element_t...]
where the time goes in v10:
time: 206 us; the launch traced here: 209 us
  blocking collectives  86.4 us (42%)
  Pallas kernels  30.4 us (15%)
  waiting for transfers between devices  29 us (14%)
  local copies, waits for them, and re-layouts  19.5 us (9%)
  starting transfers between devices  19.5 us (9%)
  matrix products  13.7 us (7%)
  other arithmetic  8.79 us (4%)
    all_to_all x2, blocking collectives, summed_everywhere(): parts = lax.all_to_all(rows, axes, 0, 0, tiled=True)  86.4 us
    all_to_all x2, waiting for transfers between devices, summed_everywhere(): return lax.all_to_all(copies, axes, 0, 0, tiled=True)  24.6 us
    pallas_call x2, Pallas kernels, gather_rows(): pl.pallas_call(gather_kernel, out_shape=jax.ShapeDtypeStruct((count // gr...  14.8 us
    dot_general x34, matrix products, product(): jnp.dot(left, right, precision=lax.Precision.HIGHEST, preferred_element_t...  13.7 us
    all_to_all x2, starting transfers between devices, summed_everywhere(): return lax.all_to_all(copies, axes, 0, 0, tiled=True)  10.7 us
    pallas_call x1, Pallas kernels, two_steps(): pl.pallas_call(two_steps_kernel, out_shape=jax.ShapeDtypeStruct(field.sha...  10.2 us
    pallas_call x1, Pallas kernels, mixed_once(): pl.pallas_call(mix_kernel, out_shape=jax.ShapeDtypeStruct(rows.shape, row...  5.39 us
    ppermute x1, starting transfers between devices, advance_twice(): west = lax.ppermute(field[nx - 2:], 'gx', up_x)  4.46 us
  transfers between devices with their start and end apart: 6, of which 4 were waited for; matrix products, arithmetic and copies ran while one was open for 10% of the time, Pallas kernels for 4%

profile of v10, /device:TPU:1, one launch (start us, length us, event | category | flops | bytes accessed | tf_op | source)
XLA Modules:
  0.0 209.4 jit_solution(14946372856978636842)
XLA Ops:
  0.0 1.1 fusion.136
  1.3 4.5 %collective-permute-start = (f32[2,64,384]{2,0,1:T(2,128)S(1)}, f32[2,64,384]{2,0,1:T(2,128)S(1)}, u32[]{:S(2)}, u32[]{:S(2)}) collective-permute-start(f32[2,64,384]{2,0,1:T(2,128)S(1)} %copy.145), channel_id=1, source_target_pairs={{0,8},{8,16},{16,24},{24,32},{32,40},{40,48},{48,56},{56,64},{64,7... | collective-permute-start | bytes 589832 | tf_op jit(solution)/shard_map/ppermute | solution.py:161
  6.0 1.2 fusion.135
  7.2 1.2 fusion.134
  8.4 0.8 compare_convert_fusion
  9.2 1.0 slice_reduce_fusion.1
  10.5 0.6 fusion.141
  11.2 0.6 copy_bitcast_fusion
  11.8 0.7 reduce_max.36.busy_ref
  12.5 0.6 mul.275.coef_ref
  13.1 1.2 fusion.15.fold_ref
  14.4 0.6 slice_reduce_fusion.6
  15.1 4.2 %collective-permute-start.3 = (f32[36,2,384]{2,0,1:T(8,128)S(1)}, f32[36,2,384]{2,0,1:T(8,128)S(1)}, u32[]{:S(2)}, u32[]{:S(2)}) collective-permute-start(f32[36,2,384]{2,0,1:T(8,128)S(1)} %pad_maximum_fusion.1), channel_id=1, source_target_pairs={{1,0},{2,1},{3,2},{4,3},{5,4},{6,5},{7,6},{0,7},{9,8},{10,9},{11,1... | collective-permute-start | bytes 331784 | tf_op jit(solution)/shard_map/ppermute | solution.py:166
  19.3 0.7 copy.93.west_ref
  20.0 0.7 copy.94.east_ref
  21.1 4.1 %collective-permute-done.2 = f32[36,2,384]{2,0,1:T(8,128)S(1)} collective-permute-done((f32[36,2,384]{2,0,1:T(8,128)S(1)}, f32[36,2,384]{2,0,1:T(8,128)S(1)}, u32[]{:S(2)}, u32[]{:S(2)}) %collective-permute-start.2) | collective-permute-done | bytes 110624 | tf_op jit(solution)/shard_map/ppermute | solution.py:165
  25.2 0.6 pad_maximum_fusion.2.corner_ref
  25.8 0.6 slice_bitcast_fusion
  26.4 0.6 slice_bitcast_fusion.2
  27.1 10.2 %shard_map.82 = f32[32,64,384]{2,1,0:T(8,128)} custom-call(f32[32,64,384]{2,1,0:T(8,128)} %field_ref.1, f32[2,64,384]{2,1,0:T(8,128)} %copy.93.west_ref, f32[2,64,384]{2,1,0:T(8,128)} %copy.94.east_ref, f32[32,384]{1,0:T(8,128)} %get-tuple-element.36.south0_ref, f32[32,384]{1,0:T(8,128)} %get-tuple-element.35.south1_ref, ...), custom_call_target="tpu_custom_call" | custom-call | tf_op jit(solution)/shard_map/pallas_call | solution.py:142
  37.2 7.4 %shard_map.83 = f32[1024,128]{1,0:T(8,128)} custom-call(s32[128]{0:T(128)} %reduce_max.36.busy_ref, s32[4096]{0:T(1024)} %bitcast.121, s32[4096]{0:T(1024)} %bitcast.120, f32[12288]{0:T(1024)} %mul.275.coef_ref, f32[2048,384]{1,0:T(8,128)} %bitcast.101, f32[512,128]{1,0:T(8,128)} %fusion.15.fold_ref), custom_call_target="tpu_custom_call" | custom-call | tf_op jit(solution)/shard_map/pallas_call | solution.py:61
  44.7 46.5 %all_to_all.33 = f32[256,4,128]{2,1,0:T(4,128)S(1)} all-to-all(f32[256,4,128]{2,1,0:T(4,128)} %bitcast.105), channel_id=1, replica_groups=mesh['gx'=32,'gy'=8] {'gx','gy'}, dimensions={0} | all-to-all | bytes 1048576 | tf_op jit(solution)/shard_map/all_to_all | solution.py:204
  91.4 0.9 broadcast_in_dim.70
  92.3 5.4 %all-to-all-start.1 = ((f32[256,4,128]{2,1,0:T(4,128)}), f32[256,4,128]{2,1,0:T(4,128)S(1)}, u32[]{:S(2)}, u32[]{:S(2)}) async-start(f32[256,4,128]{2,1,0:T(4,128)} %broadcast_in_dim.70), calls=%async_computation.1 | async-start | bytes 1048576 | tf_op jit(solution)/shard_map/all_to_all | solution.py:207
  98.3 0.5 squeeze.62
  101.9 0.7 reduce_max.38.busy_ref
  102.6 0.6 mul.297.coef_ref
  103.3 7.4 %shard_map.84 = f32[1024,128]{1,0:T(8,128)} custom-call(s32[128]{0:T(128)} %reduce_max.38.busy_ref, s32[4096]{0:T(1024)} %bitcast.119, s32[4096]{0:T(1024)} %bitcast.118, f32[12288]{0:T(1024)} %mul.297.coef_ref, f32[2048,384]{1,0:T(8,128)} %bitcast.102, f32[512,128]{1,0:T(8,128)} %fusion.15.fold_ref), custom_call_target="tpu_custom_call" | custom-call | tf_op jit(solution)/shard_map/pallas_call | solution.py:61
  110.7 7.8 %all-to-all-done.1 = f32[256,4,128]{2,1,0:T(4,128)S(1)} async-done(((f32[256,4,128]{2,1,0:T(4,128)}), f32[256,4,128]{2,1,0:T(4,128)S(1)}, u32[]{:S(2)}, u32[]{:S(2)}) %all-to-all-start.1) | async-done | bytes 524320 | tf_op jit(solution)/shard_map/all_to_all | solution.py:207
  118.4 0.7 multiply_reduce_fusion.1
  119.2 1.1 fusion.12
  120.4 0.6 reduce_max.37
  121.0 0.8 fusion.7
  121.8 0.9 fusion.100
  125.1 0.9 convolution_divide_fusion.1
  126.7 0.6 fusion.8
  127.7 40.0 %all_to_all.34 = f32[256,4,128]{2,1,0:T(4,128)S(1)} all-to-all(f32[256,4,128]{2,1,0:T(4,128)S(1)} %copy.115), channel_id=1, replica_groups=mesh['gx'=32,'gy'=8] {'gx','gy'}, dimensions={0} | all-to-all | bytes 1048576 | tf_op jit(solution)/shard_map/all_to_all | solution.py:204
  167.9 0.9 broadcast_in_dim.78
  168.8 5.4 %all-to-all-start.3 = ((f32[256,4,128]{2,1,0:T(4,128)}), f32[256,4,128]{2,1,0:T(4,128)S(1)}, u32[]{:S(2)}, u32[]{:S(2)}) async-start(f32[256,4,128]{2,1,0:T(4,128)} %broadcast_in_dim.78), calls=%async_computation.3 | async-start | bytes 1048576 | tf_op jit(solution)/shard_map/all_to_all | solution.py:207
  178.2 16.8 %all-to-all-done.3 = f32[256,4,128]{2,1,0:T(4,128)S(1)} async-done(((f32[256,4,128]{2,1,0:T(4,128)}), f32[256,4,128]{2,1,0:T(4,128)S(1)}, u32[]{:S(2)}, u32[]{:S(2)}) %all-to-all-start.3) | async-done | bytes 524320 | tf_op jit(solution)/shard_map/all_to_all | solution.py:207
  195.0 0.8 multiply_reduce_fusion
  195.7 1.1 fusion.10
  196.9 0.6 reduce_max.39
  197.5 0.8 fusion.3
  198.3 0.9 fusion.101
  201.7 0.9 convolution_divide_fusion
  203.2 0.8 mul.319.mix_ref
  204.0 5.4 %shard_map.85 = f32[2048,384]{1,0:T(8,128)} custom-call(f32[2048,384]{1,0:T(8,128)} %bitcast.103, f32[128,128]{1,0:T(8,128)} %mul.319.mix_ref), custom_call_target="tpu_custom_call" | custom-call | tf_op jit(solution)/shard_map/pallas_call | solution.py:189
  (110 shorter events, 14.8 us)
Async XLA Ops:
  0.0 10.4 %copy-start.1 = (f32[2,3,4096]{2,0,1:T(2,128)S(1)}, f32[2,3,4096]{2,0,1:T(2,128)}, u32[]{:S(2)}) copy-start(f32[2,3,4096]{2,0,1:T(2,128)} %param.12) | copy-start | bytes 294916
  0.0 10.5 %copy-start.3 = (s32[2,4096]{1,0:T(2,128)S(1)}, s32[2,4096]{1,0:T(2,128)}, u32[]{:S(2)}) copy-start(s32[2,4096]{1,0:T(2,128)} %param.11) | copy-start | bytes 98308
  0.0 14.4 %copy-start.2 = (s32[2,4096]{1,0:T(2,128)S(1)}, s32[2,4096]{1,0:T(2,128)}, u32[]{:S(2)}) copy-start(s32[2,4096]{1,0:T(2,128)} %param.10) | copy-start | bytes 98308
  1.3 13.8 %collective-permute-start = (f32[2,64,384]{2,0,1:T(2,128)S(1)}, f32[2,64,384]{2,0,1:T(2,128)S(1)}, u32[]{:S(2)}, u32[]{:S(2)}) collective-permute-start(f32[2,64,384]{2,0,1:T(2,128)S(1)} %copy.145), channel_id=1, source_target_pairs={{0,8},{8,16},{16,24},{24,32},{32,40},{40,48},{48,56},{56,64},{64,7... | collective-permute-start | bytes 589832 | tf_op jit(solution)/shard_map/ppermute | solution.py:161
  5.9 9.2 %collective-permute-start.1 = (f32[2,64,384]{2,0,1:T(2,128)S(1)}, f32[2,64,384]{2,0,1:T(2,128)S(1)}, u32[]{:S(2)}, u32[]{:S(2)}) collective-permute-start(f32[2,64,384]{2,0,1:T(2,128)S(1)} %copy.146), channel_id=1, source_target_pairs={{8,0},{16,8},{24,16},{32,24},{40,32},{48,40},{56,48},{64,56},{72,6... | collective-permute-start | bytes 589832 | tf_op jit(solution)/shard_map/ppermute | solution.py:162
  15.1 6.0 %collective-permute-start.3 = (f32[36,2,384]{2,0,1:T(8,128)S(1)}, f32[36,2,384]{2,0,1:T(8,128)S(1)}, u32[]{:S(2)}, u32[]{:S(2)}) collective-permute-start(f32[36,2,384]{2,0,1:T(8,128)S(1)} %pad_maximum_fusion.1), channel_id=1, source_target_pairs={{1,0},{2,1},{3,2},{4,3},{5,4},{6,5},{7,6},{0,7},{9,8},{10,9},{11,1... | collective-permute-start | bytes 331784 | tf_op jit(solution)/shard_map/ppermute | solution.py:166
  19.3 5.9 %collective-permute-start.2 = (f32[36,2,384]{2,0,1:T(8,128)S(1)}, f32[36,2,384]{2,0,1:T(8,128)S(1)}, u32[]{:S(2)}, u32[]{:S(2)}) collective-permute-start(f32[36,2,384]{2,0,1:T(8,128)S(1)} %pad_maximum_fusion), channel_id=1, source_target_pairs={{0,1},{1,2},{2,3},{3,4},{4,5},{5,6},{6,7},{7,0},{8,9},{9,10},{10,1... | collective-permute-start | bytes 331784 | tf_op jit(solution)/shard_map/ppermute | solution.py:165
  44.6 54.4 %copy-start.6 = (s32[1,1,2,16]{3,2,1,0:T(2,128)S(1)}, s32[1,1,2,16]{3,2,1,0:T(2,128)}, u32[]{:S(2)}) copy-start(s32[1,1,2,16]{3,2,1,0:T(2,128)} %param.15) | copy-start | bytes 388
  91.1 8.5 %copy-start.4 = (f32[2,4096]{1,0:T(2,128)S(1)}, f32[2,4096]{1,0:T(2,128)}, u32[]{:S(2)}) copy-start(f32[2,4096]{1,0:T(2,128)} %param.13) | copy-start | bytes 98308
  91.1 8.5 %copy-start.5 = (f32[2,4096]{1,0:T(2,128)S(1)}, f32[2,4096]{1,0:T(2,128)}, u32[]{:S(2)}) copy-start(f32[2,4096]{1,0:T(2,128)} %param.14) | copy-start | bytes 98308
  92.3 26.2 %all-to-all-start.1 = ((f32[256,4,128]{2,1,0:T(4,128)}), f32[256,4,128]{2,1,0:T(4,128)S(1)}, u32[]{:S(2)}, u32[]{:S(2)}) async-start(f32[256,4,128]{2,1,0:T(4,128)} %broadcast_in_dim.70), calls=%async_computation.1 | async-start | bytes 1048576 | tf_op jit(solution)/shard_map/all_to_all | solution.py:207
  119.2 7.5 %copy-start = (f32[1024,128]{1,0:T(8,128)S(1)}, f32[1024,128]{1,0:T(8,128)}, u32[]{:S(2)}) copy-start(f32[1024,128]{1,0:T(8,128)} %shard_map.84) | copy-start | bytes 1572868
  168.8 26.2 %all-to-all-start.3 = ((f32[256,4,128]{2,1,0:T(4,128)}), f32[256,4,128]{2,1,0:T(4,128)S(1)}, u32[]{:S(2)}, u32[]{:S(2)}) async-start(f32[256,4,128]{2,1,0:T(4,128)} %broadcast_in_dim.78), calls=%async_computation.3 | async-start | bytes 1048576 | tf_op jit(solution)/shard_map/all_to_all | solution.py:207

commit v11 on v10

--- a/solution.py
+++ b/solution.py
@@ -265,7 +265,7 @@
         middle = 1.5 * unit_matrix - 0.5 * product(inverse_root, approach)
         return (product(approach, middle), product(middle, inverse_root))
 
-    approach, inverse_root = lax.fori_loop(0, NSIT, refine, (system / row_bound, unit_matrix), unroll=True)
+    approach, inverse_root = lax.fori_loop(0, NSIT, refine, (system / row_bound, unit_matrix))
     inverse = product(inverse_root, inverse_root) / row_bound
     weights = product(inverse, projection[:, None])[:, 0]
     centring = unit_matrix - 1.0 / members

time: 206 us -> 204 us (level); the launches traced: 209 us -> 204 us
  blocking collectives: 86.4 us -> 81.9 us
  matrix products: 13.7 us -> 11 us
    all_to_all x2, blocking collectives: 86.4 us -> 81.9 us  [summed_everywhere(): parts = lax.all_to_all(rows, axes, 0, 0, tiled=True)]
    dot_general x34 -> x36, matrix products: 13.7 us -> 11 us  [product(): jnp.dot(left, right, precision=lax.Precision.HIGHEST, preferred_element_t...]
where the time goes in v11:
time: 204 us
  blocking collectives  81.9 us (40%)
  Pallas kernels  30.2 us (15%)
  waiting for transfers between devices  28.9 us (14%)
  local copies, waits for them, and re-layouts  19.6 us (10%)
  starting transfers between devices  19.5 us (10%)
  matrix products  11 us (5%)
  other arithmetic  10.1 us (5%)
    all_to_all x2, blocking collectives, summed_everywhere(): parts = lax.all_to_all(rows, axes, 0, 0, tiled=True)  81.9 us
    all_to_all x2, waiting for transfers between devices, summed_everywhere(): return lax.all_to_all(copies, axes, 0, 0, tiled=True)  24.5 us
    pallas_call x2, Pallas kernels, gather_rows(): pl.pallas_call(gather_kernel, out_shape=jax.ShapeDtypeStruct((count // gr...  14.7 us
    dot_general x36, matrix products, product(): jnp.dot(left, right, precision=lax.Precision.HIGHEST, preferred_element_t...  11 us
    all_to_all x2, starting transfers between devices, summed_everywhere(): return lax.all_to_all(copies, axes, 0, 0, tiled=True)  10.7 us
    pallas_call x1, Pallas kernels, two_steps(): pl.pallas_call(two_steps_kernel, out_shape=jax.ShapeDtypeStruct(field.sha...  10.2 us
    pallas_call x1, Pallas kernels, mixed_once(): pl.pallas_call(mix_kernel, out_shape=jax.ShapeDtypeStruct(rows.shape, row...  5.39 us
    ppermute x1, starting transfers between devices, advance_twice(): west = lax.ppermute(field[nx - 2:], 'gx', up_x)  4.46 us
  transfers between devices with their start and end apart: 6, of which 4 were waited for; matrix products, arithmetic and copies ran while one was open for 10% of the time, Pallas kernels for 4%

profile of v11, /device:TPU:1, one launch (start us, length us, event | category | flops | bytes accessed | tf_op | source)
XLA Modules:
  0.0 203.7 jit_solution(10564674386727705041)
XLA Ops:
  0.0 1.1 fusion.135
  1.3 4.5 %collective-permute-start = (f32[2,64,384]{2,0,1:T(2,128)S(1)}, f32[2,64,384]{2,0,1:T(2,128)S(1)}, u32[]{:S(2)}, u32[]{:S(2)}) collective-permute-start(f32[2,64,384]{2,0,1:T(2,128)S(1)} %copy.117), channel_id=1, source_target_pairs={{0,8},{8,16},{16,24},{24,32},{32,40},{40,48},{48,56},{56,64},{64,7... | collective-permute-start | bytes 589832 | tf_op jit(solution)/shard_map/ppermute | solution.py:161
  6.0 1.2 fusion.134
  7.2 1.2 fusion.133
  8.4 0.8 compare_convert_fusion
  9.2 1.0 slice_reduce_fusion.1
  10.5 0.6 fusion.140
  11.2 0.6 copy_bitcast_fusion
  11.8 0.7 reduce_max.36.busy_ref
  12.5 0.6 mul.238.coef_ref
  13.1 1.2 fusion.13.fold_ref
  14.4 0.6 slice_reduce_fusion.6
  15.1 4.2 %collective-permute-start.3 = (f32[36,2,384]{2,0,1:T(8,128)S(1)}, f32[36,2,384]{2,0,1:T(8,128)S(1)}, u32[]{:S(2)}, u32[]{:S(2)}) collective-permute-start(f32[36,2,384]{2,0,1:T(8,128)S(1)} %pad_maximum_fusion.1), channel_id=1, source_target_pairs={{1,0},{2,1},{3,2},{4,3},{5,4},{6,5},{7,6},{0,7},{9,8},{10,9},{11,1... | collective-permute-start | bytes 331784 | tf_op jit(solution)/shard_map/ppermute | solution.py:166
  19.3 0.7 copy.79.west_ref
  20.0 0.7 copy.80.east_ref
  21.1 4.1 %collective-permute-done.2 = f32[36,2,384]{2,0,1:T(8,128)S(1)} collective-permute-done((f32[36,2,384]{2,0,1:T(8,128)S(1)}, f32[36,2,384]{2,0,1:T(8,128)S(1)}, u32[]{:S(2)}, u32[]{:S(2)}) %collective-permute-start.2) | collective-permute-done | bytes 110624 | tf_op jit(solution)/shard_map/ppermute | solution.py:165
  25.2 0.6 pad_maximum_fusion.2.corner_ref
  25.8 0.6 slice_bitcast_fusion
  26.4 0.6 slice_bitcast_fusion.2
  27.1 10.2 %shard_map.82 = f32[32,64,384]{2,1,0:T(8,128)} custom-call(f32[32,64,384]{2,1,0:T(8,128)} %field_ref.1, f32[2,64,384]{2,1,0:T(8,128)} %copy.79.west_ref, f32[2,64,384]{2,1,0:T(8,128)} %copy.80.east_ref, f32[32,384]{1,0:T(8,128)} %get-tuple-element.134.south0_ref, f32[32,384]{1,0:T(8,128)} %get-tuple-element.133.south1_ref, ...), custom_call_target="tpu_custom_call" | custom-call | tf_op jit(solution)/shard_map/pallas_call | solution.py:142
  37.2 7.3 %shard_map.83 = f32[1024,128]{1,0:T(8,128)} custom-call(s32[128]{0:T(128)} %reduce_max.36.busy_ref, s32[4096]{0:T(1024)} %bitcast.129, s32[4096]{0:T(1024)} %bitcast.128, f32[12288]{0:T(1024)} %mul.238.coef_ref, f32[2048,384]{1,0:T(8,128)} %bitcast.109, f32[512,128]{1,0:T(8,128)} %fusion.13.fold_ref), custom_call_target="tpu_custom_call" | custom-call | tf_op jit(solution)/shard_map/pallas_call | solution.py:61
  44.5 44.3 %all_to_all.33 = f32[256,4,128]{2,1,0:T(4,128)S(1)} all-to-all(f32[256,4,128]{2,1,0:T(4,128)} %bitcast.113), channel_id=1, replica_groups=mesh['gx'=32,'gy'=8] {'gx','gy'}, dimensions={0} | all-to-all | bytes 1048576 | tf_op jit(solution)/shard_map/all_to_all | solution.py:204
  89.1 0.9 broadcast_in_dim.70
  90.0 5.4 %all-to-all-start.1 = ((f32[256,4,128]{2,1,0:T(4,128)}), f32[256,4,128]{2,1,0:T(4,128)S(1)}, u32[]{:S(2)}, u32[]{:S(2)}) async-start(f32[256,4,128]{2,1,0:T(4,128)} %broadcast_in_dim.70), calls=%async_computation.1 | async-start | bytes 1048576 | tf_op jit(solution)/shard_map/all_to_all | solution.py:207
  99.7 0.7 reduce_max.38.busy_ref
  100.5 0.6 mul.256.coef_ref
  101.1 7.4 %shard_map.84 = f32[1024,128]{1,0:T(8,128)} custom-call(s32[128]{0:T(128)} %reduce_max.38.busy_ref, s32[4096]{0:T(1024)} %bitcast.127, s32[4096]{0:T(1024)} %bitcast.126, f32[12288]{0:T(1024)} %mul.256.coef_ref, f32[2048,384]{1,0:T(8,128)} %bitcast.110, f32[512,128]{1,0:T(8,128)} %fusion.13.fold_ref), custom_call_target="tpu_custom_call" | custom-call | tf_op jit(solution)/shard_map/pallas_call | solution.py:61
  108.5 7.7 %all-to-all-done.1 = f32[256,4,128]{2,1,0:T(4,128)S(1)} async-done(((f32[256,4,128]{2,1,0:T(4,128)}), f32[256,4,128]{2,1,0:T(4,128)S(1)}, u32[]{:S(2)}, u32[]{:S(2)}) %all-to-all-start.1) | async-done | bytes 524320 | tf_op jit(solution)/shard_map/all_to_all | solution.py:207
  116.2 0.8 multiply_reduce_fusion.1
  116.9 1.1 fusion.10
  118.1 0.6 reduce_max.37
  119.4 0.6 broadcast_divide_fusion.1
  120.1 2.2 %while.26 = (s32[]{:T(128)}, f32[32,32]{0,1:T(8,128)S(1)}, f32[32,32]{1,0:T(8,128)S(1)}, s32[]{:T(128)}) while((s32[]{:T(128)}, f32[32,32]{0,1:T(8,128)S(1)}, f32[32,32]{1,0:T(8,128)S(1)}, s32[]{:T(128)}) %tuple.87), condition=%wide.region_5.6_spmd.clone, body=%wide.region_4.5_spmd.clone.sunk | while | flops 1183746 | bytes 53301 | solution.py:268
  122.3 0.9 convolution_divide_fusion.1
  123.9 0.6 fusion.6
  124.9 37.6 %all_to_all.34 = f32[256,4,128]{2,1,0:T(4,128)S(1)} all-to-all(f32[256,4,128]{2,1,0:T(4,128)S(1)} %copy.98), channel_id=1, replica_groups=mesh['gx'=32,'gy'=8] {'gx','gy'}, dimensions={0} | all-to-all | bytes 1048576 | tf_op jit(solution)/shard_map/all_to_all | solution.py:204
  162.8 0.9 broadcast_in_dim.78
  163.6 5.4 %all-to-all-start.3 = ((f32[256,4,128]{2,1,0:T(4,128)}), f32[256,4,128]{2,1,0:T(4,128)S(1)}, u32[]{:S(2)}, u32[]{:S(2)}) async-start(f32[256,4,128]{2,1,0:T(4,128)} %broadcast_in_dim.78), calls=%async_computation.3 | async-start | bytes 1048576 | tf_op jit(solution)/shard_map/all_to_all | solution.py:207
  169.8 0.5 squeeze.67
  173.0 16.8 %all-to-all-done.3 = f32[256,4,128]{2,1,0:T(4,128)S(1)} async-done(((f32[256,4,128]{2,1,0:T(4,128)}), f32[256,4,128]{2,1,0:T(4,128)S(1)}, u32[]{:S(2)}, u32[]{:S(2)}) %all-to-all-start.3) | async-done | bytes 524320 | tf_op jit(solution)/shard_map/all_to_all | solution.py:207
  189.8 0.7 multiply_reduce_fusion
  190.6 1.1 fusion.8
  191.7 0.6 reduce_max.39
  193.0 0.6 broadcast_divide_fusion
  193.7 2.2 %while.27 = (s32[]{:T(128)}, f32[32,32]{0,1:T(8,128)S(1)}, f32[32,32]{1,0:T(8,128)S(1)}, s32[]{:T(128)}) while((s32[]{:T(128)}, f32[32,32]{0,1:T(8,128)S(1)}, f32[32,32]{1,0:T(8,128)S(1)}, s32[]{:T(128)}) %tuple.86), condition=%wide.region_12.13_spmd.clone, body=%wide.region_11.12_spmd.clone.sunk | while | flops 1183746 | bytes 53301 | solution.py:268
  196.0 0.9 convolution_divide_fusion
  197.5 0.8 mul.274.mix_ref
  198.3 5.4 %shard_map.85 = f32[2048,384]{1,0:T(8,128)} custom-call(f32[2048,384]{1,0:T(8,128)} %bitcast.111, f32[128,128]{1,0:T(8,128)} %mul.274.mix_ref), custom_call_target="tpu_custom_call" | custom-call | tf_op jit(solution)/shard_map/pallas_call | solution.py:189
  (140 shorter events, 15.5 us)
Async XLA Ops:
  0.0 10.4 %copy-start.4 = (f32[2,3,4096]{2,0,1:T(2,128)S(1)}, f32[2,3,4096]{2,0,1:T(2,128)}, u32[]{:S(2)}) copy-start(f32[2,3,4096]{2,0,1:T(2,128)} %param.16) | copy-start | bytes 294916
  0.0 10.5 %copy-start.6 = (s32[2,4096]{1,0:T(2,128)S(1)}, s32[2,4096]{1,0:T(2,128)}, u32[]{:S(2)}) copy-start(s32[2,4096]{1,0:T(2,128)} %param.15) | copy-start | bytes 98308
  0.0 14.4 %copy-start.5 = (s32[2,4096]{1,0:T(2,128)S(1)}, s32[2,4096]{1,0:T(2,128)}, u32[]{:S(2)}) copy-start(s32[2,4096]{1,0:T(2,128)} %param.14) | copy-start | bytes 98308
  1.3 13.8 %collective-permute-start = (f32[2,64,384]{2,0,1:T(2,128)S(1)}, f32[2,64,384]{2,0,1:T(2,128)S(1)}, u32[]{:S(2)}, u32[]{:S(2)}) collective-permute-start(f32[2,64,384]{2,0,1:T(2,128)S(1)} %copy.117), channel_id=1, source_target_pairs={{0,8},{8,16},{16,24},{24,32},{32,40},{40,48},{48,56},{56,64},{64,7... | collective-permute-start | bytes 589832 | tf_op jit(solution)/shard_map/ppermute | solution.py:161
  5.9 9.2 %collective-permute-start.1 = (f32[2,64,384]{2,0,1:T(2,128)S(1)}, f32[2,64,384]{2,0,1:T(2,128)S(1)}, u32[]{:S(2)}, u32[]{:S(2)}) collective-permute-start(f32[2,64,384]{2,0,1:T(2,128)S(1)} %copy.118), channel_id=1, source_target_pairs={{8,0},{16,8},{24,16},{32,24},{40,32},{48,40},{56,48},{64,56},{72,6... | collective-permute-start | bytes 589832 | tf_op jit(solution)/shard_map/ppermute | solution.py:162
  15.1 6.0 %collective-permute-start.3 = (f32[36,2,384]{2,0,1:T(8,128)S(1)}, f32[36,2,384]{2,0,1:T(8,128)S(1)}, u32[]{:S(2)}, u32[]{:S(2)}) collective-permute-start(f32[36,2,384]{2,0,1:T(8,128)S(1)} %pad_maximum_fusion.1), channel_id=1, source_target_pairs={{1,0},{2,1},{3,2},{4,3},{5,4},{6,5},{7,6},{0,7},{9,8},{10,9},{11,1... | collective-permute-start | bytes 331784 | tf_op jit(solution)/shard_map/ppermute | solution.py:166
  19.3 5.9 %collective-permute-start.2 = (f32[36,2,384]{2,0,1:T(8,128)S(1)}, f32[36,2,384]{2,0,1:T(8,128)S(1)}, u32[]{:S(2)}, u32[]{:S(2)}) collective-permute-start(f32[36,2,384]{2,0,1:T(8,128)S(1)} %pad_maximum_fusion), channel_id=1, source_target_pairs={{0,1},{1,2},{2,3},{3,4},{4,5},{5,6},{6,7},{7,0},{8,9},{9,10},{10,1... | collective-permute-start | bytes 331784 | tf_op jit(solution)/shard_map/ppermute | solution.py:165
  44.5 52.3 %copy-start.9 = (s32[1,1,2,16]{3,2,1,0:T(2,128)S(1)}, s32[1,1,2,16]{3,2,1,0:T(2,128)}, u32[]{:S(2)}) copy-start(s32[1,1,2,16]{3,2,1,0:T(2,128)} %param.19) | copy-start | bytes 388
  88.8 8.5 %copy-start.7 = (f32[2,4096]{1,0:T(2,128)S(1)}, f32[2,4096]{1,0:T(2,128)}, u32[]{:S(2)}) copy-start(f32[2,4096]{1,0:T(2,128)} %param.17) | copy-start | bytes 98308
  88.8 8.5 %copy-start.8 = (f32[2,4096]{1,0:T(2,128)S(1)}, f32[2,4096]{1,0:T(2,128)}, u32[]{:S(2)}) copy-start(f32[2,4096]{1,0:T(2,128)} %param.18) | copy-start | bytes 98308
  90.0 26.2 %all-to-all-start.1 = ((f32[256,4,128]{2,1,0:T(4,128)}), f32[256,4,128]{2,1,0:T(4,128)S(1)}, u32[]{:S(2)}, u32[]{:S(2)}) async-start(f32[256,4,128]{2,1,0:T(4,128)} %broadcast_in_dim.70), calls=%async_computation.1 | async-start | bytes 1048576 | tf_op jit(solution)/shard_map/all_to_all | solution.py:207
  99.6 17.3 %copy-start.1 = (f32[32,32]{1,0:T(8,128)}, f32[32,32]{1,0:T(8,128)S(1)}, u32[]{:S(2)}) copy-start(f32[32,32]{1,0:T(8,128)S(1)} %copy.92) | copy-start | bytes 12292
  116.9 7.0 %copy-start = (f32[1024,128]{1,0:T(8,128)S(1)}, f32[1024,128]{1,0:T(8,128)}, u32[]{:S(2)}) copy-start(f32[1024,128]{1,0:T(8,128)} %shard_map.84) | copy-start | bytes 1572868
  116.9 3.1 %copy-start.3 = (f32[32,32]{1,0:T(8,128)S(1)}, f32[32,32]{1,0:T(8,128)}, u32[]{:S(2)}) copy-start(f32[32,32]{1,0:T(8,128)} %copy-done.1) | copy-start | bytes 12292
  163.6 26.2 %all-to-all-start.3 = ((f32[256,4,128]{2,1,0:T(4,128)}), f32[256,4,128]{2,1,0:T(4,128)S(1)}, u32[]{:S(2)}, u32[]{:S(2)}) async-start(f32[256,4,128]{2,1,0:T(4,128)} %broadcast_in_dim.78), calls=%async_computation.3 | async-start | bytes 1048576 | tf_op jit(solution)/shard_map/all_to_all | solution.py:207
  189.8 3.9 %copy-start.2 = (f32[32,32]{1,0:T(8,128)S(1)}, f32[32,32]{1,0:T(8,128)}, u32[]{:S(2)}) copy-start(f32[32,32]{1,0:T(8,128)} %copy-done.1) | copy-start | bytes 12292

commit v12 on v9

--- a/solution.py
+++ b/solution.py
@@ -24,9 +24,13 @@
     lane_level = lax.broadcasted_iota(jnp.int32, (1, width), 1) // ENS
     sublane = lax.broadcasted_iota(jnp.int32, (8, width), 0)
     groups = width // ENS
-    spread_ref[...] = jnp.zeros(spread_ref.shape, spread_ref.dtype)
 
     def body(block, carry):
+        @pl.when(busy_ref[block] == 0)
+        def _():
+            first = pl.multiple_of(block * 8, 8)
+            spread_ref[pl.ds(first, 8), :] = jnp.zeros((8, spread_ref.shape[1]), jnp.float32)
+
         @pl.when(busy_ref[block] > 0)
         def _():
             gathered = [jnp.zeros((8, width), jnp.float32) for k in range(groups)]

time: 206 us -> 209 us (1.015); the launches traced: 204 us -> 212 us
  Pallas kernels: 30.8 us -> 37.4 us
  blocking collectives: 81.5 us -> 86.4 us
  waiting for transfers between devices: 28.9 us -> 25.4 us
    pallas_call x2, Pallas kernels: 14.8 us -> 21.4 us  [gather_rows(): pl.pallas_call(gather_kernel, out_shape=jax.ShapeDtypeStruct((count // gr...]
    all_to_all x2, blocking collectives: 81.5 us -> 86.4 us  [summed_everywhere(): parts = lax.all_to_all(rows, axes, 0, 0, tiled=True)]
    all_to_all x2, waiting for transfers between devices: 24.5 us -> 20.9 us  [summed_everywhere(): return lax.all_to_all(copies, axes, 0, 0, tiled=True)]
  transfers between devices with their start and end apart: 6 -> 6, of which waited for: 4 -> 4; matrix products, arithmetic and copies ran while one was open for 10% -> 9% of each run, Pallas kernels for 4% -> 5%
where the time goes in v12:
time: 209 us; the launch traced here: 212 us
  blocking collectives  86.4 us (41%)
  Pallas kernels  37.4 us (18%)
  waiting for transfers between devices  25.4 us (12%)
  local copies, waits for them, and re-layouts  19.6 us (9%)
  starting transfers between devices  19.5 us (9%)
  matrix products  11 us (5%)
  other arithmetic  10.1 us (5%)
    all_to_all x2, blocking collectives, summed_everywhere(): parts = lax.all_to_all(rows, axes, 0, 0, tiled=True)  86.4 us
    pallas_call x2, Pallas kernels, gather_rows(): pl.pallas_call(gather_kernel, out_shape=jax.ShapeDtypeStruct((count // gr...  21.4 us
    all_to_all x2, waiting for transfers between devices, summed_everywhere(): return lax.all_to_all(copies, axes, 0, 0, tiled=True)  20.9 us
    dot_general x36, matrix products, product(): jnp.dot(left, right, precision=lax.Precision.HIGHEST, preferred_element_t...  11 us
    all_to_all x2, starting transfers between devices, summed_everywhere(): return lax.all_to_all(copies, axes, 0, 0, tiled=True)  10.7 us
    pallas_call x1, Pallas kernels, two_steps(): pl.pallas_call(two_steps_kernel, out_shape=jax.ShapeDtypeStruct(field.sha...  10.2 us
    pallas_call x1, Pallas kernels, mixed_once(): pl.pallas_call(mix_kernel, out_shape=jax.ShapeDtypeStruct(rows.shape, row...  5.85 us
    ppermute x1, starting transfers between devices, advance_twice(): west = lax.ppermute(field[nx - 2:], 'gx', up_x)  4.46 us
  transfers between devices with their start and end apart: 6, of which 4 were waited for; matrix products, arithmetic and copies ran while one was open for 9% of the time, Pallas kernels for 5%

profile of v12, /device:TPU:1, one launch (start us, length us, event | category | flops | bytes accessed | tf_op | source)
XLA Modules:
  0.0 211.8 jit_solution(16415005291729226488)
XLA Ops:
  0.0 1.1 fusion.135
  1.3 4.5 %collective-permute-start = (f32[2,64,384]{2,0,1:T(2,128)S(1)}, f32[2,64,384]{2,0,1:T(2,128)S(1)}, u32[]{:S(2)}, u32[]{:S(2)}) collective-permute-start(f32[2,64,384]{2,0,1:T(2,128)S(1)} %copy.117), channel_id=1, source_target_pairs={{0,8},{8,16},{16,24},{24,32},{32,40},{40,48},{48,56},{56,64},{64,7... | collective-permute-start | bytes 589832 | tf_op jit(solution)/shard_map/ppermute | solution.py:165
  6.0 1.2 fusion.134
  7.2 1.2 fusion.133
  8.4 0.8 compare_convert_fusion
  9.2 1.0 slice_reduce_fusion.1
  10.5 0.6 fusion.140
  11.2 0.6 copy_bitcast_fusion
  11.8 0.7 reduce_max.36.busy_ref
  12.5 0.6 mul.238.coef_ref
  13.1 1.2 fusion.13.fold_ref
  14.4 0.6 slice_reduce_fusion.6
  15.1 4.2 %collective-permute-start.3 = (f32[36,2,384]{2,0,1:T(8,128)S(1)}, f32[36,2,384]{2,0,1:T(8,128)S(1)}, u32[]{:S(2)}, u32[]{:S(2)}) collective-permute-start(f32[36,2,384]{2,0,1:T(8,128)S(1)} %pad_maximum_fusion.1), channel_id=1, source_target_pairs={{1,0},{2,1},{3,2},{4,3},{5,4},{6,5},{7,6},{0,7},{9,8},{10,9},{11,1... | collective-permute-start | bytes 331784 | tf_op jit(solution)/shard_map/ppermute | solution.py:170
  19.3 0.7 copy.79.west_ref
  20.0 0.7 copy.80.east_ref
  21.1 4.1 %collective-permute-done.2 = f32[36,2,384]{2,0,1:T(8,128)S(1)} collective-permute-done((f32[36,2,384]{2,0,1:T(8,128)S(1)}, f32[36,2,384]{2,0,1:T(8,128)S(1)}, u32[]{:S(2)}, u32[]{:S(2)}) %collective-permute-start.2) | collective-permute-done | bytes 110624 | tf_op jit(solution)/shard_map/ppermute | solution.py:169
  25.2 0.6 pad_maximum_fusion.2.corner_ref
  25.8 0.6 slice_bitcast_fusion
  26.4 0.6 slice_bitcast_fusion.2
  27.1 10.2 %shard_map.82 = f32[32,64,384]{2,1,0:T(8,128)} custom-call(f32[32,64,384]{2,1,0:T(8,128)} %field_ref.1, f32[2,64,384]{2,1,0:T(8,128)} %copy.79.west_ref, f32[2,64,384]{2,1,0:T(8,128)} %copy.80.east_ref, f32[32,384]{1,0:T(8,128)} %get-tuple-element.134.south0_ref, f32[32,384]{1,0:T(8,128)} %get-tuple-element.133.south1_ref, ...), custom_call_target="tpu_custom_call" | custom-call | tf_op jit(solution)/shard_map/pallas_call | solution.py:146
  37.2 10.4 %shard_map.83 = f32[1024,128]{1,0:T(8,128)} custom-call(s32[128]{0:T(128)} %reduce_max.36.busy_ref, s32[4096]{0:T(1024)} %bitcast.129, s32[4096]{0:T(1024)} %bitcast.128, f32[12288]{0:T(1024)} %mul.238.coef_ref, f32[2048,384]{1,0:T(8,128)} %bitcast.109, f32[512,128]{1,0:T(8,128)} %fusion.13.fold_ref), custom_call_target="tpu_custom_call" | custom-call | tf_op jit(solution)/shard_map/pallas_call | solution.py:65
  47.7 46.8 %all_to_all.33 = f32[256,4,128]{2,1,0:T(4,128)S(1)} all-to-all(f32[256,4,128]{2,1,0:T(4,128)} %bitcast.113), channel_id=1, replica_groups=mesh['gx'=32,'gy'=8] {'gx','gy'}, dimensions={0} | all-to-all | bytes 1048576 | tf_op jit(solution)/shard_map/all_to_all | solution.py:208
  94.7 0.9 broadcast_in_dim.70
  95.6 5.4 %all-to-all-start.1 = ((f32[256,4,128]{2,1,0:T(4,128)}), f32[256,4,128]{2,1,0:T(4,128)S(1)}, u32[]{:S(2)}, u32[]{:S(2)}) async-start(f32[256,4,128]{2,1,0:T(4,128)} %broadcast_in_dim.70), calls=%async_computation.1 | async-start | bytes 1048576 | tf_op jit(solution)/shard_map/all_to_all | solution.py:211
  101.7 0.5 squeeze.62
  105.3 0.7 reduce_max.38.busy_ref
  106.1 0.6 mul.256.coef_ref
  106.7 10.9 %shard_map.84 = f32[1024,128]{1,0:T(8,128)} custom-call(s32[128]{0:T(128)} %reduce_max.38.busy_ref, s32[4096]{0:T(1024)} %bitcast.127, s32[4096]{0:T(1024)} %bitcast.126, f32[12288]{0:T(1024)} %mul.256.coef_ref, f32[2048,384]{1,0:T(8,128)} %bitcast.110, f32[512,128]{1,0:T(8,128)} %fusion.13.fold_ref), custom_call_target="tpu_custom_call" | custom-call | tf_op jit(solution)/shard_map/pallas_call | solution.py:65
  117.6 4.2 %all-to-all-done.1 = f32[256,4,128]{2,1,0:T(4,128)S(1)} async-done(((f32[256,4,128]{2,1,0:T(4,128)}), f32[256,4,128]{2,1,0:T(4,128)S(1)}, u32[]{:S(2)}, u32[]{:S(2)}) %all-to-all-start.1) | async-done | bytes 524320 | tf_op jit(solution)/shard_map/all_to_all | solution.py:211
  121.8 0.8 multiply_reduce_fusion.1
  122.6 1.1 fusion.10
  123.7 0.6 reduce_max.37
  125.1 0.6 broadcast_divide_fusion.1
  125.7 2.2 %while.26 = (s32[]{:T(128)}, f32[32,32]{0,1:T(8,128)S(1)}, f32[32,32]{1,0:T(8,128)S(1)}, s32[]{:T(128)}) while((s32[]{:T(128)}, f32[32,32]{0,1:T(8,128)S(1)}, f32[32,32]{1,0:T(8,128)S(1)}, s32[]{:T(128)}) %tuple.87), condition=%wide.region_5.6_spmd.clone, body=%wide.region_4.5_spmd.clone.sunk | while | flops 1183746 | bytes 53301 | solution.py:272
  128.0 0.9 convolution_divide_fusion.1
  129.6 0.6 fusion.6
  130.5 39.6 %all_to_all.34 = f32[256,4,128]{2,1,0:T(4,128)S(1)} all-to-all(f32[256,4,128]{2,1,0:T(4,128)S(1)} %copy.98), channel_id=1, replica_groups=mesh['gx'=32,'gy'=8] {'gx','gy'}, dimensions={0} | all-to-all | bytes 1048576 | tf_op jit(solution)/shard_map/all_to_all | solution.py:208
  170.4 0.9 broadcast_in_dim.78
  171.2 5.4 %all-to-all-start.3 = ((f32[256,4,128]{2,1,0:T(4,128)}), f32[256,4,128]{2,1,0:T(4,128)S(1)}, u32[]{:S(2)}, u32[]{:S(2)}) async-start(f32[256,4,128]{2,1,0:T(4,128)} %broadcast_in_dim.78), calls=%async_computation.3 | async-start | bytes 1048576 | tf_op jit(solution)/shard_map/all_to_all | solution.py:211
  180.6 16.8 %all-to-all-done.3 = f32[256,4,128]{2,1,0:T(4,128)S(1)} async-done(((f32[256,4,128]{2,1,0:T(4,128)}), f32[256,4,128]{2,1,0:T(4,128)S(1)}, u32[]{:S(2)}, u32[]{:S(2)}) %all-to-all-start.3) | async-done | bytes 524320 | tf_op jit(solution)/shard_map/all_to_all | solution.py:211
  197.4 0.8 multiply_reduce_fusion
  198.2 1.1 fusion.8
  199.4 0.6 reduce_max.39
  200.7 0.6 broadcast_divide_fusion
  201.3 2.2 %while.27 = (s32[]{:T(128)}, f32[32,32]{0,1:T(8,128)S(1)}, f32[32,32]{1,0:T(8,128)S(1)}, s32[]{:T(128)}) while((s32[]{:T(128)}, f32[32,32]{0,1:T(8,128)S(1)}, f32[32,32]{1,0:T(8,128)S(1)}, s32[]{:T(128)}) %tuple.86), condition=%wide.region_12.13_spmd.clone, body=%wide.region_11.12_spmd.clone.sunk | while | flops 1183746 | bytes 53301 | solution.py:272
  203.6 0.9 convolution_divide_fusion
  205.2 0.8 mul.274.mix_ref
  205.9 5.9 %shard_map.85 = f32[2048,384]{1,0:T(8,128)} custom-call(f32[2048,384]{1,0:T(8,128)} %bitcast.111, f32[128,128]{1,0:T(8,128)} %mul.274.mix_ref), custom_call_target="tpu_custom_call" | custom-call | tf_op jit(solution)/shard_map/pallas_call | solution.py:193
  (140 shorter events, 15.5 us)
Async XLA Ops:
  0.0 10.4 %copy-start.4 = (f32[2,3,4096]{2,0,1:T(2,128)S(1)}, f32[2,3,4096]{2,0,1:T(2,128)}, u32[]{:S(2)}) copy-start(f32[2,3,4096]{2,0,1:T(2,128)} %param.16) | copy-start | bytes 294916
  0.0 10.5 %copy-start.6 = (s32[2,4096]{1,0:T(2,128)S(1)}, s32[2,4096]{1,0:T(2,128)}, u32[]{:S(2)}) copy-start(s32[2,4096]{1,0:T(2,128)} %param.15) | copy-start | bytes 98308
  0.0 14.4 %copy-start.5 = (s32[2,4096]{1,0:T(2,128)S(1)}, s32[2,4096]{1,0:T(2,128)}, u32[]{:S(2)}) copy-start(s32[2,4096]{1,0:T(2,128)} %param.14) | copy-start | bytes 98308
  1.3 13.8 %collective-permute-start = (f32[2,64,384]{2,0,1:T(2,128)S(1)}, f32[2,64,384]{2,0,1:T(2,128)S(1)}, u32[]{:S(2)}, u32[]{:S(2)}) collective-permute-start(f32[2,64,384]{2,0,1:T(2,128)S(1)} %copy.117), channel_id=1, source_target_pairs={{0,8},{8,16},{16,24},{24,32},{32,40},{40,48},{48,56},{56,64},{64,7... | collective-permute-start | bytes 589832 | tf_op jit(solution)/shard_map/ppermute | solution.py:165
  5.9 9.2 %collective-permute-start.1 = (f32[2,64,384]{2,0,1:T(2,128)S(1)}, f32[2,64,384]{2,0,1:T(2,128)S(1)}, u32[]{:S(2)}, u32[]{:S(2)}) collective-permute-start(f32[2,64,384]{2,0,1:T(2,128)S(1)} %copy.118), channel_id=1, source_target_pairs={{8,0},{16,8},{24,16},{32,24},{40,32},{48,40},{56,48},{64,56},{72,6... | collective-permute-start | bytes 589832 | tf_op jit(solution)/shard_map/ppermute | solution.py:166
  15.1 6.0 %collective-permute-start.3 = (f32[36,2,384]{2,0,1:T(8,128)S(1)}, f32[36,2,384]{2,0,1:T(8,128)S(1)}, u32[]{:S(2)}, u32[]{:S(2)}) collective-permute-start(f32[36,2,384]{2,0,1:T(8,128)S(1)} %pad_maximum_fusion.1), channel_id=1, source_target_pairs={{1,0},{2,1},{3,2},{4,3},{5,4},{6,5},{7,6},{0,7},{9,8},{10,9},{11,1... | collective-permute-start | bytes 331784 | tf_op jit(solution)/shard_map/ppermute | solution.py:170
  19.3 5.9 %collective-permute-start.2 = (f32[36,2,384]{2,0,1:T(8,128)S(1)}, f32[36,2,384]{2,0,1:T(8,128)S(1)}, u32[]{:S(2)}, u32[]{:S(2)}) collective-permute-start(f32[36,2,384]{2,0,1:T(8,128)S(1)} %pad_maximum_fusion), channel_id=1, source_target_pairs={{0,1},{1,2},{2,3},{3,4},{4,5},{5,6},{6,7},{7,0},{8,9},{9,10},{10,1... | collective-permute-start | bytes 331784 | tf_op jit(solution)/shard_map/ppermute | solution.py:169
  47.7 54.7 %copy-start.9 = (s32[1,1,2,16]{3,2,1,0:T(2,128)S(1)}, s32[1,1,2,16]{3,2,1,0:T(2,128)}, u32[]{:S(2)}) copy-start(s32[1,1,2,16]{3,2,1,0:T(2,128)} %param.19) | copy-start | bytes 388
  94.5 8.5 %copy-start.7 = (f32[2,4096]{1,0:T(2,128)S(1)}, f32[2,4096]{1,0:T(2,128)}, u32[]{:S(2)}) copy-start(f32[2,4096]{1,0:T(2,128)} %param.17) | copy-start | bytes 98308
  94.5 8.5 %copy-start.8 = (f32[2,4096]{1,0:T(2,128)S(1)}, f32[2,4096]{1,0:T(2,128)}, u32[]{:S(2)}) copy-start(f32[2,4096]{1,0:T(2,128)} %param.18) | copy-start | bytes 98308
  95.6 26.2 %all-to-all-start.1 = ((f32[256,4,128]{2,1,0:T(4,128)}), f32[256,4,128]{2,1,0:T(4,128)S(1)}, u32[]{:S(2)}, u32[]{:S(2)}) async-start(f32[256,4,128]{2,1,0:T(4,128)} %broadcast_in_dim.70), calls=%async_computation.1 | async-start | bytes 1048576 | tf_op jit(solution)/shard_map/all_to_all | solution.py:211
  105.2 17.3 %copy-start.1 = (f32[32,32]{1,0:T(8,128)}, f32[32,32]{1,0:T(8,128)S(1)}, u32[]{:S(2)}) copy-start(f32[32,32]{1,0:T(8,128)S(1)} %copy.92) | copy-start | bytes 12292
  122.6 7.0 %copy-start = (f32[1024,128]{1,0:T(8,128)S(1)}, f32[1024,128]{1,0:T(8,128)}, u32[]{:S(2)}) copy-start(f32[1024,128]{1,0:T(8,128)} %shard_map.84) | copy-start | bytes 1572868
  122.6 3.1 %copy-start.3 = (f32[32,32]{1,0:T(8,128)S(1)}, f32[32,32]{1,0:T(8,128)}, u32[]{:S(2)}) copy-start(f32[32,32]{1,0:T(8,128)} %copy-done.1) | copy-start | bytes 12292
  171.2 26.2 %all-to-all-start.3 = ((f32[256,4,128]{2,1,0:T(4,128)}), f32[256,4,128]{2,1,0:T(4,128)S(1)}, u32[]{:S(2)}, u32[]{:S(2)}) async-start(f32[256,4,128]{2,1,0:T(4,128)} %broadcast_in_dim.78), calls=%async_computation.3 | async-start | bytes 1048576 | tf_op jit(solution)/shard_map/all_to_all | solution.py:211
  197.4 3.9 %copy-start.2 = (f32[32,32]{1,0:T(8,128)S(1)}, f32[32,32]{1,0:T(8,128)}, u32[]{:S(2)}) copy-start(f32[32,32]{1,0:T(8,128)} %copy-done.1) | copy-start | bytes 12292
